TPU v7x, 512 devices: a whole 4x8x8 slice. The times are simulated.
512 devices in a mesh: tm: 8 (over y), space: 64 (over x, z, core).
Axes of the slice: x: 4, y: 8, z: 8, core: 2. Of those that a mesh axis runs over, the one named last changes fastest.
Arguments:
- starts: float32 [8, 256, 32768], P('tm', None, 'space'), may hold values from -6 to 6
- vel_x: float32 [256, 32768], P(None, 'space'), may hold values from -1 to 1
- vel_y: float32 [256, 32768], P(None, 'space'), may hold values from -1 to 1
- kappa: float32 [256, 32768], P(None, 'space'), may hold values from 0.02 to 0.25
Outputs:
- new_ends: float32 [8, 256, 32768], P('tm', None, 'space')
All inputs are finite; a program needn't handle non-finite values.
Results may differ from a plain program's by a relative error of at most 0.00002.
Values sent between devices are 32-bit elements; how exact they have to be, the bound alone decides.
No kernel may reach another device: no remote copies, remote signals or barrier semaphores. Data moves between devices by JAX's collectives and lax.ppermute only.
A program may use at most 64 MiB of HBM per device.

v0:
```python
import jax
import jax.numpy as jnp
from jax import lax
from jax.sharding import PartitionSpec as P

FINE = 8
CSTEPS = 2


DT = 1.0 / 12.0


def with_halo(cells, sides, width):
    for axis, dim in sides:
        count = lax.axis_size(axis)
        ends = count - 1
        head = lax.slice_in_dim(cells, 0, width, axis=dim)
        tail = lax.slice_in_dim(cells, cells.shape[dim] - width, cells.shape[dim], axis=dim)
        cells = jnp.concatenate(
            [
                lax.ppermute(tail, axis, [(i, (i + 1) % count) for i in range(ends)]),
                cells,
                lax.ppermute(head, axis, [((i + 1) % count, i) for i in range(ends)]),
            ],
            axis=dim,
        )
    return cells


def shifted(block, axis, distance):
    devices = range(lax.axis_size(axis))
    route = [(i - distance, i) for i in devices if i - distance in devices]
    return lax.ppermute(block, axis, route)


def advance(wide, coef, size):
    padded = jnp.pad(wide, ((1, 1), (0, 0)))
    mid = padded[1:-1, 1:-1]
    left = padded[1:-1, :-2]
    right = padded[1:-1, 2:]
    upper = padded[:-2, 1:-1]
    lower = padded[2:, 1:-1]
    moved = jnp.maximum(coef[0], 0.0) * (mid - left) + jnp.minimum(coef[0], 0.0) * (right - mid)
    moved = (
        moved
        + jnp.maximum(coef[1], 0.0) * (mid - upper)
        + jnp.minimum(coef[1], 0.0) * (lower - mid)
    )
    spread = upper + lower + left + right - 4.0 * mid
    return mid - size * moved + size * coef[2] * spread


def coarse(field, coef):
    for step in range(CSTEPS):
        wide = with_halo(field, (("space", 1),), 1)
        field = advance(wide, coef, DT * FINE / CSTEPS)
    return field


def local(starts, vel_x, vel_y, kappa):
    coef = jnp.stack([vel_x, vel_y, kappa])
    state = starts[0]
    field = state
    for step in range(FINE):
        wide = with_halo(field, (("space", 1),), 1)
        field = advance(wide, coef, DT)
    old_coarse = coarse(state, coef)
    first = lax.axis_index("tm") == 0
    carried = jnp.where(first, field, field - old_coarse)
    slices = lax.axis_size("tm")
    current = carried
    for turn in range(slices - 1):
        incoming = shifted(current, "tm", 1)
        current = carried + coarse(incoming, coef)
    return current[None]


def solution(mesh):
    placed = (P("tm", None, "space"), P(None, "space"), P(None, "space"), P(None, "space"))
    return jax.shard_map(
        local, mesh=mesh, in_specs=placed, out_specs=P("tm", None, "space"), check_vma=False
    )
```

profile of v0, /device:TPU:36, one launch (start us, length us, event | category | flops | bytes accessed | tf_op | source)
XLA Modules:
  0.0 364.9 jit_solution(2772392709990552687)
XLA Ops:
  1.1 1.9 collective-permute-start
  3.1 10.5 %collective-permute-start.1 = (f32[256,1]{1,0:T(8,128)S(1)}, f32[256,1]{1,0:T(8,128)S(1)}, u32[]{:S(2)}, u32[]{:S(2)}) collective-permute-start(f32[256,1]{1,0:T(8,128)S(1)} %get-tuple-element.55), channel_id=1, source_target_pairs={{1,0},{2,1},{3,2},{4,3},{5,4},{6,5},{7,6},{8,7},{9,8},{10,9},{11,1... | collective-permute-start | bytes 3080 | tf_op jit(solution)/shard_map/ppermute | solution.py:23
  14.1 1.9 collective-permute-done.1
  17.4 2.4 multiply_add_fusion.1
  19.9 1.9 collective-permute-start.2
  21.8 5.9 %collective-permute-start.3 = (f32[256,1]{1,0:T(8,128)S(1)}, f32[256,1]{1,0:T(8,128)S(1)}, u32[]{:S(2)}, u32[]{:S(2)}) collective-permute-start(f32[256,1]{1,0:T(8,128)S(1)} %get-tuple-element.51), channel_id=1, source_target_pairs={{1,0},{2,1},{3,2},{4,3},{5,4},{6,5},{7,6},{8,7},{9,8},{10,9},{11,1... | collective-permute-start | bytes 3080 | tf_op jit(solution)/shard_map/ppermute | solution.py:23
  31.3 1.9 collective-permute-start.4
  33.2 5.9 %collective-permute-start.5 = (f32[256,1]{1,0:T(8,128)S(1)}, f32[256,1]{1,0:T(8,128)S(1)}, u32[]{:S(2)}, u32[]{:S(2)}) collective-permute-start(f32[256,1]{1,0:T(8,128)S(1)} %get-tuple-element.49), channel_id=1, source_target_pairs={{1,0},{2,1},{3,2},{4,3},{5,4},{6,5},{7,6},{8,7},{9,8},{10,9},{11,1... | collective-permute-start | bytes 3080 | tf_op jit(solution)/shard_map/ppermute | solution.py:23
  42.7 1.9 collective-permute-start.6
  44.7 5.9 %collective-permute-start.7 = (f32[256,1]{1,0:T(8,128)S(1)}, f32[256,1]{1,0:T(8,128)S(1)}, u32[]{:S(2)}, u32[]{:S(2)}) collective-permute-start(f32[256,1]{1,0:T(8,128)S(1)} %get-tuple-element.47), channel_id=1, source_target_pairs={{1,0},{2,1},{3,2},{4,3},{5,4},{6,5},{7,6},{8,7},{9,8},{10,9},{11,1... | collective-permute-start | bytes 3080 | tf_op jit(solution)/shard_map/ppermute | solution.py:23
  54.1 1.9 collective-permute-start.8
  56.1 5.9 %collective-permute-start.9 = (f32[256,1]{1,0:T(8,128)S(1)}, f32[256,1]{1,0:T(8,128)S(1)}, u32[]{:S(2)}, u32[]{:S(2)}) collective-permute-start(f32[256,1]{1,0:T(8,128)S(1)} %get-tuple-element.45), channel_id=1, source_target_pairs={{1,0},{2,1},{3,2},{4,3},{5,4},{6,5},{7,6},{8,7},{9,8},{10,9},{11,1... | collective-permute-start | bytes 3080 | tf_op jit(solution)/shard_map/ppermute | solution.py:23
  65.6 1.9 collective-permute-start.10
  67.5 5.9 %collective-permute-start.11 = (f32[256,1]{1,0:T(8,128)S(1)}, f32[256,1]{1,0:T(8,128)S(1)}, u32[]{:S(2)}, u32[]{:S(2)}) collective-permute-start(f32[256,1]{1,0:T(8,128)S(1)} %get-tuple-element.43), channel_id=1, source_target_pairs={{1,0},{2,1},{3,2},{4,3},{5,4},{6,5},{7,6},{8,7},{9,8},{10,9},{11,1... | collective-permute-start | bytes 3080 | tf_op jit(solution)/shard_map/ppermute | solution.py:23
  79.5 5.9 %collective-permute-start.13 = (f32[256,1]{1,0:T(8,128)S(1)}, f32[256,1]{1,0:T(8,128)S(1)}, u32[]{:S(2)}, u32[]{:S(2)}) collective-permute-start(f32[256,1]{1,0:T(8,128)S(1)} %get-tuple-element.41), channel_id=1, source_target_pairs={{1,0},{2,1},{3,2},{4,3},{5,4},{6,5},{7,6},{8,7},{9,8},{10,9},{11,1... | collective-permute-start | bytes 3080 | tf_op jit(solution)/shard_map/ppermute | solution.py:23
  89.2 1.9 collective-permute-start.14
  91.1 5.9 %collective-permute-start.15 = (f32[256,1]{1,0:T(8,128)S(1)}, f32[256,1]{1,0:T(8,128)S(1)}, u32[]{:S(2)}, u32[]{:S(2)}) collective-permute-start(f32[256,1]{1,0:T(8,128)S(1)} %get-tuple-element.37), channel_id=1, source_target_pairs={{1,0},{2,1},{3,2},{4,3},{5,4},{6,5},{7,6},{8,7},{9,8},{10,9},{11,1... | collective-permute-start | bytes 3080 | tf_op jit(solution)/shard_map/ppermute | solution.py:23
  97.1 1.9 collective-permute-start.16
  99.1 5.8 %collective-permute-start.17 = (f32[256,1]{1,0:T(8,128)S(1)}, f32[256,1]{1,0:T(8,128)S(1)}, u32[]{:S(2)}, u32[]{:S(2)}) collective-permute-start(f32[256,1]{1,0:T(8,128)S(1)} %get-tuple-element.53), channel_id=1, source_target_pairs={{1,0},{2,1},{3,2},{4,3},{5,4},{6,5},{7,6},{8,7},{9,8},{10,9},{11,1... | collective-permute-start | bytes 3080 | tf_op jit(solution)/shard_map/ppermute | solution.py:23
  109.1 2.6 collective-permute-start.18
  111.7 9.7 %collective-permute-done.18 = f32[256,512]{1,0:T(8,128)S(1)} collective-permute-done((f32[256,512]{1,0:T(8,128)S(1)}, f32[256,512]{1,0:T(8,128)S(1)}, u32[]{:S(2)}, u32[]{:S(2)}) %collective-permute-start.18) | collective-permute-done | bytes 524320 | tf_op jit(solution)/shard_map/ppermute | solution.py:33
  121.5 1.9 collective-permute-start.19
  123.4 5.9 %collective-permute-start.20 = (f32[256,1]{1,0:T(8,128)S(1)}, f32[256,1]{1,0:T(8,128)S(1)}, u32[]{:S(2)}, u32[]{:S(2)}) collective-permute-start(f32[256,1]{1,0:T(8,128)S(1)} %get-tuple-element.35), channel_id=1, source_target_pairs={{1,0},{2,1},{3,2},{4,3},{5,4},{6,5},{7,6},{8,7},{9,8},{10,9},{11,1... | collective-permute-start | bytes 3080 | tf_op jit(solution)/shard_map/ppermute | solution.py:23
  132.8 1.9 collective-permute-start.21
  134.7 5.9 %collective-permute-start.22 = (f32[256,1]{1,0:T(8,128)S(1)}, f32[256,1]{1,0:T(8,128)S(1)}, u32[]{:S(2)}, u32[]{:S(2)}) collective-permute-start(f32[256,1]{1,0:T(8,128)S(1)} %get-tuple-element.33), channel_id=1, source_target_pairs={{1,0},{2,1},{3,2},{4,3},{5,4},{6,5},{7,6},{8,7},{9,8},{10,9},{11,1... | collective-permute-start | bytes 3080 | tf_op jit(solution)/shard_map/ppermute | solution.py:23
  144.1 1.9 collective-permute-start.23
  146.1 10.4 %collective-permute-done.23 = f32[256,512]{1,0:T(8,128)S(1)} collective-permute-done((f32[256,512]{1,0:T(8,128)S(1)}, f32[256,512]{1,0:T(8,128)S(1)}, u32[]{:S(2)}, u32[]{:S(2)}) %collective-permute-start.23) | collective-permute-done | bytes 524320 | tf_op jit(solution)/shard_map/ppermute | solution.py:33
  158.5 7.3 %collective-permute-start.25 = (f32[256,1]{1,0:T(8,128)S(1)}, f32[256,1]{1,0:T(8,128)S(1)}, u32[]{:S(2)}, u32[]{:S(2)}) collective-permute-start(f32[256,1]{1,0:T(8,128)S(1)} %get-tuple-element.31), channel_id=1, source_target_pairs={{1,0},{2,1},{3,2},{4,3},{5,4},{6,5},{7,6},{8,7},{9,8},{10,9},{11,1... | collective-permute-start | bytes 3080 | tf_op jit(solution)/shard_map/ppermute | solution.py:23
  171.4 5.9 %collective-permute-start.27 = (f32[256,1]{1,0:T(8,128)S(1)}, f32[256,1]{1,0:T(8,128)S(1)}, u32[]{:S(2)}, u32[]{:S(2)}) collective-permute-start(f32[256,1]{1,0:T(8,128)S(1)} %get-tuple-element.29), channel_id=1, source_target_pairs={{1,0},{2,1},{3,2},{4,3},{5,4},{6,5},{7,6},{8,7},{9,8},{10,9},{11,1... | collective-permute-start | bytes 3080 | tf_op jit(solution)/shard_map/ppermute | solution.py:23
  182.7 10.4 %collective-permute-done.28 = f32[256,512]{1,0:T(8,128)S(1)} collective-permute-done((f32[256,512]{1,0:T(8,128)S(1)}, f32[256,512]{1,0:T(8,128)S(1)}, u32[]{:S(2)}, u32[]{:S(2)}) %collective-permute-start.28) | collective-permute-done | bytes 524320 | tf_op jit(solution)/shard_map/ppermute | solution.py:33
  195.1 7.3 %collective-permute-start.30 = (f32[256,1]{1,0:T(8,128)S(1)}, f32[256,1]{1,0:T(8,128)S(1)}, u32[]{:S(2)}, u32[]{:S(2)}) collective-permute-start(f32[256,1]{1,0:T(8,128)S(1)} %get-tuple-element.27), channel_id=1, source_target_pairs={{1,0},{2,1},{3,2},{4,3},{5,4},{6,5},{7,6},{8,7},{9,8},{10,9},{11,1... | collective-permute-start | bytes 3080 | tf_op jit(solution)/shard_map/ppermute | solution.py:23
  208.0 5.9 %collective-permute-start.32 = (f32[256,1]{1,0:T(8,128)S(1)}, f32[256,1]{1,0:T(8,128)S(1)}, u32[]{:S(2)}, u32[]{:S(2)}) collective-permute-start(f32[256,1]{1,0:T(8,128)S(1)} %get-tuple-element.25), channel_id=1, source_target_pairs={{1,0},{2,1},{3,2},{4,3},{5,4},{6,5},{7,6},{8,7},{9,8},{10,9},{11,1... | collective-permute-start | bytes 3080 | tf_op jit(solution)/shard_map/ppermute | solution.py:23
  217.5 1.9 collective-permute-start.33
  219.4 10.4 %collective-permute-done.33 = f32[256,512]{1,0:T(8,128)S(1)} collective-permute-done((f32[256,512]{1,0:T(8,128)S(1)}, f32[256,512]{1,0:T(8,128)S(1)}, u32[]{:S(2)}, u32[]{:S(2)}) %collective-permute-start.33) | collective-permute-done | bytes 524320 | tf_op jit(solution)/shard_map/ppermute | solution.py:33
  229.8 1.9 collective-permute-start.34
  231.8 7.3 %collective-permute-start.35 = (f32[256,1]{1,0:T(8,128)S(1)}, f32[256,1]{1,0:T(8,128)S(1)}, u32[]{:S(2)}, u32[]{:S(2)}) collective-permute-start(f32[256,1]{1,0:T(8,128)S(1)} %get-tuple-element.23), channel_id=1, source_target_pairs={{1,0},{2,1},{3,2},{4,3},{5,4},{6,5},{7,6},{8,7},{9,8},{10,9},{11,1... | collective-permute-start | bytes 3080 | tf_op jit(solution)/shard_map/ppermute | solution.py:23
  242.8 1.9 collective-permute-start.36
  244.7 5.9 %collective-permute-start.37 = (f32[256,1]{1,0:T(8,128)S(1)}, f32[256,1]{1,0:T(8,128)S(1)}, u32[]{:S(2)}, u32[]{:S(2)}) collective-permute-start(f32[256,1]{1,0:T(8,128)S(1)} %get-tuple-element.21), channel_id=1, source_target_pairs={{1,0},{2,1},{3,2},{4,3},{5,4},{6,5},{7,6},{8,7},{9,8},{10,9},{11,1... | collective-permute-start | bytes 3080 | tf_op jit(solution)/shard_map/ppermute | solution.py:23
  256.0 10.4 %collective-permute-done.38 = f32[256,512]{1,0:T(8,128)S(1)} collective-permute-done((f32[256,512]{1,0:T(8,128)S(1)}, f32[256,512]{1,0:T(8,128)S(1)}, u32[]{:S(2)}, u32[]{:S(2)}) %collective-permute-start.38) | collective-permute-done | bytes 524320 | tf_op jit(solution)/shard_map/ppermute | solution.py:33
  268.4 7.3 %collective-permute-start.40 = (f32[256,1]{1,0:T(8,128)S(1)}, f32[256,1]{1,0:T(8,128)S(1)}, u32[]{:S(2)}, u32[]{:S(2)}) collective-permute-start(f32[256,1]{1,0:T(8,128)S(1)} %get-tuple-element.19), channel_id=1, source_target_pairs={{1,0},{2,1},{3,2},{4,3},{5,4},{6,5},{7,6},{8,7},{9,8},{10,9},{11,1... | collective-permute-start | bytes 3080 | tf_op jit(solution)/shard_map/ppermute | solution.py:23
  281.3 6.1 %collective-permute-start.42 = (f32[256,1]{1,0:T(8,128)S(1)}, f32[256,1]{1,0:T(8,128)S(1)}, u32[]{:S(2)}, u32[]{:S(2)}) collective-permute-start(f32[256,1]{1,0:T(8,128)S(1)} %get-tuple-element.17), channel_id=1, source_target_pairs={{1,0},{2,1},{3,2},{4,3},{5,4},{6,5},{7,6},{8,7},{9,8},{10,9},{11,1... | collective-permute-start | bytes 3080 | tf_op jit(solution)/shard_map/ppermute | solution.py:23
  292.7 10.4 %collective-permute-done.43 = f32[256,512]{1,0:T(8,128)S(1)} collective-permute-done((f32[256,512]{1,0:T(8,128)S(1)}, f32[256,512]{1,0:T(8,128)S(1)}, u32[]{:S(2)}, u32[]{:S(2)}) %collective-permute-start.43) | collective-permute-done | bytes 524320 | tf_op jit(solution)/shard_map/ppermute | solution.py:33
  305.1 7.3 %collective-permute-start.45 = (f32[256,1]{1,0:T(8,128)S(1)}, f32[256,1]{1,0:T(8,128)S(1)}, u32[]{:S(2)}, u32[]{:S(2)}) collective-permute-start(f32[256,1]{1,0:T(8,128)S(1)} %get-tuple-element.15), channel_id=1, source_target_pairs={{1,0},{2,1},{3,2},{4,3},{5,4},{6,5},{7,6},{8,7},{9,8},{10,9},{11,1... | collective-permute-start | bytes 3080 | tf_op jit(solution)/shard_map/ppermute | solution.py:23
  318.0 5.9 %collective-permute-start.47 = (f32[256,1]{1,0:T(8,128)S(1)}, f32[256,1]{1,0:T(8,128)S(1)}, u32[]{:S(2)}, u32[]{:S(2)}) collective-permute-start(f32[256,1]{1,0:T(8,128)S(1)} %get-tuple-element.13), channel_id=1, source_target_pairs={{1,0},{2,1},{3,2},{4,3},{5,4},{6,5},{7,6},{8,7},{9,8},{10,9},{11,1... | collective-permute-start | bytes 3080 | tf_op jit(solution)/shard_map/ppermute | solution.py:23
  329.4 10.4 %collective-permute-done.48 = f32[256,512]{1,0:T(8,128)S(1)} collective-permute-done((f32[256,512]{1,0:T(8,128)S(1)}, f32[256,512]{1,0:T(8,128)S(1)}, u32[]{:S(2)}, u32[]{:S(2)}) %collective-permute-start.48) | collective-permute-done | bytes 524320 | tf_op jit(solution)/shard_map/ppermute | solution.py:33
  339.8 1.9 collective-permute-start.49
  341.7 7.3 %collective-permute-start.50 = (f32[256,1]{1,0:T(8,128)S(1)}, f32[256,1]{1,0:T(8,128)S(1)}, u32[]{:S(2)}, u32[]{:S(2)}) collective-permute-start(f32[256,1]{1,0:T(8,128)S(1)} %get-tuple-element.11), channel_id=1, source_target_pairs={{1,0},{2,1},{3,2},{4,3},{5,4},{6,5},{7,6},{8,7},{9,8},{10,9},{11,1... | collective-permute-start | bytes 3080 | tf_op jit(solution)/shard_map/ppermute | solution.py:23
  354.7 5.9 %collective-permute-start.52 = (f32[256,1]{1,0:T(8,128)S(1)}, f32[256,1]{1,0:T(8,128)S(1)}, u32[]{:S(2)}, u32[]{:S(2)}) collective-permute-start(f32[256,1]{1,0:T(8,128)S(1)} %get-tuple-element.9), channel_id=1, source_target_pairs={{1,0},{2,1},{3,2},{4,3},{5,4},{6,5},{7,6},{8,7},{9,8},{10,9},{11,1... | collective-permute-start | bytes 3080 | tf_op jit(solution)/shard_map/ppermute | solution.py:23
  (134 shorter events, 107.6 us)
Async XLA Ops:
  1.1 13.0 %collective-permute-start = (f32[256,1]{1,0:T(8,128)S(1)}, f32[256,1]{1,0:T(8,128)S(1)}, u32[]{:S(2)}, u32[]{:S(2)}) collective-permute-start(f32[256,1]{1,0:T(8,128)S(1)} %get-tuple-element.54), channel_id=1, source_target_pairs={{0,1},{1,2},{2,3},{3,4},{4,5},{5,6},{6,7},{7,8},{8,9},{9,10},{10,1... | collective-permute-start | bytes 3080 | tf_op jit(solution)/shard_map/ppermute | solution.py:21
  3.1 13.0 %collective-permute-start.1 = (f32[256,1]{1,0:T(8,128)S(1)}, f32[256,1]{1,0:T(8,128)S(1)}, u32[]{:S(2)}, u32[]{:S(2)}) collective-permute-start(f32[256,1]{1,0:T(8,128)S(1)} %get-tuple-element.55), channel_id=1, source_target_pairs={{1,0},{2,1},{3,2},{4,3},{5,4},{6,5},{7,6},{8,7},{9,8},{10,9},{11,1... | collective-permute-start | bytes 3080 | tf_op jit(solution)/shard_map/ppermute | solution.py:23
  19.9 8.5 %collective-permute-start.2 = (f32[256,1]{1,0:T(8,128)S(1)}, f32[256,1]{1,0:T(8,128)S(1)}, u32[]{:S(2)}, u32[]{:S(2)}) collective-permute-start(f32[256,1]{1,0:T(8,128)S(1)} %get-tuple-element.50), channel_id=1, source_target_pairs={{0,1},{1,2},{2,3},{3,4},{4,5},{5,6},{6,7},{7,8},{8,9},{9,10},{10,1... | collective-permute-start | bytes 3080 | tf_op jit(solution)/shard_map/ppermute | solution.py:21
  21.8 8.4 %collective-permute-start.3 = (f32[256,1]{1,0:T(8,128)S(1)}, f32[256,1]{1,0:T(8,128)S(1)}, u32[]{:S(2)}, u32[]{:S(2)}) collective-permute-start(f32[256,1]{1,0:T(8,128)S(1)} %get-tuple-element.51), channel_id=1, source_target_pairs={{1,0},{2,1},{3,2},{4,3},{5,4},{6,5},{7,6},{8,7},{9,8},{10,9},{11,1... | collective-permute-start | bytes 3080 | tf_op jit(solution)/shard_map/ppermute | solution.py:23
  31.3 8.5 %collective-permute-start.4 = (f32[256,1]{1,0:T(8,128)S(1)}, f32[256,1]{1,0:T(8,128)S(1)}, u32[]{:S(2)}, u32[]{:S(2)}) collective-permute-start(f32[256,1]{1,0:T(8,128)S(1)} %get-tuple-element.48), channel_id=1, source_target_pairs={{0,1},{1,2},{2,3},{3,4},{4,5},{5,6},{6,7},{7,8},{8,9},{9,10},{10,1... | collective-permute-start | bytes 3080 | tf_op jit(solution)/shard_map/ppermute | solution.py:21
  33.2 8.4 %collective-permute-start.5 = (f32[256,1]{1,0:T(8,128)S(1)}, f32[256,1]{1,0:T(8,128)S(1)}, u32[]{:S(2)}, u32[]{:S(2)}) collective-permute-start(f32[256,1]{1,0:T(8,128)S(1)} %get-tuple-element.49), channel_id=1, source_target_pairs={{1,0},{2,1},{3,2},{4,3},{5,4},{6,5},{7,6},{8,7},{9,8},{10,9},{11,1... | collective-permute-start | bytes 3080 | tf_op jit(solution)/shard_map/ppermute | solution.py:23
  42.7 8.5 %collective-permute-start.6 = (f32[256,1]{1,0:T(8,128)S(1)}, f32[256,1]{1,0:T(8,128)S(1)}, u32[]{:S(2)}, u32[]{:S(2)}) collective-permute-start(f32[256,1]{1,0:T(8,128)S(1)} %get-tuple-element.46), channel_id=1, source_target_pairs={{0,1},{1,2},{2,3},{3,4},{4,5},{5,6},{6,7},{7,8},{8,9},{9,10},{10,1... | collective-permute-start | bytes 3080 | tf_op jit(solution)/shard_map/ppermute | solution.py:21
  44.7 8.4 %collective-permute-start.7 = (f32[256,1]{1,0:T(8,128)S(1)}, f32[256,1]{1,0:T(8,128)S(1)}, u32[]{:S(2)}, u32[]{:S(2)}) collective-permute-start(f32[256,1]{1,0:T(8,128)S(1)} %get-tuple-element.47), channel_id=1, source_target_pairs={{1,0},{2,1},{3,2},{4,3},{5,4},{6,5},{7,6},{8,7},{9,8},{10,9},{11,1... | collective-permute-start | bytes 3080 | tf_op jit(solution)/shard_map/ppermute | solution.py:23
  54.1 8.5 %collective-permute-start.8 = (f32[256,1]{1,0:T(8,128)S(1)}, f32[256,1]{1,0:T(8,128)S(1)}, u32[]{:S(2)}, u32[]{:S(2)}) collective-permute-start(f32[256,1]{1,0:T(8,128)S(1)} %get-tuple-element.44), channel_id=1, source_target_pairs={{0,1},{1,2},{2,3},{3,4},{4,5},{5,6},{6,7},{7,8},{8,9},{9,10},{10,1... | collective-permute-start | bytes 3080 | tf_op jit(solution)/shard_map/ppermute | solution.py:21
  56.1 8.4 %collective-permute-start.9 = (f32[256,1]{1,0:T(8,128)S(1)}, f32[256,1]{1,0:T(8,128)S(1)}, u32[]{:S(2)}, u32[]{:S(2)}) collective-permute-start(f32[256,1]{1,0:T(8,128)S(1)} %get-tuple-element.45), channel_id=1, source_target_pairs={{1,0},{2,1},{3,2},{4,3},{5,4},{6,5},{7,6},{8,7},{9,8},{10,9},{11,1... | collective-permute-start | bytes 3080 | tf_op jit(solution)/shard_map/ppermute | solution.py:23
  65.6 8.5 %collective-permute-start.10 = (f32[256,1]{1,0:T(8,128)S(1)}, f32[256,1]{1,0:T(8,128)S(1)}, u32[]{:S(2)}, u32[]{:S(2)}) collective-permute-start(f32[256,1]{1,0:T(8,128)S(1)} %get-tuple-element.42), channel_id=1, source_target_pairs={{0,1},{1,2},{2,3},{3,4},{4,5},{5,6},{6,7},{7,8},{8,9},{9,10},{10,1... | collective-permute-start | bytes 3080 | tf_op jit(solution)/shard_map/ppermute | solution.py:21
  67.5 8.4 %collective-permute-start.11 = (f32[256,1]{1,0:T(8,128)S(1)}, f32[256,1]{1,0:T(8,128)S(1)}, u32[]{:S(2)}, u32[]{:S(2)}) collective-permute-start(f32[256,1]{1,0:T(8,128)S(1)} %get-tuple-element.43), channel_id=1, source_target_pairs={{1,0},{2,1},{3,2},{4,3},{5,4},{6,5},{7,6},{8,7},{9,8},{10,9},{11,1... | collective-permute-start | bytes 3080 | tf_op jit(solution)/shard_map/ppermute | solution.py:23
  77.6 8.7 %collective-permute-start.12 = (f32[256,1]{1,0:T(8,128)}, f32[256,1]{1,0:T(8,128)S(1)}, u32[]{:S(2)}, u32[]{:S(2)}) collective-permute-start(f32[256,1]{1,0:T(8,128)} %get-tuple-element.40), channel_id=1, source_target_pairs={{0,1},{1,2},{2,3},{3,4},{4,5},{5,6},{6,7},{7,8},{8,9},{9,10},{10,1... | collective-permute-start | bytes 3080 | tf_op jit(solution)/shard_map/ppermute | solution.py:21
  79.5 8.4 %collective-permute-start.13 = (f32[256,1]{1,0:T(8,128)S(1)}, f32[256,1]{1,0:T(8,128)S(1)}, u32[]{:S(2)}, u32[]{:S(2)}) collective-permute-start(f32[256,1]{1,0:T(8,128)S(1)} %get-tuple-element.41), channel_id=1, source_target_pairs={{1,0},{2,1},{3,2},{4,3},{5,4},{6,5},{7,6},{8,7},{9,8},{10,9},{11,1... | collective-permute-start | bytes 3080 | tf_op jit(solution)/shard_map/ppermute | solution.py:23
  89.2 15.6 %collective-permute-start.14 = (f32[256,1]{1,0:T(8,128)S(1)}, f32[256,1]{1,0:T(8,128)S(1)}, u32[]{:S(2)}, u32[]{:S(2)}) collective-permute-start(f32[256,1]{1,0:T(8,128)S(1)} %get-tuple-element.36), channel_id=1, source_target_pairs={{0,1},{1,2},{2,3},{3,4},{4,5},{5,6},{6,7},{7,8},{8,9},{9,10},{10,1... | collective-permute-start | bytes 3080 | tf_op jit(solution)/shard_map/ppermute | solution.py:21
  91.1 13.7 %collective-permute-start.15 = (f32[256,1]{1,0:T(8,128)S(1)}, f32[256,1]{1,0:T(8,128)S(1)}, u32[]{:S(2)}, u32[]{:S(2)}) collective-permute-start(f32[256,1]{1,0:T(8,128)S(1)} %get-tuple-element.37), channel_id=1, source_target_pairs={{1,0},{2,1},{3,2},{4,3},{5,4},{6,5},{7,6},{8,7},{9,8},{10,9},{11,1... | collective-permute-start | bytes 3080 | tf_op jit(solution)/shard_map/ppermute | solution.py:23
  109.1 12.3 %collective-permute-start.18 = (f32[256,512]{1,0:T(8,128)S(1)}, f32[256,512]{1,0:T(8,128)S(1)}, u32[]{:S(2)}, u32[]{:S(2)}) collective-permute-start(f32[256,512]{1,0:T(8,128)S(1)} %subtract_select_fusion), channel_id=1, source_target_pairs={{0,64},{64,128},{128,192},{192,256},{256,320},{320,384},{384,448},... | collective-permute-start | bytes 1572872 | tf_op jit(solution)/shard_map/ppermute | solution.py:33
  132.8 8.5 %collective-permute-start.21 = (f32[256,1]{1,0:T(8,128)S(1)}, f32[256,1]{1,0:T(8,128)S(1)}, u32[]{:S(2)}, u32[]{:S(2)}) collective-permute-start(f32[256,1]{1,0:T(8,128)S(1)} %get-tuple-element.32), channel_id=1, source_target_pairs={{0,1},{1,2},{2,3},{3,4},{4,5},{5,6},{6,7},{7,8},{8,9},{9,10},{10,1... | collective-permute-start | bytes 3080 | tf_op jit(solution)/shard_map/ppermute | solution.py:21
  134.7 8.4 %collective-permute-start.22 = (f32[256,1]{1,0:T(8,128)S(1)}, f32[256,1]{1,0:T(8,128)S(1)}, u32[]{:S(2)}, u32[]{:S(2)}) collective-permute-start(f32[256,1]{1,0:T(8,128)S(1)} %get-tuple-element.33), channel_id=1, source_target_pairs={{1,0},{2,1},{3,2},{4,3},{5,4},{6,5},{7,6},{8,7},{9,8},{10,9},{11,1... | collective-permute-start | bytes 3080 | tf_op jit(solution)/shard_map/ppermute | solution.py:23
  144.1 12.3 %collective-permute-start.23 = (f32[256,512]{1,0:T(8,128)S(1)}, f32[256,512]{1,0:T(8,128)S(1)}, u32[]{:S(2)}, u32[]{:S(2)}) collective-permute-start(f32[256,512]{1,0:T(8,128)S(1)} %fusion.181), channel_id=1, source_target_pairs={{0,64},{64,128},{128,192},{192,256},{256,320},{320,384},{384,448},... | collective-permute-start | bytes 1572872 | tf_op jit(solution)/shard_map/ppermute | solution.py:33
  156.5 10.0 %collective-permute-start.24 = (f32[256,1]{1,0:T(8,128)S(1)}, f32[256,1]{1,0:T(8,128)S(1)}, u32[]{:S(2)}, u32[]{:S(2)}) collective-permute-start(f32[256,1]{1,0:T(8,128)S(1)} %get-tuple-element.30), channel_id=1, source_target_pairs={{0,1},{1,2},{2,3},{3,4},{4,5},{5,6},{6,7},{7,8},{8,9},{9,10},{10,1... | collective-permute-start | bytes 3080 | tf_op jit(solution)/shard_map/ppermute | solution.py:21
  158.5 9.9 %collective-permute-start.25 = (f32[256,1]{1,0:T(8,128)S(1)}, f32[256,1]{1,0:T(8,128)S(1)}, u32[]{:S(2)}, u32[]{:S(2)}) collective-permute-start(f32[256,1]{1,0:T(8,128)S(1)} %get-tuple-element.31), channel_id=1, source_target_pairs={{1,0},{2,1},{3,2},{4,3},{5,4},{6,5},{7,6},{8,7},{9,8},{10,9},{11,1... | collective-permute-start | bytes 3080 | tf_op jit(solution)/shard_map/ppermute | solution.py:23
  169.4 8.5 %collective-permute-start.26 = (f32[256,1]{1,0:T(8,128)S(1)}, f32[256,1]{1,0:T(8,128)S(1)}, u32[]{:S(2)}, u32[]{:S(2)}) collective-permute-start(f32[256,1]{1,0:T(8,128)S(1)} %get-tuple-element.28), channel_id=1, source_target_pairs={{0,1},{1,2},{2,3},{3,4},{4,5},{5,6},{6,7},{7,8},{8,9},{9,10},{10,1... | collective-permute-start | bytes 3080 | tf_op jit(solution)/shard_map/ppermute | solution.py:21
  171.4 8.4 %collective-permute-start.27 = (f32[256,1]{1,0:T(8,128)S(1)}, f32[256,1]{1,0:T(8,128)S(1)}, u32[]{:S(2)}, u32[]{:S(2)}) collective-permute-start(f32[256,1]{1,0:T(8,128)S(1)} %get-tuple-element.29), channel_id=1, source_target_pairs={{1,0},{2,1},{3,2},{4,3},{5,4},{6,5},{7,6},{8,7},{9,8},{10,9},{11,1... | collective-permute-start | bytes 3080 | tf_op jit(solution)/shard_map/ppermute | solution.py:23
  180.8 12.3 %collective-permute-start.28 = (f32[256,512]{1,0:T(8,128)S(1)}, f32[256,512]{1,0:T(8,128)S(1)}, u32[]{:S(2)}, u32[]{:S(2)}) collective-permute-start(f32[256,512]{1,0:T(8,128)S(1)} %fusion.152), channel_id=1, source_target_pairs={{0,64},{64,128},{128,192},{192,256},{256,320},{320,384},{384,448},... | collective-permute-start | bytes 1572872 | tf_op jit(solution)/shard_map/ppermute | solution.py:33
  193.2 10.0 %collective-permute-start.29 = (f32[256,1]{1,0:T(8,128)S(1)}, f32[256,1]{1,0:T(8,128)S(1)}, u32[]{:S(2)}, u32[]{:S(2)}) collective-permute-start(f32[256,1]{1,0:T(8,128)S(1)} %get-tuple-element.26), channel_id=1, source_target_pairs={{0,1},{1,2},{2,3},{3,4},{4,5},{5,6},{6,7},{7,8},{8,9},{9,10},{10,1... | collective-permute-start | bytes 3080 | tf_op jit(solution)/shard_map/ppermute | solution.py:21
  195.1 9.9 %collective-permute-start.30 = (f32[256,1]{1,0:T(8,128)S(1)}, f32[256,1]{1,0:T(8,128)S(1)}, u32[]{:S(2)}, u32[]{:S(2)}) collective-permute-start(f32[256,1]{1,0:T(8,128)S(1)} %get-tuple-element.27), channel_id=1, source_target_pairs={{1,0},{2,1},{3,2},{4,3},{5,4},{6,5},{7,6},{8,7},{9,8},{10,9},{11,1... | collective-permute-start | bytes 3080 | tf_op jit(solution)/shard_map/ppermute | solution.py:23
  206.1 8.5 %collective-permute-start.31 = (f32[256,1]{1,0:T(8,128)S(1)}, f32[256,1]{1,0:T(8,128)S(1)}, u32[]{:S(2)}, u32[]{:S(2)}) collective-permute-start(f32[256,1]{1,0:T(8,128)S(1)} %get-tuple-element.24), channel_id=1, source_target_pairs={{0,1},{1,2},{2,3},{3,4},{4,5},{5,6},{6,7},{7,8},{8,9},{9,10},{10,1... | collective-permute-start | bytes 3080 | tf_op jit(solution)/shard_map/ppermute | solution.py:21
  208.0 8.4 %collective-permute-start.32 = (f32[256,1]{1,0:T(8,128)S(1)}, f32[256,1]{1,0:T(8,128)S(1)}, u32[]{:S(2)}, u32[]{:S(2)}) collective-permute-start(f32[256,1]{1,0:T(8,128)S(1)} %get-tuple-element.25), channel_id=1, source_target_pairs={{1,0},{2,1},{3,2},{4,3},{5,4},{6,5},{7,6},{8,7},{9,8},{10,9},{11,1... | collective-permute-start | bytes 3080 | tf_op jit(solution)/shard_map/ppermute | solution.py:23
  217.5 12.3 %collective-permute-start.33 = (f32[256,512]{1,0:T(8,128)S(1)}, f32[256,512]{1,0:T(8,128)S(1)}, u32[]{:S(2)}, u32[]{:S(2)}) collective-permute-start(f32[256,512]{1,0:T(8,128)S(1)} %fusion.123), channel_id=1, source_target_pairs={{0,64},{64,128},{128,192},{192,256},{256,320},{320,384},{384,448},... | collective-permute-start | bytes 1572872 | tf_op jit(solution)/shard_map/ppermute | solution.py:33
  229.8 10.0 %collective-permute-start.34 = (f32[256,1]{1,0:T(8,128)S(1)}, f32[256,1]{1,0:T(8,128)S(1)}, u32[]{:S(2)}, u32[]{:S(2)}) collective-permute-start(f32[256,1]{1,0:T(8,128)S(1)} %get-tuple-element.22), channel_id=1, source_target_pairs={{0,1},{1,2},{2,3},{3,4},{4,5},{5,6},{6,7},{7,8},{8,9},{9,10},{10,1... | collective-permute-start | bytes 3080 | tf_op jit(solution)/shard_map/ppermute | solution.py:21
  231.8 9.9 %collective-permute-start.35 = (f32[256,1]{1,0:T(8,128)S(1)}, f32[256,1]{1,0:T(8,128)S(1)}, u32[]{:S(2)}, u32[]{:S(2)}) collective-permute-start(f32[256,1]{1,0:T(8,128)S(1)} %get-tuple-element.23), channel_id=1, source_target_pairs={{1,0},{2,1},{3,2},{4,3},{5,4},{6,5},{7,6},{8,7},{9,8},{10,9},{11,1... | collective-permute-start | bytes 3080 | tf_op jit(solution)/shard_map/ppermute | solution.py:23
  242.8 8.5 %collective-permute-start.36 = (f32[256,1]{1,0:T(8,128)S(1)}, f32[256,1]{1,0:T(8,128)S(1)}, u32[]{:S(2)}, u32[]{:S(2)}) collective-permute-start(f32[256,1]{1,0:T(8,128)S(1)} %get-tuple-element.20), channel_id=1, source_target_pairs={{0,1},{1,2},{2,3},{3,4},{4,5},{5,6},{6,7},{7,8},{8,9},{9,10},{10,1... | collective-permute-start | bytes 3080 | tf_op jit(solution)/shard_map/ppermute | solution.py:21
  244.7 8.4 %collective-permute-start.37 = (f32[256,1]{1,0:T(8,128)S(1)}, f32[256,1]{1,0:T(8,128)S(1)}, u32[]{:S(2)}, u32[]{:S(2)}) collective-permute-start(f32[256,1]{1,0:T(8,128)S(1)} %get-tuple-element.21), channel_id=1, source_target_pairs={{1,0},{2,1},{3,2},{4,3},{5,4},{6,5},{7,6},{8,7},{9,8},{10,9},{11,1... | collective-permute-start | bytes 3080 | tf_op jit(solution)/shard_map/ppermute | solution.py:23
  254.1 12.3 %collective-permute-start.38 = (f32[256,512]{1,0:T(8,128)S(1)}, f32[256,512]{1,0:T(8,128)S(1)}, u32[]{:S(2)}, u32[]{:S(2)}) collective-permute-start(f32[256,512]{1,0:T(8,128)S(1)} %fusion.94), channel_id=1, source_target_pairs={{0,64},{64,128},{128,192},{192,256},{256,320},{320,384},{384,448},... | collective-permute-start | bytes 1572872 | tf_op jit(solution)/shard_map/ppermute | solution.py:33
  266.5 10.0 %collective-permute-start.39 = (f32[256,1]{1,0:T(8,128)S(1)}, f32[256,1]{1,0:T(8,128)S(1)}, u32[]{:S(2)}, u32[]{:S(2)}) collective-permute-start(f32[256,1]{1,0:T(8,128)S(1)} %get-tuple-element.18), channel_id=1, source_target_pairs={{0,1},{1,2},{2,3},{3,4},{4,5},{5,6},{6,7},{7,8},{8,9},{9,10},{10,1... | collective-permute-start | bytes 3080 | tf_op jit(solution)/shard_map/ppermute | solution.py:21
  268.4 9.9 %collective-permute-start.40 = (f32[256,1]{1,0:T(8,128)S(1)}, f32[256,1]{1,0:T(8,128)S(1)}, u32[]{:S(2)}, u32[]{:S(2)}) collective-permute-start(f32[256,1]{1,0:T(8,128)S(1)} %get-tuple-element.19), channel_id=1, source_target_pairs={{1,0},{2,1},{3,2},{4,3},{5,4},{6,5},{7,6},{8,7},{9,8},{10,9},{11,1... | collective-permute-start | bytes 3080 | tf_op jit(solution)/shard_map/ppermute | solution.py:23
  279.4 8.5 %collective-permute-start.41 = (f32[256,1]{1,0:T(8,128)S(1)}, f32[256,1]{1,0:T(8,128)S(1)}, u32[]{:S(2)}, u32[]{:S(2)}) collective-permute-start(f32[256,1]{1,0:T(8,128)S(1)} %get-tuple-element.16), channel_id=1, source_target_pairs={{0,1},{1,2},{2,3},{3,4},{4,5},{5,6},{6,7},{7,8},{8,9},{9,10},{10,1... | collective-permute-start | bytes 3080 | tf_op jit(solution)/shard_map/ppermute | solution.py:21
  281.3 8.4 %collective-permute-start.42 = (f32[256,1]{1,0:T(8,128)S(1)}, f32[256,1]{1,0:T(8,128)S(1)}, u32[]{:S(2)}, u32[]{:S(2)}) collective-permute-start(f32[256,1]{1,0:T(8,128)S(1)} %get-tuple-element.17), channel_id=1, source_target_pairs={{1,0},{2,1},{3,2},{4,3},{5,4},{6,5},{7,6},{8,7},{9,8},{10,9},{11,1... | collective-permute-start | bytes 3080 | tf_op jit(solution)/shard_map/ppermute | solution.py:23
  290.8 12.3 %collective-permute-start.43 = (f32[256,512]{1,0:T(8,128)S(1)}, f32[256,512]{1,0:T(8,128)S(1)}, u32[]{:S(2)}, u32[]{:S(2)}) collective-permute-start(f32[256,512]{1,0:T(8,128)S(1)} %fusion.65), channel_id=1, source_target_pairs={{0,64},{64,128},{128,192},{192,256},{256,320},{320,384},{384,448},... | collective-permute-start | bytes 1572872 | tf_op jit(solution)/shard_map/ppermute | solution.py:33
  303.2 10.0 %collective-permute-start.44 = (f32[256,1]{1,0:T(8,128)S(1)}, f32[256,1]{1,0:T(8,128)S(1)}, u32[]{:S(2)}, u32[]{:S(2)}) collective-permute-start(f32[256,1]{1,0:T(8,128)S(1)} %get-tuple-element.14), channel_id=1, source_target_pairs={{0,1},{1,2},{2,3},{3,4},{4,5},{5,6},{6,7},{7,8},{8,9},{9,10},{10,1... | collective-permute-start | bytes 3080 | tf_op jit(solution)/shard_map/ppermute | solution.py:21
  305.1 9.9 %collective-permute-start.45 = (f32[256,1]{1,0:T(8,128)S(1)}, f32[256,1]{1,0:T(8,128)S(1)}, u32[]{:S(2)}, u32[]{:S(2)}) collective-permute-start(f32[256,1]{1,0:T(8,128)S(1)} %get-tuple-element.15), channel_id=1, source_target_pairs={{1,0},{2,1},{3,2},{4,3},{5,4},{6,5},{7,6},{8,7},{9,8},{10,9},{11,1... | collective-permute-start | bytes 3080 | tf_op jit(solution)/shard_map/ppermute | solution.py:23
  316.1 8.5 %collective-permute-start.46 = (f32[256,1]{1,0:T(8,128)S(1)}, f32[256,1]{1,0:T(8,128)S(1)}, u32[]{:S(2)}, u32[]{:S(2)}) collective-permute-start(f32[256,1]{1,0:T(8,128)S(1)} %get-tuple-element.12), channel_id=1, source_target_pairs={{0,1},{1,2},{2,3},{3,4},{4,5},{5,6},{6,7},{7,8},{8,9},{9,10},{10,1... | collective-permute-start | bytes 3080 | tf_op jit(solution)/shard_map/ppermute | solution.py:21
  318.0 8.4 %collective-permute-start.47 = (f32[256,1]{1,0:T(8,128)S(1)}, f32[256,1]{1,0:T(8,128)S(1)}, u32[]{:S(2)}, u32[]{:S(2)}) collective-permute-start(f32[256,1]{1,0:T(8,128)S(1)} %get-tuple-element.13), channel_id=1, source_target_pairs={{1,0},{2,1},{3,2},{4,3},{5,4},{6,5},{7,6},{8,7},{9,8},{10,9},{11,1... | collective-permute-start | bytes 3080 | tf_op jit(solution)/shard_map/ppermute | solution.py:23
  327.4 12.3 %collective-permute-start.48 = (f32[256,512]{1,0:T(8,128)S(1)}, f32[256,512]{1,0:T(8,128)S(1)}, u32[]{:S(2)}, u32[]{:S(2)}) collective-permute-start(f32[256,512]{1,0:T(8,128)S(1)} %fusion.36), channel_id=1, source_target_pairs={{0,64},{64,128},{128,192},{192,256},{256,320},{320,384},{384,448},... | collective-permute-start | bytes 1572872 | tf_op jit(solution)/shard_map/ppermute | solution.py:33
  339.8 10.0 %collective-permute-start.49 = (f32[256,1]{1,0:T(8,128)S(1)}, f32[256,1]{1,0:T(8,128)S(1)}, u32[]{:S(2)}, u32[]{:S(2)}) collective-permute-start(f32[256,1]{1,0:T(8,128)S(1)} %get-tuple-element.10), channel_id=1, source_target_pairs={{0,1},{1,2},{2,3},{3,4},{4,5},{5,6},{6,7},{7,8},{8,9},{9,10},{10,1... | collective-permute-start | bytes 3080 | tf_op jit(solution)/shard_map/ppermute | solution.py:21
  341.7 9.9 %collective-permute-start.50 = (f32[256,1]{1,0:T(8,128)S(1)}, f32[256,1]{1,0:T(8,128)S(1)}, u32[]{:S(2)}, u32[]{:S(2)}) collective-permute-start(f32[256,1]{1,0:T(8,128)S(1)} %get-tuple-element.11), channel_id=1, source_target_pairs={{1,0},{2,1},{3,2},{4,3},{5,4},{6,5},{7,6},{8,7},{9,8},{10,9},{11,1... | collective-permute-start | bytes 3080 | tf_op jit(solution)/shard_map/ppermute | solution.py:23
  352.7 8.5 %collective-permute-start.51 = (f32[256,1]{1,0:T(8,128)S(1)}, f32[256,1]{1,0:T(8,128)S(1)}, u32[]{:S(2)}, u32[]{:S(2)}) collective-permute-start(f32[256,1]{1,0:T(8,128)S(1)} %get-tuple-element.8), channel_id=1, source_target_pairs={{0,1},{1,2},{2,3},{3,4},{4,5},{5,6},{6,7},{7,8},{8,9},{9,10},{10,1... | collective-permute-start | bytes 3080 | tf_op jit(solution)/shard_map/ppermute | solution.py:21
  (9 other events, 90.6 us)
where the time goes:
time: 367 us; the launch traced here: 365 us
  starting transfers between devices  207 us (56%)
  waiting for transfers between devices  126 us (34%)
  other arithmetic  26.9 us (7%)
  local copies, waits for them, and re-layouts  3.89 us (1%)
    ppermute x23, starting transfers between devices, with_halo(): lax.ppermute(head, axis, [((i + 1) % count, i) for i in range(ends)])  149 us
    ppermute x7, waiting for transfers between devices, shifted(): return lax.ppermute(block, axis, route)  71.8 us
    ppermute x23, starting transfers between devices, with_halo(): lax.ppermute(tail, axis, [(i, (i + 1) % count) for i in range(ends)])  44.2 us
    ppermute x23, waiting for transfers between devices, with_halo(): lax.ppermute(head, axis, [((i + 1) % count, i) for i in range(ends)])  39.3 us
    ppermute x23, waiting for transfers between devices, with_halo(): lax.ppermute(tail, axis, [(i, (i + 1) % count) for i in range(ends)])  14.9 us
    ppermute x7, starting transfers between devices, shifted(): return lax.ppermute(block, axis, route)  14.1 us
    add x14, other arithmetic, advance(): return mid - size * moved + size * coef[2] * spread  11.8 us
    concatenate x23, other arithmetic, with_halo(): jnp.concatenate([lax.ppermute(tail, axis, [(i, (i + 1) % count) for i in...  7.67 us
  transfers between devices with their start and end apart: 53, of which 51 were waited for; matrix products, arithmetic and copies ran while one was open for 0% of the time, Pallas kernels for 0%

commit v1 on v0

v1 whole, which is shorter than its diff:
```python
import jax
import jax.numpy as jnp
from jax import lax
from jax.sharding import PartitionSpec as P

FINE = 8
CSTEPS = 2


DT = 1.0 / 12.0


def shifted(block, axis, distance):
    devices = range(lax.axis_size(axis))
    route = [(i - distance, i) for i in devices if i - distance in devices]
    return lax.ppermute(block, axis, route)


def with_halo(cells, axis, width):
    head = cells[..., :width]
    tail = cells[..., cells.shape[-1] - width:]
    left = shifted(tail, axis, 1)
    right = shifted(head, axis, -1)
    return jnp.concatenate([left, cells, right], axis=-1)


def advance(wide, coef, size):
    padded = jnp.pad(wide, ((1, 1), (0, 0)))
    mid = padded[1:-1, 1:-1]
    left = padded[1:-1, :-2]
    right = padded[1:-1, 2:]
    upper = padded[:-2, 1:-1]
    lower = padded[2:, 1:-1]
    moved = jnp.maximum(coef[0], 0.0) * (mid - left) + jnp.minimum(coef[0], 0.0) * (right - mid)
    moved = (
        moved
        + jnp.maximum(coef[1], 0.0) * (mid - upper)
        + jnp.minimum(coef[1], 0.0) * (lower - mid)
    )
    spread = upper + lower + left + right - 4.0 * mid
    return mid - size * moved + size * coef[2] * spread


def local(starts, vel_x, vel_y, kappa):
    slices = lax.axis_size("tm")
    chain = CSTEPS * (slices - 1)
    top = FINE + chain
    n = starts.shape[-1]
    packed = jnp.stack([starts[0], vel_x, vel_y, kappa])
    wide = with_halo(packed, "space", top)
    state = wide[0]
    coef_all = wide[1:]

    def coef_at(h):
        return coef_all[:, :, top - h: top + n + h]

    def run(field, h, steps, size):
        for _ in range(steps):
            h -= 1
            field = advance(field, coef_at(h), size)
        return field, h

    field, h = run(state, top, FINE, DT)
    start_c = state[:, top - chain - CSTEPS: top + n + chain + CSTEPS]
    old_coarse, _ = run(start_c, chain + CSTEPS, CSTEPS, DT * FINE / CSTEPS)
    first = lax.axis_index("tm") == 0
    carried = jnp.where(first, field, field - old_coarse)
    current = carried
    h = chain
    for turn in range(slices - 1):
        incoming = shifted(current, "tm", 1)
        moved, h = run(incoming, h, CSTEPS, DT * FINE / CSTEPS)
        current = carried[:, chain - h: chain + n + h] + moved
    return current[None]


def solution(mesh):
    placed = (P("tm", None, "space"), P(None, "space"), P(None, "space"), P(None, "space"))
    return jax.shard_map(
        local, mesh=mesh, in_specs=placed, out_specs=P("tm", None, "space"), check_vma=False
    )
```

time: 367 us -> 147 us (0.40)
  the two profiles are of different devices: /device:TPU:36 before, /device:TPU:228 now
where the time goes in v1:
time: 147 us
  waiting for transfers between devices  104 us (71%)
  starting transfers between devices  19.9 us (14%)
  other arithmetic  18.1 us (12%)
  local copies, waits for them, and re-layouts  4.04 us (3%)
    ppermute x9, waiting for transfers between devices, shifted(): return lax.ppermute(block, axis, route)  104 us
    ppermute x9, starting transfers between devices, shifted(): return lax.ppermute(block, axis, route)  19.9 us
    add x14, other arithmetic, advance(): return mid - size * moved + size * coef[2] * spread  11.2 us
    add x6, other arithmetic, local(): current = carried[:, chain - h:chain + n + h] + moved  4.71 us
    unnamed x8, local copies, waits for them, and re-layouts  2.96 us
  transfers between devices with their start and end apart: 9, of which 9 were waited for; matrix products, arithmetic and copies ran while one was open for 0% of the time, Pallas kernels for 0%

profile of v1, /device:TPU:228, one launch (start us, length us, event | category | flops | bytes accessed | tf_op | source)
XLA Modules:
  0.0 146.6 jit_solution(7777058477192087914)
XLA Ops:
  0.0 1.3 copy.5
  1.3 1.2 copy.6
  2.6 0.0 copy-done
  2.6 0.2 copy.7
  2.8 0.0 copy-done.1
  2.8 0.2 copy.8
  3.0 1.9 %collective-permute-start = (f32[4,256,22]{1,2,0:T(8,128)S(1)}, f32[4,256,22]{1,2,0:T(8,128)S(1)}, u32[]{:S(2)}, u32[]{:S(2)}) collective-permute-start(f32[4,256,22]{1,2,0:T(8,128)S(1)} %get-tuple-element.7), channel_id=1, source_target_pairs={{0,1},{1,2},{2,3},{3,4},{4,5},{5,6},{6,7},{7,8},{8,9},{9,10},{10,1... | collective-permute-start | bytes 270344 | tf_op jit(solution)/shard_map/ppermute | solution.py:16
  5.0 3.6 %collective-permute-start.1 = (f32[4,256,22]{1,2,0:T(8,128)S(1)}, f32[4,256,22]{1,2,0:T(8,128)S(1)}, u32[]{:S(2)}, u32[]{:S(2)}) collective-permute-start(f32[4,256,22]{1,2,0:T(8,128)S(1)} %get-tuple-element.8), channel_id=1, source_target_pairs={{1,0},{2,1},{3,2},{4,3},{5,4},{6,5},{7,6},{8,7},{9,8},{10,9},{11,1... | collective-permute-start | bytes 270344 | tf_op jit(solution)/shard_map/ppermute | solution.py:16
  8.6 0.4 collective-permute-done
  9.0 2.4 %collective-permute-done.1 = f32[4,256,22]{1,2,0:T(8,128)S(1)} collective-permute-done((f32[4,256,22]{1,2,0:T(8,128)S(1)}, f32[4,256,22]{1,2,0:T(8,128)S(1)}, u32[]{:S(2)}, u32[]{:S(2)}) %collective-permute-start.1) | collective-permute-done | bytes 90144 | tf_op jit(solution)/shard_map/ppermute | solution.py:16
  11.3 0.2 pad_maximum_fusion
  11.6 0.8 fusion.2
  12.4 0.8 fusion.19
  13.2 0.8 fusion.16
  14.0 0.8 fusion.13
  14.8 0.8 fusion.10
  15.5 0.8 fusion.45
  16.3 1.3 fusion.64
  17.6 1.3 subtract_select_fusion
  18.9 2.6 %collective-permute-start.2 = (f32[256,540]{0,1:T(8,128)S(1)}, f32[256,540]{0,1:T(8,128)S(1)}, u32[]{:S(2)}, u32[]{:S(2)}) collective-permute-start(f32[256,540]{0,1:T(8,128)S(1)} %subtract_select_fusion), channel_id=1, source_target_pairs={{0,64},{64,128},{128,192},{192,256},{256,320},{320,384},{384,448},... | collective-permute-start | bytes 1658888 | tf_op jit(solution)/shard_map/ppermute | solution.py:16
  21.5 12.5 %collective-permute-done.2 = f32[256,540]{0,1:T(8,128)S(1)} collective-permute-done((f32[256,540]{0,1:T(8,128)S(1)}, f32[256,540]{0,1:T(8,128)S(1)}, u32[]{:S(2)}, u32[]{:S(2)}) %collective-permute-start.2) | collective-permute-done | bytes 552992 | tf_op jit(solution)/shard_map/ppermute | solution.py:16
  34.1 0.8 fusion.42
  34.8 0.8 fusion.93
  35.7 2.1 %collective-permute-start.3 = (f32[256,536]{0,1:T(8,128)S(1)}, f32[256,536]{0,1:T(8,128)S(1)}, u32[]{:S(2)}, u32[]{:S(2)}) collective-permute-start(f32[256,536]{0,1:T(8,128)S(1)} %fusion.93), channel_id=1, source_target_pairs={{0,64},{64,128},{128,192},{192,256},{256,320},{320,384},{384,448},... | collective-permute-start | bytes 1646600 | tf_op jit(solution)/shard_map/ppermute | solution.py:16
  37.8 14.0 %collective-permute-done.3 = f32[256,536]{0,1:T(8,128)S(1)} collective-permute-done((f32[256,536]{0,1:T(8,128)S(1)}, f32[256,536]{0,1:T(8,128)S(1)}, u32[]{:S(2)}, u32[]{:S(2)}) %collective-permute-start.3) | collective-permute-done | bytes 548896 | tf_op jit(solution)/shard_map/ppermute | solution.py:16
  51.8 0.8 fusion.89
  52.5 0.8 fusion.86
  53.4 1.9 %collective-permute-start.4 = (f32[256,532]{0,1:T(8,128)S(1)}, f32[256,532]{0,1:T(8,128)S(1)}, u32[]{:S(2)}, u32[]{:S(2)}) collective-permute-start(f32[256,532]{0,1:T(8,128)S(1)} %fusion.86), channel_id=1, source_target_pairs={{0,64},{64,128},{128,192},{192,256},{256,320},{320,384},{384,448},... | collective-permute-start | bytes 1634312 | tf_op jit(solution)/shard_map/ppermute | solution.py:16
  55.3 15.3 %collective-permute-done.4 = f32[256,532]{0,1:T(8,128)S(1)} collective-permute-done((f32[256,532]{0,1:T(8,128)S(1)}, f32[256,532]{0,1:T(8,128)S(1)}, u32[]{:S(2)}, u32[]{:S(2)}) %collective-permute-start.4) | collective-permute-done | bytes 544800 | tf_op jit(solution)/shard_map/ppermute | solution.py:16
  70.6 0.8 fusion.82
  71.4 0.8 fusion.127
  72.2 1.9 %collective-permute-start.5 = (f32[256,528]{0,1:T(8,128)S(1)}, f32[256,528]{0,1:T(8,128)S(1)}, u32[]{:S(2)}, u32[]{:S(2)}) collective-permute-start(f32[256,528]{0,1:T(8,128)S(1)} %fusion.127), channel_id=1, source_target_pairs={{0,64},{64,128},{128,192},{192,256},{256,320},{320,384},{384,448},... | collective-permute-start | bytes 1622024 | tf_op jit(solution)/shard_map/ppermute | solution.py:16
  74.1 16.3 %collective-permute-done.5 = f32[256,528]{0,1:T(8,128)S(1)} collective-permute-done((f32[256,528]{0,1:T(8,128)S(1)}, f32[256,528]{0,1:T(8,128)S(1)}, u32[]{:S(2)}, u32[]{:S(2)}) %collective-permute-start.5) | collective-permute-done | bytes 540704 | tf_op jit(solution)/shard_map/ppermute | solution.py:16
  90.4 0.8 fusion.123
  91.1 0.7 fusion.120
  91.8 1.9 %collective-permute-start.6 = (f32[256,524]{0,1:T(8,128)S(1)}, f32[256,524]{0,1:T(8,128)S(1)}, u32[]{:S(2)}, u32[]{:S(2)}) collective-permute-start(f32[256,524]{0,1:T(8,128)S(1)} %fusion.120), channel_id=1, source_target_pairs={{0,64},{64,128},{128,192},{192,256},{256,320},{320,384},{384,448},... | collective-permute-start | bytes 1609736 | tf_op jit(solution)/shard_map/ppermute | solution.py:16
  93.7 15.5 %collective-permute-done.6 = f32[256,524]{0,1:T(8,128)S(1)} collective-permute-done((f32[256,524]{0,1:T(8,128)S(1)}, f32[256,524]{0,1:T(8,128)S(1)}, u32[]{:S(2)}, u32[]{:S(2)}) %collective-permute-start.6) | collective-permute-done | bytes 536608 | tf_op jit(solution)/shard_map/ppermute | solution.py:16
  109.2 0.7 fusion.116
  110.0 0.8 fusion.161
  110.7 1.9 %collective-permute-start.7 = (f32[256,520]{0,1:T(8,128)S(1)}, f32[256,520]{0,1:T(8,128)S(1)}, u32[]{:S(2)}, u32[]{:S(2)}) collective-permute-start(f32[256,520]{0,1:T(8,128)S(1)} %fusion.161), channel_id=1, source_target_pairs={{0,64},{64,128},{128,192},{192,256},{256,320},{320,384},{384,448},... | collective-permute-start | bytes 1597448 | tf_op jit(solution)/shard_map/ppermute | solution.py:16
  112.7 14.4 %collective-permute-done.7 = f32[256,520]{0,1:T(8,128)S(1)} collective-permute-done((f32[256,520]{0,1:T(8,128)S(1)}, f32[256,520]{0,1:T(8,128)S(1)}, u32[]{:S(2)}, u32[]{:S(2)}) %collective-permute-start.7) | collective-permute-done | bytes 532512 | tf_op jit(solution)/shard_map/ppermute | solution.py:16
  127.1 0.7 fusion.157
  127.8 0.8 fusion.154
  128.6 1.9 %collective-permute-start.8 = (f32[256,516]{0,1:T(8,128)S(1)}, f32[256,516]{0,1:T(8,128)S(1)}, u32[]{:S(2)}, u32[]{:S(2)}) collective-permute-start(f32[256,516]{0,1:T(8,128)S(1)} %fusion.154), channel_id=1, source_target_pairs={{0,64},{64,128},{128,192},{192,256},{256,320},{320,384},{384,448},... | collective-permute-start | bytes 1585160 | tf_op jit(solution)/shard_map/ppermute | solution.py:16
  130.6 13.6 %collective-permute-done.8 = f32[256,516]{0,1:T(8,128)S(1)} collective-permute-done((f32[256,516]{0,1:T(8,128)S(1)}, f32[256,516]{0,1:T(8,128)S(1)}, u32[]{:S(2)}, u32[]{:S(2)}) %collective-permute-start.8) | collective-permute-done | bytes 528416 | tf_op jit(solution)/shard_map/ppermute | solution.py:16
  144.2 0.7 fusion.150
  144.9 0.7 fusion.182
  145.6 1.0 copy.14
  (5 shorter events, 0.1 us)
Async XLA Ops:
  0.0 2.6 %copy-start = (f32[256,512]{1,0:T(8,128)S(1)}, f32[256,512]{1,0:T(8,128)}, u32[]{:S(2)}) copy-start(f32[256,512]{1,0:T(8,128)} %param.7) | copy-start | bytes 1572868
  0.0 2.8 %copy-start.1 = (f32[1,256,512]{2,1,0:T(8,128)S(1)}, f32[1,256,512]{2,1,0:T(8,128)}, u32[]{:S(2)}) copy-start(f32[1,256,512]{2,1,0:T(8,128)} %param.4) | copy-start | bytes 1572868
  3.0 5.9 %collective-permute-start = (f32[4,256,22]{1,2,0:T(8,128)S(1)}, f32[4,256,22]{1,2,0:T(8,128)S(1)}, u32[]{:S(2)}, u32[]{:S(2)}) collective-permute-start(f32[4,256,22]{1,2,0:T(8,128)S(1)} %get-tuple-element.7), channel_id=1, source_target_pairs={{0,1},{1,2},{2,3},{3,4},{4,5},{5,6},{6,7},{7,8},{8,9},{9,10},{10,1... | collective-permute-start | bytes 270344 | tf_op jit(solution)/shard_map/ppermute | solution.py:16
  5.0 6.4 %collective-permute-start.1 = (f32[4,256,22]{1,2,0:T(8,128)S(1)}, f32[4,256,22]{1,2,0:T(8,128)S(1)}, u32[]{:S(2)}, u32[]{:S(2)}) collective-permute-start(f32[4,256,22]{1,2,0:T(8,128)S(1)} %get-tuple-element.8), channel_id=1, source_target_pairs={{1,0},{2,1},{3,2},{4,3},{5,4},{6,5},{7,6},{8,7},{9,8},{10,9},{11,1... | collective-permute-start | bytes 270344 | tf_op jit(solution)/shard_map/ppermute | solution.py:16
  18.9 15.1 %collective-permute-start.2 = (f32[256,540]{0,1:T(8,128)S(1)}, f32[256,540]{0,1:T(8,128)S(1)}, u32[]{:S(2)}, u32[]{:S(2)}) collective-permute-start(f32[256,540]{0,1:T(8,128)S(1)} %subtract_select_fusion), channel_id=1, source_target_pairs={{0,64},{64,128},{128,192},{192,256},{256,320},{320,384},{384,448},... | collective-permute-start | bytes 1658888 | tf_op jit(solution)/shard_map/ppermute | solution.py:16
  35.7 16.1 %collective-permute-start.3 = (f32[256,536]{0,1:T(8,128)S(1)}, f32[256,536]{0,1:T(8,128)S(1)}, u32[]{:S(2)}, u32[]{:S(2)}) collective-permute-start(f32[256,536]{0,1:T(8,128)S(1)} %fusion.93), channel_id=1, source_target_pairs={{0,64},{64,128},{128,192},{192,256},{256,320},{320,384},{384,448},... | collective-permute-start | bytes 1646600 | tf_op jit(solution)/shard_map/ppermute | solution.py:16
  53.4 17.2 %collective-permute-start.4 = (f32[256,532]{0,1:T(8,128)S(1)}, f32[256,532]{0,1:T(8,128)S(1)}, u32[]{:S(2)}, u32[]{:S(2)}) collective-permute-start(f32[256,532]{0,1:T(8,128)S(1)} %fusion.86), channel_id=1, source_target_pairs={{0,64},{64,128},{128,192},{192,256},{256,320},{320,384},{384,448},... | collective-permute-start | bytes 1634312 | tf_op jit(solution)/shard_map/ppermute | solution.py:16
  72.2 18.2 %collective-permute-start.5 = (f32[256,528]{0,1:T(8,128)S(1)}, f32[256,528]{0,1:T(8,128)S(1)}, u32[]{:S(2)}, u32[]{:S(2)}) collective-permute-start(f32[256,528]{0,1:T(8,128)S(1)} %fusion.127), channel_id=1, source_target_pairs={{0,64},{64,128},{128,192},{192,256},{256,320},{320,384},{384,448},... | collective-permute-start | bytes 1622024 | tf_op jit(solution)/shard_map/ppermute | solution.py:16
  91.8 17.4 %collective-permute-start.6 = (f32[256,524]{0,1:T(8,128)S(1)}, f32[256,524]{0,1:T(8,128)S(1)}, u32[]{:S(2)}, u32[]{:S(2)}) collective-permute-start(f32[256,524]{0,1:T(8,128)S(1)} %fusion.120), channel_id=1, source_target_pairs={{0,64},{64,128},{128,192},{192,256},{256,320},{320,384},{384,448},... | collective-permute-start | bytes 1609736 | tf_op jit(solution)/shard_map/ppermute | solution.py:16
  110.7 16.4 %collective-permute-start.7 = (f32[256,520]{0,1:T(8,128)S(1)}, f32[256,520]{0,1:T(8,128)S(1)}, u32[]{:S(2)}, u32[]{:S(2)}) collective-permute-start(f32[256,520]{0,1:T(8,128)S(1)} %fusion.161), channel_id=1, source_target_pairs={{0,64},{64,128},{128,192},{192,256},{256,320},{320,384},{384,448},... | collective-permute-start | bytes 1597448 | tf_op jit(solution)/shard_map/ppermute | solution.py:16
  128.6 15.5 %collective-permute-start.8 = (f32[256,516]{0,1:T(8,128)S(1)}, f32[256,516]{0,1:T(8,128)S(1)}, u32[]{:S(2)}, u32[]{:S(2)}) collective-permute-start(f32[256,516]{0,1:T(8,128)S(1)} %fusion.154), channel_id=1, source_target_pairs={{0,64},{64,128},{128,192},{192,256},{256,320},{320,384},{384,448},... | collective-permute-start | bytes 1585160 | tf_op jit(solution)/shard_map/ppermute | solution.py:16

commit v2 on v1

--- a/solution.py
+++ b/solution.py
@@ -63,14 +63,21 @@
     field, h = run(state, top, FINE, DT)
     start_c = state[:, top - chain - CSTEPS: top + n + chain + CSTEPS]
     old_coarse, _ = run(start_c, chain + CSTEPS, CSTEPS, DT * FINE / CSTEPS)
-    first = lax.axis_index("tm") == 0
-    carried = jnp.where(first, field, field - old_coarse)
-    current = carried
+    me = lax.axis_index("tm")
+    carried = jnp.where(me == 0, field, field - old_coarse)
+    every = lax.all_gather(carried, "tm")
+
+    def part(j, h):
+        pos = j + me - (slices - 1)
+        got = lax.dynamic_index_in_dim(every, jnp.maximum(pos, 0), 0, keepdims=False)
+        got = got[:, chain - h: chain + n + h]
+        return jnp.where(pos >= 0, got, jnp.zeros_like(got))
+
     h = chain
-    for turn in range(slices - 1):
-        incoming = shifted(current, "tm", 1)
-        moved, h = run(incoming, h, CSTEPS, DT * FINE / CSTEPS)
-        current = carried[:, chain - h: chain + n + h] + moved
+    current = part(0, h)
+    for turn in range(1, slices):
+        moved, h = run(current, h, CSTEPS, DT * FINE / CSTEPS)
+        current = part(turn, h) + moved
     return current[None]
 
 

time: 147 us -> 141 us (0.959)
  the two profiles are of different devices: /device:TPU:228 before, /device:TPU:1 now
where the time goes in v2:
time: 141 us
  waiting for transfers between devices  75.6 us (54%)
  other arithmetic  40.2 us (29%)
  between operations  13.7 us (10%)
  starting transfers between devices  10.1 us (7%)
    all_gather x1, waiting for transfers between devices, local(): every = lax.all_gather(carried, 'tm')  70.5 us
    add x14, other arithmetic, advance(): return mid - size * moved + size * coef[2] * spread  18.8 us
    ppermute x2, starting transfers between devices, shifted(): return lax.ppermute(block, axis, route)  10.1 us
    add x6, other arithmetic, local(): current = part(turn, h) + moved  8.99 us
    ppermute x2, waiting for transfers between devices, shifted(): return lax.ppermute(block, axis, route)  5.11 us
    select_n x1, other arithmetic, part(): return jnp.where(pos >= 0, got, jnp.zeros_like(got))  3.57 us
    select_n x1, other arithmetic, local(): carried = jnp.where(me == 0, field, field - old_coarse)  3.15 us
  transfers between devices with their start and end apart: 3, of which 3 were waited for; matrix products, arithmetic and copies ran while one was open for 0% of the time, Pallas kernels for 0%

profile of v2, /device:TPU:1, one launch (start us, length us, event | category | flops | bytes accessed | tf_op | source)
XLA Modules:
  0.0 140.6 jit_solution(2261006181540351606)
XLA Ops:
  6.5 0.0 copy-start
  6.5 0.0 all-gather.3.cloned.1.call-start
  6.5 1.5 %pad_maximum_fusion.4 = (f32[4,256,22]{2,1,0:T(8,128)S(1)}, f32[4,256,22]{2,1,0:T(8,128)S(1)}) fusion(f32[1,256,512]{2,1,0:T(8,128)} %bitcast.761, f32[1,256,512]{2,1,0:T(8,128)} %bitcast.763, f32[1,256,512]{2,1,0:T(8,128)} %bitcast.765, f32[1,256,512]{2,1,0:T(8,128)} %param.4), kind=kLoop, calls=%fused_computation.326 | loop fusion | flops 135168 | bytes 2277376 | tf_op jit(solution)/shard_map/slice | solution.py:21
  8.1 5.4 %collective-permute-start = (f32[4,256,22]{2,1,0:T(8,128)S(1)}, f32[4,256,22]{2,1,0:T(8,128)S(1)}, u32[]{:S(2)}, u32[]{:S(2)}) collective-permute-start(f32[4,256,22]{2,1,0:T(8,128)S(1)} %get-tuple-element.15), channel_id=1, source_target_pairs={{0,1},{1,2},{2,3},{3,4},{4,5},{5,6},{6,7},{7,8},{8,9},{9,10},{10,1... | collective-permute-start | bytes 270344 | tf_op jit(solution)/shard_map/ppermute | solution.py:16
  13.5 4.7 %collective-permute-start.1 = (f32[4,256,22]{2,1,0:T(8,128)S(1)}, f32[4,256,22]{2,1,0:T(8,128)}, u32[]{:S(2)}, u32[]{:S(2)}) collective-permute-start(f32[4,256,22]{2,1,0:T(8,128)S(1)} %get-tuple-element.16), channel_id=1, source_target_pairs={{1,0},{2,1},{3,2},{4,3},{5,4},{6,5},{7,6},{8,7},{9,8},{10,9},{11,1... | collective-permute-start | bytes 270344 | tf_op jit(solution)/shard_map/ppermute | solution.py:16
  18.2 1.4 collective-permute-done
  19.6 0.0 copy-start.3
  19.6 0.8 copy-done.3
  20.4 3.7 %collective-permute-done.1 = f32[4,256,22]{2,1,0:T(8,128)} collective-permute-done((f32[4,256,22]{2,1,0:T(8,128)S(1)}, f32[4,256,22]{2,1,0:T(8,128)}, u32[]{:S(2)}, u32[]{:S(2)}) %collective-permute-start.1) | collective-permute-done | bytes 90144 | tf_op jit(solution)/shard_map/ppermute | solution.py:16
  24.1 0.0 copy-done
  24.1 2.5 %pad_maximum_fusion = f32[4,256,556]{2,1,0:T(8,128)S(1)} fusion(f32[4,256,22]{2,1,0:T(8,128)} %collective-permute-done.1, f32[1,256,512]{2,1,0:T(8,128)S(1)} %bitcast.762, f32[1,256,512]{2,1,0:T(8,128)} %bitcast.764, f32[1,256,512]{2,1,0:T(8,128)} %bitcast.766, f32[1,256,512]{2,1,0:T(8,128)} %param.4, f32[4,256,22]{2,1,0:T(8,128)} %copy-done.3), kind=kLoop, calls=%fused_computation | loop fusion | flops 2846720 | bytes 4554752 | tf_op jit(solution)/shard_map/concatenate | solution.py:24
  26.7 0.2 slice.1076
  26.9 1.3 fusion.62
  28.2 1.3 fusion.59
  29.5 1.3 fusion.56
  30.8 1.3 fusion.53
  32.0 1.3 fusion.50
  33.3 1.3 fusion.47
  34.6 2.3 %fusion.141 = (f32[256,542]{1,0:T(8,128)S(1)}, f32[256,542]{1,0:T(8,128)S(1)}) fusion(f32[256,544]{1,0:T(8,128)S(1)} %fusion.47, f32[4,256,556]{2,1,0:T(8,128)S(1)} %pad_maximum_fusion, f32[256,544]{1,0:T(8,128)S(1)} %slice.1076, f32[256,556]{1,0:T(8,128)S(1)} %slice_bitcast_fusion), kind=kLoop, calls=%fused_computation.233 | loop fusion | flops 6382592 | bytes 8318976 | tf_op jit(solution)/shard_map/add | solution.py:41
  36.9 3.2 %subtract_select_fusion = f32[256,540]{1,0:T(8,128)} fusion(f32[256,542]{1,0:T(8,128)S(1)} %get-tuple-element.14, f32[4,256,556]{2,1,0:T(8,128)S(1)} %pad_maximum_fusion, f32[256,542]{1,0:T(8,128)S(1)} %get-tuple-element.13, pred[]{:T(512)S(6)} %eq.3), kind=kLoop, calls=%fused_computation.1 | loop fusion | flops 6635520 | bytes 7761921 | tf_op jit(solution)/shard_map/jit(_where)/select_n | solution.py:67
  40.1 0.0 all-gather.3.cloned.1.call-update
  40.1 70.5 %all-gather.3.cloned.1.call-done = f32[2048,540]{1,0:T(8,128)} async-done(((f32[256,540]{1,0:T(8,128)}), f32[2048,540]{1,0:T(8,128)}) %all-gather.3.cloned.1.call-update) | async-done | bytes 4423696 | tf_op jit(solution)/shard_map/all_gather | solution.py:68
  110.6 3.6 %select_bitcast_fusion = (f32[256,540]{1,0:T(8,128)S(1)}, f32[256,540]{1,0:T(8,128)S(1)}, f32[256,540]{1,0:T(8,128)S(1)}, f32[256,540]{1,0:T(8,128)S(1)}, f32[25...) fusion(f32[8,256,540]{2,1,0:T(8,128)} %bitcast.760, ...), kind=kLoop, calls=%fused_computation.306 | loop fusion | flops 138240 | bytes 8847393 | tf_op jit(solution)/shard_map/jit(_where)/select_n | solution.py:74
  114.2 1.3 fusion.44
  115.4 1.5 %fusion.41 = f32[256,536]{1,0:T(8,128)S(1)} fusion(f32[4,256,556]{2,1,0:T(8,128)S(1)} %pad_maximum_fusion, f32[256,540]{1,0:T(8,128)S(1)} %get-tuple-element.6, f32[256,538]{1,0:T(8,128)S(1)} %fusion.44, pred[]{:T(512)S(6)} %ge.30), kind=kLoop, calls=%fused_computation.55 | loop fusion | flops 3704832 | bytes 5791745 | tf_op jit(solution)/shard_map/add | solution.py:80
  116.9 1.3 fusion.37
  118.2 1.5 %fusion.34 = f32[256,532]{1,0:T(8,128)S(1)} fusion(f32[4,256,556]{2,1,0:T(8,128)S(1)} %pad_maximum_fusion, f32[256,540]{1,0:T(8,128)S(1)} %get-tuple-element.7, f32[256,534]{1,0:T(8,128)S(1)} %fusion.37, pred[]{:T(512)S(6)} %ge.29), kind=kLoop, calls=%fused_computation.46 | loop fusion | flops 3677184 | bytes 5787649 | tf_op jit(solution)/shard_map/add | solution.py:80
  119.7 1.3 fusion.30
  120.9 1.5 %fusion.27 = f32[256,528]{1,0:T(8,128)S(1)} fusion(f32[4,256,556]{2,1,0:T(8,128)S(1)} %pad_maximum_fusion, f32[256,540]{1,0:T(8,128)S(1)} %get-tuple-element.8, f32[256,530]{1,0:T(8,128)S(1)} %fusion.30, pred[]{:T(512)S(6)} %ge.28), kind=kLoop, calls=%fused_computation.37 | loop fusion | flops 3649536 | bytes 5783553 | tf_op jit(solution)/shard_map/add | solution.py:80
  122.4 1.3 fusion.23
  123.7 1.7 %fusion.20 = f32[256,524]{1,0:T(8,128)S(1)} fusion(f32[4,256,556]{2,1,0:T(8,128)S(1)} %pad_maximum_fusion, f32[256,540]{1,0:T(8,128)S(1)} %get-tuple-element.9, f32[256,526]{1,0:T(8,128)S(1)} %fusion.23, pred[]{:T(512)S(6)} %ge.27), kind=kLoop, calls=%fused_computation.28 | loop fusion | flops 3621888 | bytes 5779457 | tf_op jit(solution)/shard_map/add | solution.py:80
  125.4 1.3 fusion.16
  126.6 1.5 %fusion.13 = f32[256,520]{1,0:T(8,128)S(1)} fusion(f32[4,256,556]{2,1,0:T(8,128)S(1)} %pad_maximum_fusion, f32[256,540]{1,0:T(8,128)S(1)} %get-tuple-element.10, f32[256,522]{1,0:T(8,128)S(1)} %fusion.16, pred[]{:T(512)S(6)} %ge.26), kind=kLoop, calls=%fused_computation.19 | loop fusion | flops 3594240 | bytes 5775361 | tf_op jit(solution)/shard_map/add | solution.py:80
  128.1 1.3 fusion.9
  129.4 1.5 %fusion.6 = f32[256,516]{1,0:T(8,128)S(1)} fusion(f32[4,256,556]{2,1,0:T(8,128)S(1)} %pad_maximum_fusion, f32[256,540]{1,0:T(8,128)S(1)} %get-tuple-element.11, f32[256,518]{1,0:T(8,128)S(1)} %fusion.9, pred[]{:T(512)S(6)} %ge.25), kind=kLoop, calls=%fused_computation.10 | loop fusion | flops 3566592 | bytes 5771265 | tf_op jit(solution)/shard_map/add | solution.py:80
  130.8 0.0 copy-start.1
  130.9 0.0 copy-start.2
  130.9 1.3 fusion.2
  132.1 0.0 copy-done.1
  132.2 0.0 copy-done.2
  132.2 1.6 %fusion.183 = f32[1,256,512]{2,1,0:T(8,128)} fusion(f32[256,540]{1,0:T(8,128)S(1)} %get-tuple-element.12, f32[256,512]{1,0:T(8,128)S(1)} %copy-done, f32[256,514]{1,0:T(8,128)S(1)} %fusion.2, f32[256,512]{1,0:T(8,128)S(1)} %copy-done.1, f32[256,512]{1,0:T(8,128)S(1)} %copy-done.2, pred[]{:T(512)S(6)} %ge.24), kind=kLoop, calls=%fused_computation.322 | loop fusion | flops 3538944 | bytes 4849665 | tf_op jit(solution)/shard_map/broadcast_in_dim | solution.py:81
  (1 shorter events, 0.0 us)
Async XLA Ops:
  6.5 17.5 %copy-start = (f32[256,512]{1,0:T(8,128)S(1)}, f32[256,512]{1,0:T(8,128)}, u32[]{:S(2)}) copy-start(f32[256,512]{1,0:T(8,128)} %param.7) | copy-start | bytes 1572868
  6.5 104.0 %all-gather.3.cloned.1.call-start = ((), (), s32[]{:S(2)}) async-start(), calls=%async_computation | async-start | bytes 5898240 | tf_op jit(solution)/shard_map/all_gather | solution.py:68
  8.1 11.5 %collective-permute-start = (f32[4,256,22]{2,1,0:T(8,128)S(1)}, f32[4,256,22]{2,1,0:T(8,128)S(1)}, u32[]{:S(2)}, u32[]{:S(2)}) collective-permute-start(f32[4,256,22]{2,1,0:T(8,128)S(1)} %get-tuple-element.15), channel_id=1, source_target_pairs={{0,1},{1,2},{2,3},{3,4},{4,5},{5,6},{6,7},{7,8},{8,9},{9,10},{10,1... | collective-permute-start | bytes 270344 | tf_op jit(solution)/shard_map/ppermute | solution.py:16
  13.5 10.6 %collective-permute-start.1 = (f32[4,256,22]{2,1,0:T(8,128)S(1)}, f32[4,256,22]{2,1,0:T(8,128)}, u32[]{:S(2)}, u32[]{:S(2)}) collective-permute-start(f32[4,256,22]{2,1,0:T(8,128)S(1)} %get-tuple-element.16), channel_id=1, source_target_pairs={{1,0},{2,1},{3,2},{4,3},{5,4},{6,5},{7,6},{8,7},{9,8},{10,9},{11,1... | collective-permute-start | bytes 270344 | tf_op jit(solution)/shard_map/ppermute | solution.py:16
  19.6 0.8 copy-start.3
  130.8 1.3 copy-start.1
  130.9 1.3 copy-start.2
Sparse Core Ops, SparseCore 0:
  40.2 70.3 all-gather.2

commit v3 on v2

--- a/solution.py
+++ b/solution.py
@@ -65,13 +65,29 @@
     old_coarse, _ = run(start_c, chain + CSTEPS, CSTEPS, DT * FINE / CSTEPS)
     me = lax.axis_index("tm")
     carried = jnp.where(me == 0, field, field - old_coarse)
-    every = lax.all_gather(carried, "tm")
+    ring = [(i, (i + 1) % slices) for i in range(slices)]
+    back = [((i + 1) % slices, i) for i in range(slices)]
+    ahead = slices // 2
+    behind = slices - 1 - ahead
+    got = {slices - 1: carried}
+    block = carried
+    for r in range(1, ahead + 1):
+        keep = chain - CSTEPS * (r - 1)
+        block = lax.ppermute(block[:, chain - keep: chain + n + keep] if r == 1 else block, "tm", back)
+        got[r - 1] = block
+        if r < ahead:
+            block = block[:, CSTEPS: block.shape[-1] - CSTEPS]
+    wide_f = CSTEPS * behind
+    block = carried[:, chain - wide_f: chain + n + wide_f]
+    for r in range(1, behind + 1):
+        block = lax.ppermute(block, "tm", ring)
+        got[slices - 1 - r] = block
 
     def part(j, h):
-        pos = j + me - (slices - 1)
-        got = lax.dynamic_index_in_dim(every, jnp.maximum(pos, 0), 0, keepdims=False)
-        got = got[:, chain - h: chain + n + h]
-        return jnp.where(pos >= 0, got, jnp.zeros_like(got))
+        blk = got[j]
+        extra = (blk.shape[-1] - n) // 2 - h
+        blk = blk[:, extra: extra + n + 2 * h]
+        return jnp.where(me >= slices - 1 - j, blk, jnp.zeros_like(blk))
 
     h = chain
     current = part(0, h)

time: 141 us -> 109 us (0.77)
  the two profiles are of different devices: /device:TPU:1 before, /device:TPU:504 now
where the time goes in v3:
time: 109 us; the launch traced here: 108 us
  waiting for transfers between devices  47.9 us (44%)
  starting transfers between devices  29.3 us (27%)
  other arithmetic  23.5 us (22%)
  local copies, waits for them, and re-layouts  7.34 us (7%)
    ppermute x4, waiting for transfers between devices, local(): lax.ppermute(block[:, chain - keep:chain + n + keep] if r == 1 else block...  35 us
    ppermute x3, starting transfers between devices, local(): block = lax.ppermute(block, 'tm', ring)  14.4 us
    add x14, other arithmetic, advance(): return mid - size * moved + size * coef[2] * spread  11.2 us
    ppermute x3, waiting for transfers between devices, local(): block = lax.ppermute(block, 'tm', ring)  10.7 us
    ppermute x4, starting transfers between devices, local(): lax.ppermute(block[:, chain - keep:chain + n + keep] if r == 1 else block...  9.31 us
    add x6, other arithmetic, local(): current = part(turn, h) + moved  7.83 us
    ppermute x2, starting transfers between devices, shifted(): return lax.ppermute(block, axis, route)  5.56 us
    unnamed x20, local copies, waits for them, and re-layouts  4.26 us
  transfers between devices with their start and end apart: 9, of which 6 were waited for; matrix products, arithmetic and copies ran while one was open for 9% of the time, Pallas kernels for 0%

profile of v3, /device:TPU:504, one launch (start us, length us, event | category | flops | bytes accessed | tf_op | source)
XLA Modules:
  0.0 108.4 jit_solution(17527954391573289283)
XLA Ops:
  0.0 1.3 %copy.5 = f32[256,512]{0,1:T(8,128)S(1)} copy(f32[256,512]{1,0:T(8,128)} %param.5) | data formatting | bytes 1048576 | tf_op args[1]
  1.3 1.2 %copy.6 = f32[256,512]{0,1:T(8,128)S(1)} copy(f32[256,512]{1,0:T(8,128)} %param.6) | data formatting | bytes 1048576 | tf_op args[2]
  2.6 0.2 copy.7
  2.8 0.2 copy.8
  3.1 1.9 %collective-permute-start = (f32[4,256,22]{1,2,0:T(8,128)S(1)}, f32[4,256,22]{1,2,0:T(8,128)S(1)}, u32[]{:S(2)}, u32[]{:S(2)}) collective-permute-start(f32[4,256,22]{1,2,0:T(8,128)S(1)} %get-tuple-element.7), channel_id=1, source_target_pairs={{0,1},{1,2},{2,3},{3,4},{4,5},{5,6},{6,7},{7,8},{8,9},{9,10},{10,1... | collective-permute-start | bytes 270344 | tf_op jit(solution)/shard_map/ppermute | solution.py:16
  5.0 3.6 %collective-permute-start.1 = (f32[4,256,22]{1,2,0:T(8,128)S(1)}, f32[4,256,22]{1,2,0:T(8,128)S(1)}, u32[]{:S(2)}, u32[]{:S(2)}) collective-permute-start(f32[4,256,22]{1,2,0:T(8,128)S(1)} %get-tuple-element.8), channel_id=1, source_target_pairs={{1,0},{2,1},{3,2},{4,3},{5,4},{6,5},{7,6},{8,7},{9,8},{10,9},{11,1... | collective-permute-start | bytes 270344 | tf_op jit(solution)/shard_map/ppermute | solution.py:16
  8.6 0.3 collective-permute-done
  9.0 1.8 %collective-permute-done.1 = f32[4,256,22]{1,2,0:T(8,128)S(1)} collective-permute-done((f32[4,256,22]{1,2,0:T(8,128)S(1)}, f32[4,256,22]{1,2,0:T(8,128)S(1)}, u32[]{:S(2)}, u32[]{:S(2)}) %collective-permute-start.1) | collective-permute-done | bytes 90144 | tf_op jit(solution)/shard_map/ppermute | solution.py:16
  10.8 1.4 %pad_maximum_fusion = f32[4,256,556]{1,2,0:T(8,128)S(1)} fusion(f32[4,256,22]{1,2,0:T(8,128)S(1)} %collective-permute-done.1, f32[1,256,512]{1,2,0:T(8,128)} %bitcast.748, f32[1,256,512]{1,2,0:T(8,128)S(1)} %bitcast.746, f32[1,256,512]{1,2,0:T(8,128)S(1)} %bitcast.744, f32[1,256,512]{1,2,0:T(8,128)} %copy-done.4, f32[4,256,22]{1,2,0:T(8,128)S(1)} %collective-permute-done), kind=kLoop, calls=%fused_computation | loop fusion | flops 2846720 | bytes 4554752 | tf_op jit(solution)/shard_map/concatenate | solution.py:24
  12.3 0.8 fusion.2
  13.1 0.8 fusion.19
  13.9 0.8 fusion.16
  14.7 0.8 fusion.13
  15.5 0.8 fusion.10
  16.2 0.8 fusion.45
  17.0 1.3 %fusion.64 = (f32[256,542]{0,1:T(8,128)S(1)}, f32[256,542]{0,1:T(8,128)S(1)}) fusion(f32[256,544]{0,1:T(8,128)S(1)} %fusion.45, f32[4,256,556]{1,2,0:T(8,128)S(1)} %pad_maximum_fusion, f32[256,544]{0,1:T(8,128)S(1)} %slice.1076, f32[256,556]{0,1:T(8,128)S(1)} %slice_bitcast_fusion), kind=kLoop, calls=%fused_computation.158 | loop fusion | flops 6382592 | bytes 7237632 | tf_op jit(solution)/shard_map/add | solution.py:41
  18.3 1.3 %subtract_select_fusion = f32[256,540]{0,1:T(8,128)S(1)} fusion(f32[256,542]{0,1:T(8,128)S(1)} %get-tuple-element.6, f32[4,256,556]{1,2,0:T(8,128)S(1)} %pad_maximum_fusion, f32[256,542]{0,1:T(8,128)S(1)} %get-tuple-element.5, pred[]{:T(512)S(6)} %eq.3), kind=kLoop, calls=%fused_computation.49 | loop fusion | flops 6635520 | bytes 6680577 | tf_op jit(solution)/shard_map/jit(_where)/select_n | solution.py:67
  19.6 3.3 %collective-permute-start.5 = (f32[256,540]{0,1:T(8,128)S(1)}, f32[256,540]{0,1:T(8,128)S(1)}, u32[]{:S(2)}, u32[]{:S(2)}) collective-permute-start(f32[256,540]{0,1:T(8,128)S(1)} %subtract_select_fusion), channel_id=1, source_target_pairs={{64,0},{128,64},{192,128},{256,192},{320,256},{384,320},{448,384},... | collective-permute-start | bytes 1658888 | tf_op jit(solution)/shard_map/ppermute | solution.py:76
  23.0 3.8 %collective-permute-start.2 = (f32[256,524]{0,1:T(8,128)S(1)}, f32[256,524]{0,1:T(8,128)}, u32[]{:S(2)}, u32[]{:S(2)}) collective-permute-start(f32[256,524]{0,1:T(8,128)S(1)} %slice.1081), channel_id=1, source_target_pairs={{0,64},{64,128},{128,192},{192,256},{256,320},{320,384},{384,448},... | collective-permute-start | bytes 1609736 | tf_op jit(solution)/shard_map/ppermute | solution.py:83
  26.8 10.4 %collective-permute-done.5 = f32[256,540]{0,1:T(8,128)S(1)} collective-permute-done((f32[256,540]{0,1:T(8,128)S(1)}, f32[256,540]{0,1:T(8,128)S(1)}, u32[]{:S(2)}, u32[]{:S(2)}) %collective-permute-start.5) | collective-permute-done | bytes 552992 | tf_op jit(solution)/shard_map/ppermute | solution.py:76
  37.2 0.8 copy-done.5
  38.0 0.8 slice.1084
  38.8 2.0 %collective-permute-start.6 = (f32[256,536]{0,1:T(8,128)}, f32[256,536]{0,1:T(8,128)}, u32[]{:S(2)}, u32[]{:S(2)}) collective-permute-start(f32[256,536]{0,1:T(8,128)} %slice.1084), channel_id=1, source_target_pairs={{64,0},{128,64},{192,128},{256,192},{320,256},{384,320},{448,384},... | collective-permute-start | bytes 1646600 | tf_op jit(solution)/shard_map/ppermute | solution.py:76
  40.9 5.0 %collective-permute-start.3 = (f32[256,524]{0,1:T(8,128)}, f32[256,524]{0,1:T(8,128)}, u32[]{:S(2)}, u32[]{:S(2)}) collective-permute-start(f32[256,524]{0,1:T(8,128)} %collective-permute-done.2), channel_id=1, source_target_pairs={{0,64},{64,128},{128,192},{192,256},{256,320},{320,384},{384,448},... | collective-permute-start | bytes 1609736 | tf_op jit(solution)/shard_map/ppermute | solution.py:83
  45.9 1.1 %broadcast_select_fusion = f32[256,540]{0,1:T(8,128)S(1)} fusion(f32[256,540]{0,1:T(8,128)} %copy-done.5, pred[]{:T(512)S(6)} %ge.31), kind=kLoop, calls=%fused_computation.357 | loop fusion | flops 138240 | bytes 1105921 | tf_op jit(solution)/shard_map/jit(_where)/select_n | solution.py:90
  47.0 0.8 fusion.42
  47.8 10.7 %collective-permute-done.3 = f32[256,524]{0,1:T(8,128)} collective-permute-done((f32[256,524]{0,1:T(8,128)}, f32[256,524]{0,1:T(8,128)}, u32[]{:S(2)}, u32[]{:S(2)}) %collective-permute-start.3) | collective-permute-done | bytes 536608 | tf_op jit(solution)/shard_map/ppermute | solution.py:83
  58.5 5.6 %collective-permute-start.4 = (f32[256,524]{0,1:T(8,128)}, f32[256,524]{0,1:T(8,128)S(1)}, u32[]{:S(2)}, u32[]{:S(2)}) collective-permute-start(f32[256,524]{0,1:T(8,128)} %collective-permute-done.3), channel_id=1, source_target_pairs={{0,64},{64,128},{128,192},{192,256},{256,320},{320,384},{384,448},... | collective-permute-start | bytes 1609736 | tf_op jit(solution)/shard_map/ppermute | solution.py:83
  64.1 1.1 %slice.1085 = f32[256,532]{0,1:T(8,128)S(1)} slice(f32[256,536]{0,1:T(8,128)} %collective-permute-done.6), slice={[0:256], [2:534]} | slice | bytes 1089536 | tf_op jit(solution)/shard_map/slice | solution.py:79
  65.2 2.1 %collective-permute-start.7 = (f32[256,532]{0,1:T(8,128)S(1)}, f32[256,532]{0,1:T(8,128)S(1)}, u32[]{:S(2)}, u32[]{:S(2)}) collective-permute-start(f32[256,532]{0,1:T(8,128)S(1)} %slice.1085), channel_id=1, source_target_pairs={{64,0},{128,64},{192,128},{256,192},{320,256},{384,320},{448,384},... | collective-permute-start | bytes 1634312 | tf_op jit(solution)/shard_map/ppermute | solution.py:76
  67.3 1.9 %fusion.93 = f32[256,536]{0,1:T(8,128)S(1)} fusion(f32[4,256,556]{1,2,0:T(8,128)S(1)} %pad_maximum_fusion, f32[256,538]{0,1:T(8,128)S(1)} %fusion.42, f32[256,536]{0,1:T(8,128)} %collective-permute-done.6, pred[]{:T(512)S(6)} %ge.30), kind=kLoop, calls=%fused_computation.203 | loop fusion | flops 3704832 | bytes 4947969 | tf_op jit(solution)/shard_map/add | solution.py:96
  69.2 0.8 fusion.89
  69.9 12.2 %collective-permute-done.7 = f32[256,532]{0,1:T(8,128)S(1)} collective-permute-done((f32[256,532]{0,1:T(8,128)S(1)}, f32[256,532]{0,1:T(8,128)S(1)}, u32[]{:S(2)}, u32[]{:S(2)}) %collective-permute-start.7) | collective-permute-done | bytes 544800 | tf_op jit(solution)/shard_map/ppermute | solution.py:76
  82.2 1.9 %collective-permute-start.8 = (f32[256,528]{0,1:T(8,128)S(1)}, f32[256,528]{0,1:T(8,128)S(1)}, u32[]{:S(2)}, u32[]{:S(2)}) collective-permute-start(f32[256,528]{0,1:T(8,128)S(1)} %slice.1086), channel_id=1, source_target_pairs={{64,0},{128,64},{192,128},{256,192},{320,256},{384,320},{448,384},... | collective-permute-start | bytes 1622024 | tf_op jit(solution)/shard_map/ppermute | solution.py:76
  84.1 0.8 fusion.86
  84.9 0.7 fusion.82
  85.7 12.4 %collective-permute-done.8 = f32[256,528]{0,1:T(8,128)S(1)} collective-permute-done((f32[256,528]{0,1:T(8,128)S(1)}, f32[256,528]{0,1:T(8,128)S(1)}, u32[]{:S(2)}, u32[]{:S(2)}) %collective-permute-start.8) | collective-permute-done | bytes 540704 | tf_op jit(solution)/shard_map/ppermute | solution.py:76
  98.1 0.8 fusion.127
  98.9 0.7 fusion.123
  99.6 0.7 fusion.120
  100.3 0.7 fusion.116
  101.1 1.8 %fusion.161 = f32[256,520]{0,1:T(8,128)S(1)} fusion(f32[4,256,556]{1,2,0:T(8,128)S(1)} %pad_maximum_fusion, f32[256,524]{0,1:T(8,128)} %collective-permute-done.3, f32[256,522]{0,1:T(8,128)S(1)} %fusion.116, pred[]{:T(512)S(6)} %ge.26), kind=kLoop, calls=%fused_computation.311 | loop fusion | flops 3594240 | bytes 4800513 | tf_op jit(solution)/shard_map/add | solution.py:96
  102.9 0.7 fusion.157
  103.6 1.8 %fusion.154 = f32[256,516]{0,1:T(8,128)S(1)} fusion(f32[4,256,556]{1,2,0:T(8,128)S(1)} %pad_maximum_fusion, f32[256,524]{0,1:T(8,128)} %collective-permute-done.2, f32[256,518]{0,1:T(8,128)S(1)} %fusion.157, pred[]{:T(512)S(6)} %ge.25), kind=kLoop, calls=%fused_computation.302 | loop fusion | flops 3566592 | bytes 4784129 | tf_op jit(solution)/shard_map/add | solution.py:96
  105.5 0.7 fusion.150
  106.2 0.3 copy-done.1
  106.7 0.7 fusion.183
  107.4 1.0 copy.14
  (22 shorter events, 0.4 us)
Async XLA Ops:
  0.0 2.6 %copy-start.6 = (f32[256,512]{1,0:T(8,128)S(1)}, f32[256,512]{1,0:T(8,128)}, u32[]{:S(2)}) copy-start(f32[256,512]{1,0:T(8,128)} %param.7) | copy-start | bytes 1572868
  0.0 2.8 %copy-start.7 = (f32[1,256,512]{2,1,0:T(8,128)S(1)}, f32[1,256,512]{2,1,0:T(8,128)}, u32[]{:S(2)}) copy-start(f32[1,256,512]{2,1,0:T(8,128)} %param.4) | copy-start | bytes 1572868
  2.8 6.2 %copy-start = (f32[256,512]{0,1:T(8,128)}, f32[256,512]{0,1:T(8,128)S(1)}, u32[]{:S(2)}) copy-start(f32[256,512]{0,1:T(8,128)S(1)} %copy.7) | copy-start | bytes 1572868
  3.0 6.0 %copy-start.4 = (f32[1,256,512]{1,2,0:T(8,128)}, f32[1,256,512]{1,2,0:T(8,128)S(1)}, u32[]{:S(2)}) copy-start(f32[1,256,512]{1,2,0:T(8,128)S(1)} %copy.8) | copy-start | bytes 1572868
  3.1 5.9 %collective-permute-start = (f32[4,256,22]{1,2,0:T(8,128)S(1)}, f32[4,256,22]{1,2,0:T(8,128)S(1)}, u32[]{:S(2)}, u32[]{:S(2)}) collective-permute-start(f32[4,256,22]{1,2,0:T(8,128)S(1)} %get-tuple-element.7), channel_id=1, source_target_pairs={{0,1},{1,2},{2,3},{3,4},{4,5},{5,6},{6,7},{7,8},{8,9},{9,10},{10,1... | collective-permute-start | bytes 270344 | tf_op jit(solution)/shard_map/ppermute | solution.py:16
  5.0 5.8 %collective-permute-start.1 = (f32[4,256,22]{1,2,0:T(8,128)S(1)}, f32[4,256,22]{1,2,0:T(8,128)S(1)}, u32[]{:S(2)}, u32[]{:S(2)}) collective-permute-start(f32[4,256,22]{1,2,0:T(8,128)S(1)} %get-tuple-element.8), channel_id=1, source_target_pairs={{1,0},{2,1},{3,2},{4,3},{5,4},{6,5},{7,6},{8,7},{9,8},{10,9},{11,1... | collective-permute-start | bytes 270344 | tf_op jit(solution)/shard_map/ppermute | solution.py:16
  19.6 3.3 %copy-start.2 = (f32[256,540]{0,1:T(8,128)}, f32[256,540]{0,1:T(8,128)S(1)}, u32[]{:S(2)}) copy-start(f32[256,540]{0,1:T(8,128)S(1)} %subtract_select_fusion) | copy-start | bytes 1658884
  19.6 17.5 %collective-permute-start.5 = (f32[256,540]{0,1:T(8,128)S(1)}, f32[256,540]{0,1:T(8,128)S(1)}, u32[]{:S(2)}, u32[]{:S(2)}) collective-permute-start(f32[256,540]{0,1:T(8,128)S(1)} %subtract_select_fusion), channel_id=1, source_target_pairs={{64,0},{128,64},{192,128},{256,192},{320,256},{384,320},{448,384},... | collective-permute-start | bytes 1658888 | tf_op jit(solution)/shard_map/ppermute | solution.py:76
  23.0 17.9 %collective-permute-start.2 = (f32[256,524]{0,1:T(8,128)S(1)}, f32[256,524]{0,1:T(8,128)}, u32[]{:S(2)}, u32[]{:S(2)}) collective-permute-start(f32[256,524]{0,1:T(8,128)S(1)} %slice.1081), channel_id=1, source_target_pairs={{0,64},{64,128},{128,192},{192,256},{256,320},{320,384},{384,448},... | collective-permute-start | bytes 1609736 | tf_op jit(solution)/shard_map/ppermute | solution.py:83
  37.2 0.8 copy-start.5
  38.8 25.3 %collective-permute-start.6 = (f32[256,536]{0,1:T(8,128)}, f32[256,536]{0,1:T(8,128)}, u32[]{:S(2)}, u32[]{:S(2)}) collective-permute-start(f32[256,536]{0,1:T(8,128)} %slice.1084), channel_id=1, source_target_pairs={{64,0},{128,64},{192,128},{256,192},{320,256},{384,320},{448,384},... | collective-permute-start | bytes 1646600 | tf_op jit(solution)/shard_map/ppermute | solution.py:76
  40.9 17.6 %collective-permute-start.3 = (f32[256,524]{0,1:T(8,128)}, f32[256,524]{0,1:T(8,128)}, u32[]{:S(2)}, u32[]{:S(2)}) collective-permute-start(f32[256,524]{0,1:T(8,128)} %collective-permute-done.2), channel_id=1, source_target_pairs={{0,64},{64,128},{128,192},{192,256},{256,320},{320,384},{384,448},... | collective-permute-start | bytes 1609736 | tf_op jit(solution)/shard_map/ppermute | solution.py:83
  58.5 41.1 %collective-permute-start.4 = (f32[256,524]{0,1:T(8,128)}, f32[256,524]{0,1:T(8,128)S(1)}, u32[]{:S(2)}, u32[]{:S(2)}) collective-permute-start(f32[256,524]{0,1:T(8,128)} %collective-permute-done.3), channel_id=1, source_target_pairs={{0,64},{64,128},{128,192},{192,256},{256,320},{320,384},{384,448},... | collective-permute-start | bytes 1609736 | tf_op jit(solution)/shard_map/ppermute | solution.py:83
  65.2 16.9 %collective-permute-start.7 = (f32[256,532]{0,1:T(8,128)S(1)}, f32[256,532]{0,1:T(8,128)S(1)}, u32[]{:S(2)}, u32[]{:S(2)}) collective-permute-start(f32[256,532]{0,1:T(8,128)S(1)} %slice.1085), channel_id=1, source_target_pairs={{64,0},{128,64},{192,128},{256,192},{320,256},{384,320},{448,384},... | collective-permute-start | bytes 1634312 | tf_op jit(solution)/shard_map/ppermute | solution.py:76
  82.2 15.9 %collective-permute-start.8 = (f32[256,528]{0,1:T(8,128)S(1)}, f32[256,528]{0,1:T(8,128)S(1)}, u32[]{:S(2)}, u32[]{:S(2)}) collective-permute-start(f32[256,528]{0,1:T(8,128)S(1)} %slice.1086), channel_id=1, source_target_pairs={{64,0},{128,64},{192,128},{256,192},{320,256},{384,320},{448,384},... | collective-permute-start | bytes 1622024 | tf_op jit(solution)/shard_map/ppermute | solution.py:76
  105.5 1.0 copy-start.1
  105.5 1.2 %copy-start.3 = (f32[256,540]{0,1:T(8,128)S(1)}, f32[256,540]{0,1:T(8,128)}, u32[]{:S(2)}) copy-start(f32[256,540]{0,1:T(8,128)} %copy-done.2) | copy-start | bytes 1658884

commit v4 on v3

--- a/solution.py
+++ b/solution.py
@@ -69,19 +69,24 @@
     back = [((i + 1) % slices, i) for i in range(slices)]
     ahead = slices // 2
     behind = slices - 1 - ahead
-    got = {slices - 1: carried}
-    block = carried
+    rows = carried.shape[0]
+    cuts = [(0, rows // 2), (rows // 2, rows)]
+    pieces = {slices - 1: [carried]}
+    wide_f = CSTEPS * behind
+    bwd = [carried[a:b] for a, b in cuts]
+    fwd = [carried[a:b, chain - wide_f: chain + n + wide_f] for a, b in cuts]
     for r in range(1, ahead + 1):
         keep = chain - CSTEPS * (r - 1)
-        block = lax.ppermute(block[:, chain - keep: chain + n + keep] if r == 1 else block, "tm", back)
-        got[r - 1] = block
+        if r == 1:
+            bwd = [blk[:, chain - keep: chain + n + keep] for blk in bwd]
+        bwd = [lax.ppermute(blk, "tm", back) for blk in bwd]
+        pieces[r - 1] = bwd
         if r < ahead:
-            block = block[:, CSTEPS: block.shape[-1] - CSTEPS]
-    wide_f = CSTEPS * behind
-    block = carried[:, chain - wide_f: chain + n + wide_f]
-    for r in range(1, behind + 1):
-        block = lax.ppermute(block, "tm", ring)
-        got[slices - 1 - r] = block
+            bwd = [blk[:, CSTEPS: blk.shape[-1] - CSTEPS] for blk in bwd]
+        if r <= behind:
+            fwd = [lax.ppermute(blk, "tm", ring) for blk in fwd]
+            pieces[slices - 1 - r] = fwd
+    got = {j: (p[0] if len(p) == 1 else jnp.concatenate(p, axis=0)) for j, p in pieces.items()}
 
     def part(j, h):
         blk = got[j]

time: 109 us -> 131 us (1.20)
  starting transfers between devices: 29.3 us -> 49 us
  other arithmetic: 23.5 us -> 37 us
  waiting for transfers between devices: 47.9 us -> 38.3 us
  local copies, waits for them, and re-layouts: 7.34 us -> 5.91 us
    ppermute x7 -> x14, starting transfers between devices: 23.7 us -> 43.4 us  [the longest x6 25.2 us: local(): fwd = [lax.ppermute(blk, 'tm', ring) for blk in fwd]]
    ppermute x7 -> x14, waiting for transfers between devices: 45.7 us -> 32.4 us  [the longest x8 24.7 us: local(): bwd = [lax.ppermute(blk, 'tm', back) for blk in bwd]]
    add x14, other arithmetic: 11.2 us -> 18.8 us  [advance(): return mid - size * moved + size * coef[2] * spread]
    ppermute x2, waiting for transfers between devices: 2.18 us -> 5.88 us  [shifted(): return lax.ppermute(block, axis, route)]
    unnamed x20 -> x10, local copies, waits for them, and re-layouts: 4.26 us -> 0.85 us
    slice x4 -> x8, local copies, waits for them, and re-layouts: 2.01 us -> 4.78 us  [the longest x6 2.82 us: local(): bwd = [blk[:, CSTEPS:blk.shape[-1] - CSTEPS] for blk in bwd]]
    slice x1, other arithmetic: 0.02 us -> 1.55 us  [with_halo(): tail = cells[..., cells.shape[-1] - width:]]
  transfers between devices with their start and end apart: 9 -> 16, of which waited for: 6 -> 9; matrix products, arithmetic and copies ran while one was open for 9% -> 11% of each run, Pallas kernels for 0% -> 0%
where the time goes in v4:
time: 131 us
  starting transfers between devices  49 us (37%)
  waiting for transfers between devices  38.3 us (29%)
  other arithmetic  37 us (28%)
  local copies, waits for them, and re-layouts  5.91 us (5%)
    ppermute x6, starting transfers between devices, local(): fwd = [lax.ppermute(blk, 'tm', ring) for blk in fwd]  25.2 us
    ppermute x8, waiting for transfers between devices, local(): bwd = [lax.ppermute(blk, 'tm', back) for blk in bwd]  24.7 us
    add x14, other arithmetic, advance(): return mid - size * moved + size * coef[2] * spread  18.8 us
    ppermute x8, starting transfers between devices, local(): bwd = [lax.ppermute(blk, 'tm', back) for blk in bwd]  18.3 us
    add x6, other arithmetic, local(): current = part(turn, h) + moved  9.11 us
    ppermute x6, waiting for transfers between devices, local(): fwd = [lax.ppermute(blk, 'tm', ring) for blk in fwd]  7.71 us
    ppermute x2, waiting for transfers between devices, shifted(): return lax.ppermute(block, axis, route)  5.88 us
    ppermute x2, starting transfers between devices, shifted(): return lax.ppermute(block, axis, route)  5.56 us
  transfers between devices with their start and end apart: 16, of which 9 were waited for; matrix products, arithmetic and copies ran while one was open for 11% of the time, Pallas kernels for 0%

profile of v4, /device:TPU:504, one launch (start us, length us, event | category | flops | bytes accessed | tf_op | source)
XLA Modules:
  0.0 130.7 jit_solution(14633406514391841910)
XLA Ops:
  0.0 1.5 %pad_maximum_fusion.6 = (f32[4,256,22]{2,1,0:T(8,128)S(1)}, f32[4,256,22]{2,1,0:T(8,128)S(1)}) fusion(f32[1,256,512]{2,1,0:T(8,128)} %bitcast.743, f32[1,256,512]{2,1,0:T(8,128)} %bitcast.745, f32[1,256,512]{2,1,0:T(8,128)} %bitcast.747, f32[1,256,512]{2,1,0:T(8,128)} %param.4), kind=kLoop, calls=%fused_computation.321 | loop fusion | flops 135168 | bytes 2277376 | tf_op jit(solution)/shard_map/slice | solution.py:21
  1.6 1.9 %collective-permute-start = (f32[4,256,22]{2,1,0:T(8,128)S(1)}, f32[4,256,22]{2,1,0:T(8,128)S(1)}, u32[]{:S(2)}, u32[]{:S(2)}) collective-permute-start(f32[4,256,22]{2,1,0:T(8,128)S(1)} %get-tuple-element.7), channel_id=1, source_target_pairs={{0,1},{1,2},{2,3},{3,4},{4,5},{5,6},{6,7},{7,8},{8,9},{9,10},{10,1... | collective-permute-start | bytes 270344 | tf_op jit(solution)/shard_map/ppermute | solution.py:16
  3.5 3.6 %collective-permute-start.1 = (f32[4,256,22]{2,1,0:T(8,128)S(1)}, f32[4,256,22]{2,1,0:T(8,128)}, u32[]{:S(2)}, u32[]{:S(2)}) collective-permute-start(f32[4,256,22]{2,1,0:T(8,128)S(1)} %get-tuple-element.8), channel_id=1, source_target_pairs={{1,0},{2,1},{3,2},{4,3},{5,4},{6,5},{7,6},{8,7},{9,8},{10,9},{11,1... | collective-permute-start | bytes 270344 | tf_op jit(solution)/shard_map/ppermute | solution.py:16
  7.1 4.9 %collective-permute-done = f32[4,256,22]{2,1,0:T(8,128)S(1)} collective-permute-done((f32[4,256,22]{2,1,0:T(8,128)S(1)}, f32[4,256,22]{2,1,0:T(8,128)S(1)}, u32[]{:S(2)}, u32[]{:S(2)}) %collective-permute-start) | collective-permute-done | bytes 90144 | tf_op jit(solution)/shard_map/ppermute | solution.py:16
  13.8 2.5 %pad_maximum_fusion = f32[4,256,556]{2,1,0:T(8,128)S(1)} fusion(f32[4,256,22]{2,1,0:T(8,128)} %collective-permute-done.1, f32[1,256,512]{2,1,0:T(8,128)S(1)} %bitcast.744, f32[1,256,512]{2,1,0:T(8,128)} %bitcast.746, f32[1,256,512]{2,1,0:T(8,128)} %bitcast.748, f32[1,256,512]{2,1,0:T(8,128)} %param.4, f32[4,256,22]{2,1,0:T(8,128)} %copy-done.4), kind=kLoop, calls=%fused_computation | loop fusion | flops 2846720 | bytes 4554752 | tf_op jit(solution)/shard_map/concatenate | solution.py:24
  16.4 1.3 fusion.64
  17.9 1.3 fusion.61
  19.2 1.3 fusion.58
  20.5 1.3 fusion.55
  21.7 1.3 fusion.52
  23.0 1.3 fusion.49
  24.3 2.3 %fusion.143 = (f32[256,542]{1,0:T(8,128)S(1)}, f32[256,542]{1,0:T(8,128)S(1)}) fusion(f32[256,544]{1,0:T(8,128)S(1)} %fusion.49, f32[4,256,556]{2,1,0:T(8,128)S(1)} %pad_maximum_fusion, f32[256,544]{1,0:T(8,128)S(1)} %slice.1100, f32[256,556]{1,0:T(8,128)S(1)} %slice_bitcast_fusion), kind=kLoop, calls=%fused_computation.236 | loop fusion | flops 6382592 | bytes 8318976 | tf_op jit(solution)/shard_map/add | solution.py:41
  26.6 2.3 %subtract_select_fusion = f32[256,540]{1,0:T(8,128)S(1)} fusion(f32[256,542]{1,0:T(8,128)S(1)} %get-tuple-element.6, f32[4,256,556]{2,1,0:T(8,128)S(1)} %pad_maximum_fusion, f32[256,542]{1,0:T(8,128)S(1)} %get-tuple-element.5, pred[]{:T(512)S(6)} %eq.3), kind=kLoop, calls=%fused_computation.1 | loop fusion | flops 6635520 | bytes 7761921 | tf_op jit(solution)/shard_map/jit(_where)/select_n | solution.py:67
  29.9 3.2 %collective-permute-start.12 = (f32[128,540]{1,0:T(8,128)}, f32[128,540]{1,0:T(8,128)}, u32[]{:S(2)}, u32[]{:S(2)}) collective-permute-start(f32[128,540]{1,0:T(8,128)} %get-tuple-element.10), channel_id=1, source_target_pairs={{64,0},{128,64},{192,128},{256,192},{320,256},{384,320},{448,384},... | collective-permute-start | bytes 829448 | tf_op jit(solution)/shard_map/ppermute | solution.py:82
  33.1 3.3 %collective-permute-start.8 = (f32[128,540]{1,0:T(8,128)}, f32[128,540]{1,0:T(8,128)}, u32[]{:S(2)}, u32[]{:S(2)}) collective-permute-start(f32[128,540]{1,0:T(8,128)} %get-tuple-element.9), channel_id=1, source_target_pairs={{64,0},{128,64},{192,128},{256,192},{320,256},{384,320},{448,384},... | collective-permute-start | bytes 829448 | tf_op jit(solution)/shard_map/ppermute | solution.py:82
  37.4 3.8 %collective-permute-start.2 = (f32[128,524]{1,0:T(8,128)}, f32[128,524]{1,0:T(8,128)}, u32[]{:S(2)}, u32[]{:S(2)}) collective-permute-start(f32[128,524]{1,0:T(8,128)} %get-tuple-element.11), channel_id=1, source_target_pairs={{0,64},{64,128},{128,192},{192,256},{256,320},{320,384},{384,448},... | collective-permute-start | bytes 804872 | tf_op jit(solution)/shard_map/ppermute | solution.py:87
  41.2 2.6 %collective-permute-start.3 = (f32[128,524]{1,0:T(8,128)}, f32[128,524]{1,0:T(8,128)}, u32[]{:S(2)}, u32[]{:S(2)}) collective-permute-start(f32[128,524]{1,0:T(8,128)} %get-tuple-element.12), channel_id=1, source_target_pairs={{0,64},{64,128},{128,192},{192,256},{256,320},{320,384},{384,448},... | collective-permute-start | bytes 804872 | tf_op jit(solution)/shard_map/ppermute | solution.py:87
  43.8 5.7 %collective-permute-done.2 = f32[128,524]{1,0:T(8,128)} collective-permute-done((f32[128,524]{1,0:T(8,128)}, f32[128,524]{1,0:T(8,128)}, u32[]{:S(2)}, u32[]{:S(2)}) %collective-permute-start.2) | collective-permute-done | bytes 268320 | tf_op jit(solution)/shard_map/ppermute | solution.py:87
  49.5 5.0 %collective-permute-start.4 = (f32[128,524]{1,0:T(8,128)}, f32[128,524]{1,0:T(8,128)S(1)}, u32[]{:S(2)}, u32[]{:S(2)}) collective-permute-start(f32[128,524]{1,0:T(8,128)} %collective-permute-done.2), channel_id=1, source_target_pairs={{0,64},{64,128},{128,192},{192,256},{256,320},{320,384},{384,448},... | collective-permute-start | bytes 804872 | tf_op jit(solution)/shard_map/ppermute | solution.py:87
  54.5 2.0 %collective-permute-done.3 = f32[128,524]{1,0:T(8,128)} collective-permute-done((f32[128,524]{1,0:T(8,128)}, f32[128,524]{1,0:T(8,128)}, u32[]{:S(2)}, u32[]{:S(2)}) %collective-permute-start.3) | collective-permute-done | bytes 268320 | tf_op jit(solution)/shard_map/ppermute | solution.py:87
  56.6 5.0 %collective-permute-start.5 = (f32[128,524]{1,0:T(8,128)}, f32[128,524]{1,0:T(8,128)S(1)}, u32[]{:S(2)}, u32[]{:S(2)}) collective-permute-start(f32[128,524]{1,0:T(8,128)} %collective-permute-done.3), channel_id=1, source_target_pairs={{0,64},{64,128},{128,192},{192,256},{256,320},{320,384},{384,448},... | collective-permute-start | bytes 804872 | tf_op jit(solution)/shard_map/ppermute | solution.py:87
  62.7 1.9 %collective-permute-start.13 = (f32[128,536]{1,0:T(8,128)S(1)}, f32[128,536]{1,0:T(8,128)S(1)}, u32[]{:S(2)}, u32[]{:S(2)}) collective-permute-start(f32[128,536]{1,0:T(8,128)S(1)} %slice.1112), channel_id=1, source_target_pairs={{64,0},{128,64},{192,128},{256,192},{320,256},{384,320},{448,384},... | collective-permute-start | bytes 823304 | tf_op jit(solution)/shard_map/ppermute | solution.py:82
  65.7 2.2 %collective-permute-start.9 = (f32[128,536]{1,0:T(8,128)S(1)}, f32[128,536]{1,0:T(8,128)S(1)}, u32[]{:S(2)}, u32[]{:S(2)}) collective-permute-start(f32[128,536]{1,0:T(8,128)S(1)} %slice.1108), channel_id=1, source_target_pairs={{64,0},{128,64},{192,128},{256,192},{320,256},{384,320},{448,384},... | collective-permute-start | bytes 823304 | tf_op jit(solution)/shard_map/ppermute | solution.py:82
  69.1 1.3 fusion.44
  70.3 4.9 %collective-permute-start.6 = (f32[128,524]{1,0:T(8,128)S(1)}, f32[128,524]{1,0:T(8,128)S(1)}, u32[]{:S(2)}, u32[]{:S(2)}) collective-permute-start(f32[128,524]{1,0:T(8,128)S(1)} %collective-permute-done.4), channel_id=1, source_target_pairs={{0,64},{64,128},{128,192},{192,256},{256,320},{320,384},{384,448},... | collective-permute-start | bytes 804872 | tf_op jit(solution)/shard_map/ppermute | solution.py:87
  75.2 3.9 %collective-permute-start.7 = (f32[128,524]{1,0:T(8,128)S(1)}, f32[128,524]{1,0:T(8,128)S(1)}, u32[]{:S(2)}, u32[]{:S(2)}) collective-permute-start(f32[128,524]{1,0:T(8,128)S(1)} %collective-permute-done.5), channel_id=1, source_target_pairs={{0,64},{64,128},{128,192},{192,256},{256,320},{320,384},{384,448},... | collective-permute-start | bytes 804872 | tf_op jit(solution)/shard_map/ppermute | solution.py:87
  79.2 4.1 %collective-permute-done.9 = f32[128,536]{1,0:T(8,128)S(1)} collective-permute-done((f32[128,536]{1,0:T(8,128)S(1)}, f32[128,536]{1,0:T(8,128)S(1)}, u32[]{:S(2)}, u32[]{:S(2)}) %collective-permute-start.9) | collective-permute-done | bytes 274464 | tf_op jit(solution)/shard_map/ppermute | solution.py:82
  83.4 1.9 %collective-permute-start.10 = (f32[128,532]{1,0:T(8,128)S(1)}, f32[128,532]{1,0:T(8,128)S(1)}, u32[]{:S(2)}, u32[]{:S(2)}) collective-permute-start(f32[128,532]{1,0:T(8,128)S(1)} %slice.1109), channel_id=1, source_target_pairs={{64,0},{128,64},{192,128},{256,192},{320,256},{384,320},{448,384},... | collective-permute-start | bytes 817160 | tf_op jit(solution)/shard_map/ppermute | solution.py:82
  85.5 1.9 %collective-permute-start.14 = (f32[128,532]{1,0:T(8,128)S(1)}, f32[128,532]{1,0:T(8,128)S(1)}, u32[]{:S(2)}, u32[]{:S(2)}) collective-permute-start(f32[128,532]{1,0:T(8,128)S(1)} %slice.1113), channel_id=1, source_target_pairs={{64,0},{128,64},{192,128},{256,192},{320,256},{384,320},{448,384},... | collective-permute-start | bytes 817160 | tf_op jit(solution)/shard_map/ppermute | solution.py:82
  87.4 1.3 fusion.41
  88.7 1.3 fusion.37
  90.0 7.1 %collective-permute-done.10 = f32[128,532]{1,0:T(8,128)S(1)} collective-permute-done((f32[128,532]{1,0:T(8,128)S(1)}, f32[128,532]{1,0:T(8,128)S(1)}, u32[]{:S(2)}, u32[]{:S(2)}) %collective-permute-start.10) | collective-permute-done | bytes 272416 | tf_op jit(solution)/shard_map/ppermute | solution.py:82
  97.2 1.9 %collective-permute-start.11 = (f32[128,528]{1,0:T(8,128)S(1)}, f32[128,528]{1,0:T(8,128)S(1)}, u32[]{:S(2)}, u32[]{:S(2)}) collective-permute-start(f32[128,528]{1,0:T(8,128)S(1)} %slice.1110), channel_id=1, source_target_pairs={{64,0},{128,64},{192,128},{256,192},{320,256},{384,320},{448,384},... | collective-permute-start | bytes 811016 | tf_op jit(solution)/shard_map/ppermute | solution.py:82
  99.2 4.9 %collective-permute-done.14 = f32[128,532]{1,0:T(8,128)S(1)} collective-permute-done((f32[128,532]{1,0:T(8,128)S(1)}, f32[128,532]{1,0:T(8,128)S(1)}, u32[]{:S(2)}, u32[]{:S(2)}) %collective-permute-start.14) | collective-permute-done | bytes 272416 | tf_op jit(solution)/shard_map/ppermute | solution.py:82
  104.3 1.9 %collective-permute-start.15 = (f32[128,528]{1,0:T(8,128)S(1)}, f32[128,528]{1,0:T(8,128)S(1)}, u32[]{:S(2)}, u32[]{:S(2)}) collective-permute-start(f32[128,528]{1,0:T(8,128)S(1)} %slice.1114), channel_id=1, source_target_pairs={{64,0},{128,64},{192,128},{256,192},{320,256},{384,320},{448,384},... | collective-permute-start | bytes 811016 | tf_op jit(solution)/shard_map/ppermute | solution.py:82
  106.2 1.3 fusion.34
  107.5 1.3 fusion.30
  108.8 2.4 %collective-permute-done.11 = f32[128,528]{1,0:T(8,128)S(1)} collective-permute-done((f32[128,528]{1,0:T(8,128)S(1)}, f32[128,528]{1,0:T(8,128)S(1)}, u32[]{:S(2)}, u32[]{:S(2)}) %collective-permute-start.11) | collective-permute-done | bytes 270368 | tf_op jit(solution)/shard_map/ppermute | solution.py:82
  111.1 6.2 %collective-permute-done.15 = f32[128,528]{1,0:T(8,128)S(1)} collective-permute-done((f32[128,528]{1,0:T(8,128)S(1)}, f32[128,528]{1,0:T(8,128)S(1)}, u32[]{:S(2)}, u32[]{:S(2)}) %collective-permute-start.15) | collective-permute-done | bytes 270368 | tf_op jit(solution)/shard_map/ppermute | solution.py:82
  117.3 1.3 fusion.27
  118.6 1.3 fusion.23
  119.9 1.3 fusion.20
  121.2 1.3 fusion.16
  122.4 1.5 %fusion.13 = f32[256,520]{1,0:T(8,128)S(1)} fusion(f32[4,256,556]{2,1,0:T(8,128)S(1)} %pad_maximum_fusion, f32[128,524]{1,0:T(8,128)S(1)} %collective-permute-done.5, f32[128,524]{1,0:T(8,128)S(1)} %collective-permute-done.4, f32[256,522]{1,0:T(8,128)S(1)} %fusion.16, pred[]{:T(512)S(6)} %ge.26), kind=kLoop, calls=%fused_computation.19 | loop fusion | flops 3727360 | bytes 5775361 | tf_op jit(solution)/shard_map/add | solution.py:101
  123.9 1.3 fusion.9
  125.2 2.5 %fusion.6 = f32[256,516]{1,0:T(8,128)S(1)} fusion(f32[4,256,556]{2,1,0:T(8,128)S(1)} %pad_maximum_fusion, f32[128,524]{1,0:T(8,128)} %collective-permute-done.3, f32[128,524]{1,0:T(8,128)} %collective-permute-done.2, f32[256,518]{1,0:T(8,128)S(1)} %fusion.9, pred[]{:T(512)S(6)} %ge.25), kind=kLoop, calls=%fused_computation.10 | loop fusion | flops 3698688 | bytes 5652481 | tf_op jit(solution)/shard_map/add | solution.py:101
  127.8 1.3 fusion.2
  129.1 1.6 %fusion.185 = f32[1,256,512]{2,1,0:T(8,128)} fusion(f32[256,540]{1,0:T(8,128)S(1)} %subtract_select_fusion, f32[256,512]{1,0:T(8,128)S(1)} %copy-done.1, f32[256,514]{1,0:T(8,128)S(1)} %fusion.2, f32[256,512]{1,0:T(8,128)S(1)} %copy-done.2, f32[256,512]{1,0:T(8,128)S(1)} %copy-done.3, pred[]{:T(512)S(6)} %ge.24), kind=kLoop, calls=%fused_computation.317 | loop fusion | flops 3538944 | bytes 4849665 | tf_op jit(solution)/shard_map/broadcast_in_dim | solution.py:102
  (29 shorter events, 8.0 us)
Async XLA Ops:
  0.0 13.8 %copy-start = (f32[256,512]{1,0:T(8,128)S(1)}, f32[256,512]{1,0:T(8,128)}, u32[]{:S(2)}) copy-start(f32[256,512]{1,0:T(8,128)} %param.7) | copy-start | bytes 1572868
  1.6 10.5 %collective-permute-start = (f32[4,256,22]{2,1,0:T(8,128)S(1)}, f32[4,256,22]{2,1,0:T(8,128)S(1)}, u32[]{:S(2)}, u32[]{:S(2)}) collective-permute-start(f32[4,256,22]{2,1,0:T(8,128)S(1)} %get-tuple-element.7), channel_id=1, source_target_pairs={{0,1},{1,2},{2,3},{3,4},{4,5},{5,6},{6,7},{7,8},{8,9},{9,10},{10,1... | collective-permute-start | bytes 270344 | tf_op jit(solution)/shard_map/ppermute | solution.py:16
  3.5 10.3 %collective-permute-start.1 = (f32[4,256,22]{2,1,0:T(8,128)S(1)}, f32[4,256,22]{2,1,0:T(8,128)}, u32[]{:S(2)}, u32[]{:S(2)}) collective-permute-start(f32[4,256,22]{2,1,0:T(8,128)S(1)} %get-tuple-element.8), channel_id=1, source_target_pairs={{1,0},{2,1},{3,2},{4,3},{5,4},{6,5},{7,6},{8,7},{9,8},{10,9},{11,1... | collective-permute-start | bytes 270344 | tf_op jit(solution)/shard_map/ppermute | solution.py:16
  12.1 0.8 copy-start.4
  29.9 31.7 %collective-permute-start.12 = (f32[128,540]{1,0:T(8,128)}, f32[128,540]{1,0:T(8,128)}, u32[]{:S(2)}, u32[]{:S(2)}) collective-permute-start(f32[128,540]{1,0:T(8,128)} %get-tuple-element.10), channel_id=1, source_target_pairs={{64,0},{128,64},{192,128},{256,192},{320,256},{384,320},{448,384},... | collective-permute-start | bytes 829448 | tf_op jit(solution)/shard_map/ppermute | solution.py:82
  33.1 31.5 %collective-permute-start.8 = (f32[128,540]{1,0:T(8,128)}, f32[128,540]{1,0:T(8,128)}, u32[]{:S(2)}, u32[]{:S(2)}) collective-permute-start(f32[128,540]{1,0:T(8,128)} %get-tuple-element.9), channel_id=1, source_target_pairs={{64,0},{128,64},{192,128},{256,192},{320,256},{384,320},{448,384},... | collective-permute-start | bytes 829448 | tf_op jit(solution)/shard_map/ppermute | solution.py:82
  37.4 12.1 %collective-permute-start.2 = (f32[128,524]{1,0:T(8,128)}, f32[128,524]{1,0:T(8,128)}, u32[]{:S(2)}, u32[]{:S(2)}) collective-permute-start(f32[128,524]{1,0:T(8,128)} %get-tuple-element.11), channel_id=1, source_target_pairs={{0,64},{64,128},{128,192},{192,256},{256,320},{320,384},{384,448},... | collective-permute-start | bytes 804872 | tf_op jit(solution)/shard_map/ppermute | solution.py:87
  41.2 15.3 %collective-permute-start.3 = (f32[128,524]{1,0:T(8,128)}, f32[128,524]{1,0:T(8,128)}, u32[]{:S(2)}, u32[]{:S(2)}) collective-permute-start(f32[128,524]{1,0:T(8,128)} %get-tuple-element.12), channel_id=1, source_target_pairs={{0,64},{64,128},{128,192},{192,256},{256,320},{320,384},{384,448},... | collective-permute-start | bytes 804872 | tf_op jit(solution)/shard_map/ppermute | solution.py:87
  49.5 20.8 %collective-permute-start.4 = (f32[128,524]{1,0:T(8,128)}, f32[128,524]{1,0:T(8,128)S(1)}, u32[]{:S(2)}, u32[]{:S(2)}) collective-permute-start(f32[128,524]{1,0:T(8,128)} %collective-permute-done.2), channel_id=1, source_target_pairs={{0,64},{64,128},{128,192},{192,256},{256,320},{320,384},{384,448},... | collective-permute-start | bytes 804872 | tf_op jit(solution)/shard_map/ppermute | solution.py:87
  56.6 18.7 %collective-permute-start.5 = (f32[128,524]{1,0:T(8,128)}, f32[128,524]{1,0:T(8,128)S(1)}, u32[]{:S(2)}, u32[]{:S(2)}) collective-permute-start(f32[128,524]{1,0:T(8,128)} %collective-permute-done.3), channel_id=1, source_target_pairs={{0,64},{64,128},{128,192},{192,256},{256,320},{320,384},{384,448},... | collective-permute-start | bytes 804872 | tf_op jit(solution)/shard_map/ppermute | solution.py:87
  62.7 22.6 %collective-permute-start.13 = (f32[128,536]{1,0:T(8,128)S(1)}, f32[128,536]{1,0:T(8,128)S(1)}, u32[]{:S(2)}, u32[]{:S(2)}) collective-permute-start(f32[128,536]{1,0:T(8,128)S(1)} %slice.1112), channel_id=1, source_target_pairs={{64,0},{128,64},{192,128},{256,192},{320,256},{384,320},{448,384},... | collective-permute-start | bytes 823304 | tf_op jit(solution)/shard_map/ppermute | solution.py:82
  65.7 17.5 %collective-permute-start.9 = (f32[128,536]{1,0:T(8,128)S(1)}, f32[128,536]{1,0:T(8,128)S(1)}, u32[]{:S(2)}, u32[]{:S(2)}) collective-permute-start(f32[128,536]{1,0:T(8,128)S(1)} %slice.1108), channel_id=1, source_target_pairs={{64,0},{128,64},{192,128},{256,192},{320,256},{384,320},{448,384},... | collective-permute-start | bytes 823304 | tf_op jit(solution)/shard_map/ppermute | solution.py:82
  70.3 49.5 %collective-permute-start.6 = (f32[128,524]{1,0:T(8,128)S(1)}, f32[128,524]{1,0:T(8,128)S(1)}, u32[]{:S(2)}, u32[]{:S(2)}) collective-permute-start(f32[128,524]{1,0:T(8,128)S(1)} %collective-permute-done.4), channel_id=1, source_target_pairs={{0,64},{64,128},{128,192},{192,256},{256,320},{320,384},{384,448},... | collective-permute-start | bytes 804872 | tf_op jit(solution)/shard_map/ppermute | solution.py:87
  75.2 44.6 %collective-permute-start.7 = (f32[128,524]{1,0:T(8,128)S(1)}, f32[128,524]{1,0:T(8,128)S(1)}, u32[]{:S(2)}, u32[]{:S(2)}) collective-permute-start(f32[128,524]{1,0:T(8,128)S(1)} %collective-permute-done.5), channel_id=1, source_target_pairs={{0,64},{64,128},{128,192},{192,256},{256,320},{320,384},{384,448},... | collective-permute-start | bytes 804872 | tf_op jit(solution)/shard_map/ppermute | solution.py:87
  83.4 13.7 %collective-permute-start.10 = (f32[128,532]{1,0:T(8,128)S(1)}, f32[128,532]{1,0:T(8,128)S(1)}, u32[]{:S(2)}, u32[]{:S(2)}) collective-permute-start(f32[128,532]{1,0:T(8,128)S(1)} %slice.1109), channel_id=1, source_target_pairs={{64,0},{128,64},{192,128},{256,192},{320,256},{384,320},{448,384},... | collective-permute-start | bytes 817160 | tf_op jit(solution)/shard_map/ppermute | solution.py:82
  85.5 18.6 %collective-permute-start.14 = (f32[128,532]{1,0:T(8,128)S(1)}, f32[128,532]{1,0:T(8,128)S(1)}, u32[]{:S(2)}, u32[]{:S(2)}) collective-permute-start(f32[128,532]{1,0:T(8,128)S(1)} %slice.1113), channel_id=1, source_target_pairs={{64,0},{128,64},{192,128},{256,192},{320,256},{384,320},{448,384},... | collective-permute-start | bytes 817160 | tf_op jit(solution)/shard_map/ppermute | solution.py:82
  97.2 13.9 %collective-permute-start.11 = (f32[128,528]{1,0:T(8,128)S(1)}, f32[128,528]{1,0:T(8,128)S(1)}, u32[]{:S(2)}, u32[]{:S(2)}) collective-permute-start(f32[128,528]{1,0:T(8,128)S(1)} %slice.1110), channel_id=1, source_target_pairs={{64,0},{128,64},{192,128},{256,192},{320,256},{384,320},{448,384},... | collective-permute-start | bytes 811016 | tf_op jit(solution)/shard_map/ppermute | solution.py:82
  104.3 13.0 %collective-permute-start.15 = (f32[128,528]{1,0:T(8,128)S(1)}, f32[128,528]{1,0:T(8,128)S(1)}, u32[]{:S(2)}, u32[]{:S(2)}) collective-permute-start(f32[128,528]{1,0:T(8,128)S(1)} %slice.1114), channel_id=1, source_target_pairs={{64,0},{128,64},{192,128},{256,192},{320,256},{384,320},{448,384},... | collective-permute-start | bytes 811016 | tf_op jit(solution)/shard_map/ppermute | solution.py:82
  127.7 1.3 %copy-start.1 = (f32[256,512]{1,0:T(8,128)S(1)}, f32[256,512]{1,0:T(8,128)}, u32[]{:S(2)}) copy-start(f32[256,512]{1,0:T(8,128)} %param.7) | copy-start | bytes 1572868
  127.7 1.3 %copy-start.2 = (f32[256,512]{1,0:T(8,128)S(1)}, f32[256,512]{1,0:T(8,128)}, u32[]{:S(2)}) copy-start(f32[256,512]{1,0:T(8,128)} %param.6) | copy-start | bytes 1572868
  127.8 1.3 %copy-start.3 = (f32[256,512]{1,0:T(8,128)S(1)}, f32[256,512]{1,0:T(8,128)}, u32[]{:S(2)}) copy-start(f32[256,512]{1,0:T(8,128)} %param.5) | copy-start | bytes 1572868

commit v5 on v3

--- a/solution.py
+++ b/solution.py
@@ -65,7 +65,7 @@
     old_coarse, _ = run(start_c, chain + CSTEPS, CSTEPS, DT * FINE / CSTEPS)
     me = lax.axis_index("tm")
     carried = jnp.where(me == 0, field, field - old_coarse)
-    ring = [(i, (i + 1) % slices) for i in range(slices)]
+    ring = [(i, i + 1) for i in range(slices - 1)]
     back = [((i + 1) % slices, i) for i in range(slices)]
     ahead = slices // 2
     behind = slices - 1 - ahead
@@ -87,6 +87,8 @@
         blk = got[j]
         extra = (blk.shape[-1] - n) // 2 - h
         blk = blk[:, extra: extra + n + 2 * h]
+        if j >= ahead:
+            return blk
         return jnp.where(me >= slices - 1 - j, blk, jnp.zeros_like(blk))
 
     h = chain

time: 109 us -> 109 us (level)
  the two profiles are of different devices: /device:TPU:504 before, /device:TPU:156 now
where the time goes in v5:
time: 109 us
  waiting for transfers between devices  50.4 us (46%)
  starting transfers between devices  29.3 us (27%)
  other arithmetic  21.4 us (20%)
  local copies, waits for them, and re-layouts  7.34 us (7%)
    ppermute x4, waiting for transfers between devices, local(): lax.ppermute(block[:, chain - keep:chain + n + keep] if r == 1 else block...  36.3 us
    ppermute x3, starting transfers between devices, local(): block = lax.ppermute(block, 'tm', ring)  15.4 us
    ppermute x3, waiting for transfers between devices, local(): block = lax.ppermute(block, 'tm', ring)  11.9 us
    add x14, other arithmetic, advance(): return mid - size * moved + size * coef[2] * spread  11.2 us
    ppermute x4, starting transfers between devices, local(): lax.ppermute(block[:, chain - keep:chain + n + keep] if r == 1 else block...  8.29 us
    add x6, other arithmetic, local(): current = part(turn, h) + moved  6.73 us
    ppermute x2, starting transfers between devices, shifted(): return lax.ppermute(block, axis, route)  5.56 us
    unnamed x20, local copies, waits for them, and re-layouts  4.26 us
  transfers between devices with their start and end apart: 9, of which 6 were waited for; matrix products, arithmetic and copies ran while one was open for 7% of the time, Pallas kernels for 0%

profile of v5, /device:TPU:156, one launch (start us, length us, event | category | flops | bytes accessed | tf_op | source)
XLA Modules:
  0.0 108.7 jit_solution(8582789494039589131)
XLA Ops:
  0.0 1.3 %copy.5 = f32[256,512]{0,1:T(8,128)S(1)} copy(f32[256,512]{1,0:T(8,128)} %param.5) | data formatting | bytes 1048576 | tf_op args[1]
  1.3 1.2 %copy.6 = f32[256,512]{0,1:T(8,128)S(1)} copy(f32[256,512]{1,0:T(8,128)} %param.6) | data formatting | bytes 1048576 | tf_op args[2]
  2.6 0.2 copy.7
  2.8 0.2 copy.8
  3.1 1.9 %collective-permute-start = (f32[4,256,22]{1,2,0:T(8,128)S(1)}, f32[4,256,22]{1,2,0:T(8,128)S(1)}, u32[]{:S(2)}, u32[]{:S(2)}) collective-permute-start(f32[4,256,22]{1,2,0:T(8,128)S(1)} %get-tuple-element.7), channel_id=1, source_target_pairs={{0,1},{1,2},{2,3},{3,4},{4,5},{5,6},{6,7},{7,8},{8,9},{9,10},{10,1... | collective-permute-start | bytes 270344 | tf_op jit(solution)/shard_map/ppermute | solution.py:16
  5.0 3.6 %collective-permute-start.1 = (f32[4,256,22]{1,2,0:T(8,128)S(1)}, f32[4,256,22]{1,2,0:T(8,128)S(1)}, u32[]{:S(2)}, u32[]{:S(2)}) collective-permute-start(f32[4,256,22]{1,2,0:T(8,128)S(1)} %get-tuple-element.8), channel_id=1, source_target_pairs={{1,0},{2,1},{3,2},{4,3},{5,4},{6,5},{7,6},{8,7},{9,8},{10,9},{11,1... | collective-permute-start | bytes 270344 | tf_op jit(solution)/shard_map/ppermute | solution.py:16
  8.6 0.3 collective-permute-done
  9.0 1.8 %collective-permute-done.1 = f32[4,256,22]{1,2,0:T(8,128)S(1)} collective-permute-done((f32[4,256,22]{1,2,0:T(8,128)S(1)}, f32[4,256,22]{1,2,0:T(8,128)S(1)}, u32[]{:S(2)}, u32[]{:S(2)}) %collective-permute-start.1) | collective-permute-done | bytes 90144 | tf_op jit(solution)/shard_map/ppermute | solution.py:16
  10.8 1.4 %pad_maximum_fusion = f32[4,256,556]{1,2,0:T(8,128)S(1)} fusion(f32[4,256,22]{1,2,0:T(8,128)S(1)} %collective-permute-done.1, f32[1,256,512]{1,2,0:T(8,128)} %bitcast.748, f32[1,256,512]{1,2,0:T(8,128)S(1)} %bitcast.746, f32[1,256,512]{1,2,0:T(8,128)S(1)} %bitcast.744, f32[1,256,512]{1,2,0:T(8,128)} %copy-done.4, f32[4,256,22]{1,2,0:T(8,128)S(1)} %collective-permute-done), kind=kLoop, calls=%fused_computation | loop fusion | flops 2846720 | bytes 4554752 | tf_op jit(solution)/shard_map/concatenate | solution.py:24
  12.3 0.8 fusion.2
  13.2 0.8 fusion.19
  13.9 0.8 fusion.16
  14.7 0.8 fusion.13
  15.5 0.8 fusion.10
  16.3 0.8 fusion.45
  17.0 1.3 %fusion.64 = (f32[256,542]{0,1:T(8,128)S(1)}, f32[256,542]{0,1:T(8,128)S(1)}) fusion(f32[256,544]{0,1:T(8,128)S(1)} %fusion.45, f32[4,256,556]{1,2,0:T(8,128)S(1)} %pad_maximum_fusion, f32[256,544]{0,1:T(8,128)S(1)} %slice.1076, f32[256,556]{0,1:T(8,128)S(1)} %slice_bitcast_fusion), kind=kLoop, calls=%fused_computation.158 | loop fusion | flops 6382592 | bytes 7237632 | tf_op jit(solution)/shard_map/add | solution.py:41
  18.3 1.3 %subtract_select_fusion = f32[256,540]{0,1:T(8,128)S(1)} fusion(f32[256,542]{0,1:T(8,128)S(1)} %get-tuple-element.6, f32[4,256,556]{1,2,0:T(8,128)S(1)} %pad_maximum_fusion, f32[256,542]{0,1:T(8,128)S(1)} %get-tuple-element.5, pred[]{:T(512)S(6)} %eq.3), kind=kLoop, calls=%fused_computation.49 | loop fusion | flops 6635520 | bytes 6680577 | tf_op jit(solution)/shard_map/jit(_where)/select_n | solution.py:67
  19.7 2.4 %collective-permute-start.5 = (f32[256,540]{0,1:T(8,128)S(1)}, f32[256,540]{0,1:T(8,128)S(1)}, u32[]{:S(2)}, u32[]{:S(2)}) collective-permute-start(f32[256,540]{0,1:T(8,128)S(1)} %subtract_select_fusion), channel_id=1, source_target_pairs={{64,0},{128,64},{192,128},{256,192},{320,256},{384,320},{448,384},... | collective-permute-start | bytes 1658888 | tf_op jit(solution)/shard_map/ppermute | solution.py:76
  22.1 4.7 %collective-permute-start.2 = (f32[256,524]{0,1:T(8,128)S(1)}, f32[256,524]{0,1:T(8,128)}, u32[]{:S(2)}, u32[]{:S(2)}) collective-permute-start(f32[256,524]{0,1:T(8,128)S(1)} %slice.1081), channel_id=1, source_target_pairs={{0,64},{64,128},{128,192},{192,256},{256,320},{320,384},{384,448},... | collective-permute-start | bytes 1609736 | tf_op jit(solution)/shard_map/ppermute | solution.py:83
  26.8 9.9 %collective-permute-done.5 = f32[256,540]{0,1:T(8,128)S(1)} collective-permute-done((f32[256,540]{0,1:T(8,128)S(1)}, f32[256,540]{0,1:T(8,128)S(1)}, u32[]{:S(2)}, u32[]{:S(2)}) %collective-permute-start.5) | collective-permute-done | bytes 552992 | tf_op jit(solution)/shard_map/ppermute | solution.py:76
  36.7 0.8 copy-done.5
  37.5 0.8 slice.1084
  38.3 1.9 %collective-permute-start.6 = (f32[256,536]{0,1:T(8,128)}, f32[256,536]{0,1:T(8,128)}, u32[]{:S(2)}, u32[]{:S(2)}) collective-permute-start(f32[256,536]{0,1:T(8,128)} %slice.1084), channel_id=1, source_target_pairs={{64,0},{128,64},{192,128},{256,192},{320,256},{384,320},{448,384},... | collective-permute-start | bytes 1646600 | tf_op jit(solution)/shard_map/ppermute | solution.py:76
  40.2 5.1 %collective-permute-start.3 = (f32[256,524]{0,1:T(8,128)}, f32[256,524]{0,1:T(8,128)}, u32[]{:S(2)}, u32[]{:S(2)}) collective-permute-start(f32[256,524]{0,1:T(8,128)} %collective-permute-done.2), channel_id=1, source_target_pairs={{0,64},{64,128},{128,192},{192,256},{256,320},{320,384},{384,448},... | collective-permute-start | bytes 1609736 | tf_op jit(solution)/shard_map/ppermute | solution.py:83
  45.5 0.8 fusion.42
  46.2 11.9 %collective-permute-done.3 = f32[256,524]{0,1:T(8,128)} collective-permute-done((f32[256,524]{0,1:T(8,128)}, f32[256,524]{0,1:T(8,128)}, u32[]{:S(2)}, u32[]{:S(2)}) %collective-permute-start.3) | collective-permute-done | bytes 536608 | tf_op jit(solution)/shard_map/ppermute | solution.py:83
  58.2 5.6 %collective-permute-start.4 = (f32[256,524]{0,1:T(8,128)}, f32[256,524]{0,1:T(8,128)S(1)}, u32[]{:S(2)}, u32[]{:S(2)}) collective-permute-start(f32[256,524]{0,1:T(8,128)} %collective-permute-done.3), channel_id=1, source_target_pairs={{0,64},{64,128},{128,192},{192,256},{256,320},{320,384},{384,448},... | collective-permute-start | bytes 1609736 | tf_op jit(solution)/shard_map/ppermute | solution.py:83
  63.8 1.1 %slice.1085 = f32[256,532]{0,1:T(8,128)S(1)} slice(f32[256,536]{0,1:T(8,128)} %collective-permute-done.6), slice={[0:256], [2:534]} | slice | bytes 1089536 | tf_op jit(solution)/shard_map/slice | solution.py:79
  64.9 2.1 %collective-permute-start.7 = (f32[256,532]{0,1:T(8,128)S(1)}, f32[256,532]{0,1:T(8,128)S(1)}, u32[]{:S(2)}, u32[]{:S(2)}) collective-permute-start(f32[256,532]{0,1:T(8,128)S(1)} %slice.1085), channel_id=1, source_target_pairs={{64,0},{128,64},{192,128},{256,192},{320,256},{384,320},{448,384},... | collective-permute-start | bytes 1634312 | tf_op jit(solution)/shard_map/ppermute | solution.py:76
  67.0 0.8 fusion.93
  67.8 0.8 fusion.89
  68.6 13.6 %collective-permute-done.7 = f32[256,532]{0,1:T(8,128)S(1)} collective-permute-done((f32[256,532]{0,1:T(8,128)S(1)}, f32[256,532]{0,1:T(8,128)S(1)}, u32[]{:S(2)}, u32[]{:S(2)}) %collective-permute-start.7) | collective-permute-done | bytes 544800 | tf_op jit(solution)/shard_map/ppermute | solution.py:76
  82.2 1.9 %collective-permute-start.8 = (f32[256,528]{0,1:T(8,128)S(1)}, f32[256,528]{0,1:T(8,128)S(1)}, u32[]{:S(2)}, u32[]{:S(2)}) collective-permute-start(f32[256,528]{0,1:T(8,128)S(1)} %slice.1086), channel_id=1, source_target_pairs={{64,0},{128,64},{192,128},{256,192},{320,256},{384,320},{448,384},... | collective-permute-start | bytes 1622024 | tf_op jit(solution)/shard_map/ppermute | solution.py:76
  84.1 0.8 fusion.86
  85.0 0.7 fusion.82
  85.7 12.8 %collective-permute-done.8 = f32[256,528]{0,1:T(8,128)S(1)} collective-permute-done((f32[256,528]{0,1:T(8,128)S(1)}, f32[256,528]{0,1:T(8,128)S(1)}, u32[]{:S(2)}, u32[]{:S(2)}) %collective-permute-start.8) | collective-permute-done | bytes 540704 | tf_op jit(solution)/shard_map/ppermute | solution.py:76
  98.5 0.8 fusion.127
  99.3 0.7 fusion.123
  100.0 0.7 fusion.120
  100.7 0.7 fusion.116
  101.4 1.8 %fusion.161 = f32[256,520]{0,1:T(8,128)S(1)} fusion(f32[4,256,556]{1,2,0:T(8,128)S(1)} %pad_maximum_fusion, f32[256,524]{0,1:T(8,128)} %collective-permute-done.3, f32[256,522]{0,1:T(8,128)S(1)} %fusion.116), kind=kLoop, calls=%fused_computation.311 | loop fusion | flops 3461120 | bytes 4800512 | tf_op jit(solution)/shard_map/add | solution.py:98
  103.3 0.7 fusion.157
  104.0 1.8 %fusion.154 = f32[256,516]{0,1:T(8,128)S(1)} fusion(f32[4,256,556]{1,2,0:T(8,128)S(1)} %pad_maximum_fusion, f32[256,524]{0,1:T(8,128)} %collective-permute-done.2, f32[256,518]{0,1:T(8,128)S(1)} %fusion.157), kind=kLoop, calls=%fused_computation.302 | loop fusion | flops 3434496 | bytes 4784128 | tf_op jit(solution)/shard_map/add | solution.py:98
  105.8 0.7 fusion.150
  106.6 0.3 copy-done.1
  106.9 0.2 copy-done.3
  107.0 0.7 fusion.182
  107.7 1.0 copy.14
  (22 shorter events, 0.3 us)
Async XLA Ops:
  0.0 2.6 %copy-start.6 = (f32[256,512]{1,0:T(8,128)S(1)}, f32[256,512]{1,0:T(8,128)}, u32[]{:S(2)}) copy-start(f32[256,512]{1,0:T(8,128)} %param.7) | copy-start | bytes 1572868
  0.0 2.8 %copy-start.7 = (f32[1,256,512]{2,1,0:T(8,128)S(1)}, f32[1,256,512]{2,1,0:T(8,128)}, u32[]{:S(2)}) copy-start(f32[1,256,512]{2,1,0:T(8,128)} %param.4) | copy-start | bytes 1572868
  2.8 6.2 %copy-start = (f32[256,512]{0,1:T(8,128)}, f32[256,512]{0,1:T(8,128)S(1)}, u32[]{:S(2)}) copy-start(f32[256,512]{0,1:T(8,128)S(1)} %copy.7) | copy-start | bytes 1572868
  3.0 6.0 %copy-start.4 = (f32[1,256,512]{1,2,0:T(8,128)}, f32[1,256,512]{1,2,0:T(8,128)S(1)}, u32[]{:S(2)}) copy-start(f32[1,256,512]{1,2,0:T(8,128)S(1)} %copy.8) | copy-start | bytes 1572868
  3.1 5.9 %collective-permute-start = (f32[4,256,22]{1,2,0:T(8,128)S(1)}, f32[4,256,22]{1,2,0:T(8,128)S(1)}, u32[]{:S(2)}, u32[]{:S(2)}) collective-permute-start(f32[4,256,22]{1,2,0:T(8,128)S(1)} %get-tuple-element.7), channel_id=1, source_target_pairs={{0,1},{1,2},{2,3},{3,4},{4,5},{5,6},{6,7},{7,8},{8,9},{9,10},{10,1... | collective-permute-start | bytes 270344 | tf_op jit(solution)/shard_map/ppermute | solution.py:16
  5.0 5.8 %collective-permute-start.1 = (f32[4,256,22]{1,2,0:T(8,128)S(1)}, f32[4,256,22]{1,2,0:T(8,128)S(1)}, u32[]{:S(2)}, u32[]{:S(2)}) collective-permute-start(f32[4,256,22]{1,2,0:T(8,128)S(1)} %get-tuple-element.8), channel_id=1, source_target_pairs={{1,0},{2,1},{3,2},{4,3},{5,4},{6,5},{7,6},{8,7},{9,8},{10,9},{11,1... | collective-permute-start | bytes 270344 | tf_op jit(solution)/shard_map/ppermute | solution.py:16
  19.7 2.4 %copy-start.2 = (f32[256,540]{0,1:T(8,128)}, f32[256,540]{0,1:T(8,128)S(1)}, u32[]{:S(2)}) copy-start(f32[256,540]{0,1:T(8,128)S(1)} %subtract_select_fusion) | copy-start | bytes 1658884
  19.7 17.0 %collective-permute-start.5 = (f32[256,540]{0,1:T(8,128)S(1)}, f32[256,540]{0,1:T(8,128)S(1)}, u32[]{:S(2)}, u32[]{:S(2)}) collective-permute-start(f32[256,540]{0,1:T(8,128)S(1)} %subtract_select_fusion), channel_id=1, source_target_pairs={{64,0},{128,64},{192,128},{256,192},{320,256},{384,320},{448,384},... | collective-permute-start | bytes 1658888 | tf_op jit(solution)/shard_map/ppermute | solution.py:76
  22.1 18.2 %collective-permute-start.2 = (f32[256,524]{0,1:T(8,128)S(1)}, f32[256,524]{0,1:T(8,128)}, u32[]{:S(2)}, u32[]{:S(2)}) collective-permute-start(f32[256,524]{0,1:T(8,128)S(1)} %slice.1081), channel_id=1, source_target_pairs={{0,64},{64,128},{128,192},{192,256},{256,320},{320,384},{384,448},... | collective-permute-start | bytes 1609736 | tf_op jit(solution)/shard_map/ppermute | solution.py:83
  36.7 0.8 copy-start.5
  38.3 25.5 %collective-permute-start.6 = (f32[256,536]{0,1:T(8,128)}, f32[256,536]{0,1:T(8,128)}, u32[]{:S(2)}, u32[]{:S(2)}) collective-permute-start(f32[256,536]{0,1:T(8,128)} %slice.1084), channel_id=1, source_target_pairs={{64,0},{128,64},{192,128},{256,192},{320,256},{384,320},{448,384},... | collective-permute-start | bytes 1646600 | tf_op jit(solution)/shard_map/ppermute | solution.py:76
  40.2 17.9 %collective-permute-start.3 = (f32[256,524]{0,1:T(8,128)}, f32[256,524]{0,1:T(8,128)}, u32[]{:S(2)}, u32[]{:S(2)}) collective-permute-start(f32[256,524]{0,1:T(8,128)} %collective-permute-done.2), channel_id=1, source_target_pairs={{0,64},{64,128},{128,192},{192,256},{256,320},{320,384},{384,448},... | collective-permute-start | bytes 1609736 | tf_op jit(solution)/shard_map/ppermute | solution.py:83
  58.2 41.8 %collective-permute-start.4 = (f32[256,524]{0,1:T(8,128)}, f32[256,524]{0,1:T(8,128)S(1)}, u32[]{:S(2)}, u32[]{:S(2)}) collective-permute-start(f32[256,524]{0,1:T(8,128)} %collective-permute-done.3), channel_id=1, source_target_pairs={{0,64},{64,128},{128,192},{192,256},{256,320},{320,384},{384,448},... | collective-permute-start | bytes 1609736 | tf_op jit(solution)/shard_map/ppermute | solution.py:83
  64.9 17.3 %collective-permute-start.7 = (f32[256,532]{0,1:T(8,128)S(1)}, f32[256,532]{0,1:T(8,128)S(1)}, u32[]{:S(2)}, u32[]{:S(2)}) collective-permute-start(f32[256,532]{0,1:T(8,128)S(1)} %slice.1085), channel_id=1, source_target_pairs={{64,0},{128,64},{192,128},{256,192},{320,256},{384,320},{448,384},... | collective-permute-start | bytes 1634312 | tf_op jit(solution)/shard_map/ppermute | solution.py:76
  82.2 16.3 %collective-permute-start.8 = (f32[256,528]{0,1:T(8,128)S(1)}, f32[256,528]{0,1:T(8,128)S(1)}, u32[]{:S(2)}, u32[]{:S(2)}) collective-permute-start(f32[256,528]{0,1:T(8,128)S(1)} %slice.1086), channel_id=1, source_target_pairs={{64,0},{128,64},{192,128},{256,192},{320,256},{384,320},{448,384},... | collective-permute-start | bytes 1622024 | tf_op jit(solution)/shard_map/ppermute | solution.py:76
  105.8 1.0 copy-start.1
  105.8 1.2 %copy-start.3 = (f32[256,540]{0,1:T(8,128)S(1)}, f32[256,540]{0,1:T(8,128)}, u32[]{:S(2)}) copy-start(f32[256,540]{0,1:T(8,128)} %copy-done.2) | copy-start | bytes 1658884

commit v6 on v5

--- a/solution.py
+++ b/solution.py
@@ -72,11 +72,8 @@
     got = {slices - 1: carried}
     block = carried
     for r in range(1, ahead + 1):
-        keep = chain - CSTEPS * (r - 1)
-        block = lax.ppermute(block[:, chain - keep: chain + n + keep] if r == 1 else block, "tm", back)
+        block = lax.ppermute(block, "tm", back)
         got[r - 1] = block
-        if r < ahead:
-            block = block[:, CSTEPS: block.shape[-1] - CSTEPS]
     wide_f = CSTEPS * behind
     block = carried[:, chain - wide_f: chain + n + wide_f]
     for r in range(1, behind + 1):

time: 109 us -> 108 us (level)
  local copies, waits for them, and re-layouts: 7.34 us -> 4.56 us
  other arithmetic: 21.4 us -> 22.5 us
    slice x3 -> x0, local copies, waits for them, and re-layouts: 1.97 us -> none  [local(): block = block[:, CSTEPS:block.shape[-1] - CSTEPS]]
    add x6, other arithmetic: 6.73 us -> 7.85 us  [local(): current = part(turn, h) + moved]
    unnamed x20 -> x18, local copies, waits for them, and re-layouts: 4.26 us -> 3.45 us
  transfers between devices with their start and end apart: 9 -> 9, of which waited for: 6 -> 6; matrix products, arithmetic and copies ran while one was open for 7% -> 6% of each run, Pallas kernels for 0% -> 0%
where the time goes in v6:
time: 108 us; the launch traced here: 107 us
  waiting for transfers between devices  50.3 us (47%)
  starting transfers between devices  29.3 us (27%)
  other arithmetic  22.5 us (21%)
  local copies, waits for them, and re-layouts  4.56 us (4%)
    ppermute x4, waiting for transfers between devices, local(): block = lax.ppermute(block, 'tm', back)  36.2 us
    ppermute x3, starting transfers between devices, local(): block = lax.ppermute(block, 'tm', ring)  15.4 us
    ppermute x3, waiting for transfers between devices, local(): block = lax.ppermute(block, 'tm', ring)  11.9 us
    add x14, other arithmetic, advance(): return mid - size * moved + size * coef[2] * spread  11.2 us
    ppermute x4, starting transfers between devices, local(): block = lax.ppermute(block, 'tm', back)  8.28 us
    add x6, other arithmetic, local(): current = part(turn, h) + moved  7.85 us
    ppermute x2, starting transfers between devices, shifted(): return lax.ppermute(block, axis, route)  5.56 us
    unnamed x18, local copies, waits for them, and re-layouts  3.45 us
  transfers between devices with their start and end apart: 9, of which 6 were waited for; matrix products, arithmetic and copies ran while one was open for 6% of the time, Pallas kernels for 0%

profile of v6, /device:TPU:156, one launch (start us, length us, event | category | flops | bytes accessed | tf_op | source)
XLA Modules:
  0.0 107.0 jit_solution(3904297262591690427)
XLA Ops:
  0.0 1.3 %copy.5 = f32[256,512]{0,1:T(8,128)S(1)} copy(f32[256,512]{1,0:T(8,128)} %param.5) | data formatting | bytes 1048576 | tf_op args[1]
  1.3 1.2 %copy.6 = f32[256,512]{0,1:T(8,128)S(1)} copy(f32[256,512]{1,0:T(8,128)} %param.6) | data formatting | bytes 1048576 | tf_op args[2]
  2.6 0.2 copy.7
  2.8 0.0 copy-start
  2.8 0.2 copy.8
  3.1 1.9 %collective-permute-start = (f32[4,256,22]{1,2,0:T(8,128)S(1)}, f32[4,256,22]{1,2,0:T(8,128)S(1)}, u32[]{:S(2)}, u32[]{:S(2)}) collective-permute-start(f32[4,256,22]{1,2,0:T(8,128)S(1)} %get-tuple-element.7), channel_id=1, source_target_pairs={{0,1},{1,2},{2,3},{3,4},{4,5},{5,6},{6,7},{7,8},{8,9},{9,10},{10,1... | collective-permute-start | bytes 270344 | tf_op jit(solution)/shard_map/ppermute | solution.py:16
  5.0 3.6 %collective-permute-start.1 = (f32[4,256,22]{1,2,0:T(8,128)S(1)}, f32[4,256,22]{1,2,0:T(8,128)S(1)}, u32[]{:S(2)}, u32[]{:S(2)}) collective-permute-start(f32[4,256,22]{1,2,0:T(8,128)S(1)} %get-tuple-element.8), channel_id=1, source_target_pairs={{1,0},{2,1},{3,2},{4,3},{5,4},{6,5},{7,6},{8,7},{9,8},{10,9},{11,1... | collective-permute-start | bytes 270344 | tf_op jit(solution)/shard_map/ppermute | solution.py:16
  8.6 0.3 collective-permute-done
  9.0 1.8 %collective-permute-done.1 = f32[4,256,22]{1,2,0:T(8,128)S(1)} collective-permute-done((f32[4,256,22]{1,2,0:T(8,128)S(1)}, f32[4,256,22]{1,2,0:T(8,128)S(1)}, u32[]{:S(2)}, u32[]{:S(2)}) %collective-permute-start.1) | collective-permute-done | bytes 90144 | tf_op jit(solution)/shard_map/ppermute | solution.py:16
  10.8 1.4 %pad_maximum_fusion = f32[4,256,556]{1,2,0:T(8,128)S(1)} fusion(f32[4,256,22]{1,2,0:T(8,128)S(1)} %collective-permute-done.1, f32[1,256,512]{1,2,0:T(8,128)} %bitcast.748, f32[1,256,512]{1,2,0:T(8,128)S(1)} %bitcast.746, f32[1,256,512]{1,2,0:T(8,128)S(1)} %bitcast.744, f32[1,256,512]{1,2,0:T(8,128)} %copy-done.4, f32[4,256,22]{1,2,0:T(8,128)S(1)} %collective-permute-done), kind=kLoop, calls=%fused_computation | loop fusion | flops 2846720 | bytes 4554752 | tf_op jit(solution)/shard_map/concatenate | solution.py:24
  12.3 0.8 fusion.2
  13.1 0.8 fusion.19
  13.9 0.8 fusion.16
  14.7 0.8 fusion.13
  15.5 0.8 fusion.10
  16.2 0.8 fusion.45
  17.0 1.3 %fusion.64 = (f32[256,542]{0,1:T(8,128)S(1)}, f32[256,542]{0,1:T(8,128)S(1)}) fusion(f32[256,544]{0,1:T(8,128)S(1)} %fusion.45, f32[4,256,556]{1,2,0:T(8,128)S(1)} %pad_maximum_fusion, f32[256,544]{0,1:T(8,128)S(1)} %slice.1076, f32[256,556]{0,1:T(8,128)S(1)} %slice_bitcast_fusion), kind=kLoop, calls=%fused_computation.158 | loop fusion | flops 6382592 | bytes 7237632 | tf_op jit(solution)/shard_map/add | solution.py:41
  18.3 1.3 %subtract_select_fusion = f32[256,540]{0,1:T(8,128)S(1)} fusion(f32[256,542]{0,1:T(8,128)S(1)} %get-tuple-element.6, f32[4,256,556]{1,2,0:T(8,128)S(1)} %pad_maximum_fusion, f32[256,542]{0,1:T(8,128)S(1)} %get-tuple-element.5, pred[]{:T(512)S(6)} %eq.3), kind=kLoop, calls=%fused_computation.49 | loop fusion | flops 6635520 | bytes 6680577 | tf_op jit(solution)/shard_map/jit(_where)/select_n | solution.py:67
  19.6 2.4 %collective-permute-start.5 = (f32[256,540]{0,1:T(8,128)S(1)}, f32[256,540]{0,1:T(8,128)}, u32[]{:S(2)}, u32[]{:S(2)}) collective-permute-start(f32[256,540]{0,1:T(8,128)S(1)} %subtract_select_fusion), channel_id=1, source_target_pairs={{64,0},{128,64},{192,128},{256,192},{320,256},{384,320},{448,384},... | collective-permute-start | bytes 1658888 | tf_op jit(solution)/shard_map/ppermute | solution.py:75
  22.1 4.7 %collective-permute-start.2 = (f32[256,524]{0,1:T(8,128)S(1)}, f32[256,524]{0,1:T(8,128)}, u32[]{:S(2)}, u32[]{:S(2)}) collective-permute-start(f32[256,524]{0,1:T(8,128)S(1)} %slice.1081), channel_id=1, source_target_pairs={{0,64},{64,128},{128,192},{192,256},{256,320},{320,384},{384,448},... | collective-permute-start | bytes 1609736 | tf_op jit(solution)/shard_map/ppermute | solution.py:80
  26.8 10.0 %collective-permute-done.5 = f32[256,540]{0,1:T(8,128)} collective-permute-done((f32[256,540]{0,1:T(8,128)S(1)}, f32[256,540]{0,1:T(8,128)}, u32[]{:S(2)}, u32[]{:S(2)}) %collective-permute-start.5) | collective-permute-done | bytes 552992 | tf_op jit(solution)/shard_map/ppermute | solution.py:75
  36.7 1.9 %collective-permute-start.6 = (f32[256,540]{0,1:T(8,128)}, f32[256,540]{0,1:T(8,128)}, u32[]{:S(2)}, u32[]{:S(2)}) collective-permute-start(f32[256,540]{0,1:T(8,128)} %collective-permute-done.5), channel_id=1, source_target_pairs={{64,0},{128,64},{192,128},{256,192},{320,256},{384,320},{448,384},... | collective-permute-start | bytes 1658888 | tf_op jit(solution)/shard_map/ppermute | solution.py:75
  38.7 5.1 %collective-permute-start.3 = (f32[256,524]{0,1:T(8,128)}, f32[256,524]{0,1:T(8,128)}, u32[]{:S(2)}, u32[]{:S(2)}) collective-permute-start(f32[256,524]{0,1:T(8,128)} %collective-permute-done.2), channel_id=1, source_target_pairs={{0,64},{64,128},{128,192},{192,256},{256,320},{320,384},{384,448},... | collective-permute-start | bytes 1609736 | tf_op jit(solution)/shard_map/ppermute | solution.py:80
  43.9 0.8 fusion.42
  44.7 11.9 %collective-permute-done.3 = f32[256,524]{0,1:T(8,128)} collective-permute-done((f32[256,524]{0,1:T(8,128)}, f32[256,524]{0,1:T(8,128)}, u32[]{:S(2)}, u32[]{:S(2)}) %collective-permute-start.3) | collective-permute-done | bytes 536608 | tf_op jit(solution)/shard_map/ppermute | solution.py:80
  56.6 5.6 %collective-permute-start.4 = (f32[256,524]{0,1:T(8,128)}, f32[256,524]{0,1:T(8,128)S(1)}, u32[]{:S(2)}, u32[]{:S(2)}) collective-permute-start(f32[256,524]{0,1:T(8,128)} %collective-permute-done.3), channel_id=1, source_target_pairs={{0,64},{64,128},{128,192},{192,256},{256,320},{320,384},{384,448},... | collective-permute-start | bytes 1609736 | tf_op jit(solution)/shard_map/ppermute | solution.py:80
  62.2 0.0 collective-permute-done.6
  62.2 1.9 %collective-permute-start.7 = (f32[256,540]{0,1:T(8,128)}, f32[256,540]{0,1:T(8,128)S(1)}, u32[]{:S(2)}, u32[]{:S(2)}) collective-permute-start(f32[256,540]{0,1:T(8,128)} %collective-permute-done.6), channel_id=1, source_target_pairs={{64,0},{128,64},{192,128},{256,192},{320,256},{384,320},{448,384},... | collective-permute-start | bytes 1658888 | tf_op jit(solution)/shard_map/ppermute | solution.py:75
  64.1 1.9 %fusion.93 = f32[256,536]{0,1:T(8,128)S(1)} fusion(f32[4,256,556]{1,2,0:T(8,128)S(1)} %pad_maximum_fusion, f32[256,540]{0,1:T(8,128)} %collective-permute-done.6, f32[256,538]{0,1:T(8,128)S(1)} %fusion.42, pred[]{:T(512)S(6)} %ge.14), kind=kLoop, calls=%fused_computation.203 | loop fusion | flops 3704832 | bytes 4947969 | tf_op jit(solution)/shard_map/add | solution.py:95
  66.0 0.8 fusion.89
  66.8 13.1 %collective-permute-done.7 = f32[256,540]{0,1:T(8,128)S(1)} collective-permute-done((f32[256,540]{0,1:T(8,128)}, f32[256,540]{0,1:T(8,128)S(1)}, u32[]{:S(2)}, u32[]{:S(2)}) %collective-permute-start.7) | collective-permute-done | bytes 552992 | tf_op jit(solution)/shard_map/ppermute | solution.py:75
  79.9 2.1 %collective-permute-start.8 = (f32[256,540]{0,1:T(8,128)S(1)}, f32[256,540]{0,1:T(8,128)S(1)}, u32[]{:S(2)}, u32[]{:S(2)}) collective-permute-start(f32[256,540]{0,1:T(8,128)S(1)} %collective-permute-done.7), channel_id=1, source_target_pairs={{64,0},{128,64},{192,128},{256,192},{320,256},{384,320},{448,384},... | collective-permute-start | bytes 1658888 | tf_op jit(solution)/shard_map/ppermute | solution.py:75
  82.0 0.8 fusion.86
  82.8 0.7 fusion.82
  83.6 13.1 %collective-permute-done.8 = f32[256,540]{0,1:T(8,128)S(1)} collective-permute-done((f32[256,540]{0,1:T(8,128)S(1)}, f32[256,540]{0,1:T(8,128)S(1)}, u32[]{:S(2)}, u32[]{:S(2)}) %collective-permute-start.8) | collective-permute-done | bytes 552992 | tf_op jit(solution)/shard_map/ppermute | solution.py:75
  96.7 0.8 fusion.127
  97.5 0.7 fusion.123
  98.2 0.7 fusion.120
  98.9 0.7 fusion.116
  99.7 1.8 %fusion.161 = f32[256,520]{0,1:T(8,128)S(1)} fusion(f32[4,256,556]{1,2,0:T(8,128)S(1)} %pad_maximum_fusion, f32[256,524]{0,1:T(8,128)} %collective-permute-done.3, f32[256,522]{0,1:T(8,128)S(1)} %fusion.116), kind=kLoop, calls=%fused_computation.314 | loop fusion | flops 3461120 | bytes 4800512 | tf_op jit(solution)/shard_map/add | solution.py:95
  101.5 0.7 fusion.157
  102.2 1.8 %fusion.154 = f32[256,516]{0,1:T(8,128)S(1)} fusion(f32[4,256,556]{1,2,0:T(8,128)S(1)} %pad_maximum_fusion, f32[256,524]{0,1:T(8,128)} %collective-permute-done.2, f32[256,518]{0,1:T(8,128)S(1)} %fusion.157), kind=kLoop, calls=%fused_computation.305 | loop fusion | flops 3434496 | bytes 4784128 | tf_op jit(solution)/shard_map/add | solution.py:95
  104.0 0.0 copy-start.1
  104.1 0.7 fusion.150
  104.8 0.3 copy-done.1
  105.1 0.2 copy-done.3
  105.3 0.7 fusion.182
  106.0 1.0 copy.14
  (17 shorter events, 0.2 us)
Async XLA Ops:
  0.0 2.6 %copy-start.5 = (f32[256,512]{1,0:T(8,128)S(1)}, f32[256,512]{1,0:T(8,128)}, u32[]{:S(2)}) copy-start(f32[256,512]{1,0:T(8,128)} %param.7) | copy-start | bytes 1572868
  0.0 2.8 %copy-start.6 = (f32[1,256,512]{2,1,0:T(8,128)S(1)}, f32[1,256,512]{2,1,0:T(8,128)}, u32[]{:S(2)}) copy-start(f32[1,256,512]{2,1,0:T(8,128)} %param.4) | copy-start | bytes 1572868
  2.8 6.2 %copy-start = (f32[256,512]{0,1:T(8,128)}, f32[256,512]{0,1:T(8,128)S(1)}, u32[]{:S(2)}) copy-start(f32[256,512]{0,1:T(8,128)S(1)} %copy.7) | copy-start | bytes 1572868
  3.0 6.0 %copy-start.4 = (f32[1,256,512]{1,2,0:T(8,128)}, f32[1,256,512]{1,2,0:T(8,128)S(1)}, u32[]{:S(2)}) copy-start(f32[1,256,512]{1,2,0:T(8,128)S(1)} %copy.8) | copy-start | bytes 1572868
  3.1 5.9 %collective-permute-start = (f32[4,256,22]{1,2,0:T(8,128)S(1)}, f32[4,256,22]{1,2,0:T(8,128)S(1)}, u32[]{:S(2)}, u32[]{:S(2)}) collective-permute-start(f32[4,256,22]{1,2,0:T(8,128)S(1)} %get-tuple-element.7), channel_id=1, source_target_pairs={{0,1},{1,2},{2,3},{3,4},{4,5},{5,6},{6,7},{7,8},{8,9},{9,10},{10,1... | collective-permute-start | bytes 270344 | tf_op jit(solution)/shard_map/ppermute | solution.py:16
  5.0 5.8 %collective-permute-start.1 = (f32[4,256,22]{1,2,0:T(8,128)S(1)}, f32[4,256,22]{1,2,0:T(8,128)S(1)}, u32[]{:S(2)}, u32[]{:S(2)}) collective-permute-start(f32[4,256,22]{1,2,0:T(8,128)S(1)} %get-tuple-element.8), channel_id=1, source_target_pairs={{1,0},{2,1},{3,2},{4,3},{5,4},{6,5},{7,6},{8,7},{9,8},{10,9},{11,1... | collective-permute-start | bytes 270344 | tf_op jit(solution)/shard_map/ppermute | solution.py:16
  19.6 2.4 %copy-start.2 = (f32[256,540]{0,1:T(8,128)}, f32[256,540]{0,1:T(8,128)S(1)}, u32[]{:S(2)}) copy-start(f32[256,540]{0,1:T(8,128)S(1)} %subtract_select_fusion) | copy-start | bytes 1658884
  19.6 17.1 %collective-permute-start.5 = (f32[256,540]{0,1:T(8,128)S(1)}, f32[256,540]{0,1:T(8,128)}, u32[]{:S(2)}, u32[]{:S(2)}) collective-permute-start(f32[256,540]{0,1:T(8,128)S(1)} %subtract_select_fusion), channel_id=1, source_target_pairs={{64,0},{128,64},{192,128},{256,192},{320,256},{384,320},{448,384},... | collective-permute-start | bytes 1658888 | tf_op jit(solution)/shard_map/ppermute | solution.py:75
  22.1 16.6 %collective-permute-start.2 = (f32[256,524]{0,1:T(8,128)S(1)}, f32[256,524]{0,1:T(8,128)}, u32[]{:S(2)}, u32[]{:S(2)}) collective-permute-start(f32[256,524]{0,1:T(8,128)S(1)} %slice.1081), channel_id=1, source_target_pairs={{0,64},{64,128},{128,192},{192,256},{256,320},{320,384},{384,448},... | collective-permute-start | bytes 1609736 | tf_op jit(solution)/shard_map/ppermute | solution.py:80
  36.7 25.5 %collective-permute-start.6 = (f32[256,540]{0,1:T(8,128)}, f32[256,540]{0,1:T(8,128)}, u32[]{:S(2)}, u32[]{:S(2)}) collective-permute-start(f32[256,540]{0,1:T(8,128)} %collective-permute-done.5), channel_id=1, source_target_pairs={{64,0},{128,64},{192,128},{256,192},{320,256},{384,320},{448,384},... | collective-permute-start | bytes 1658888 | tf_op jit(solution)/shard_map/ppermute | solution.py:75
  38.7 17.9 %collective-permute-start.3 = (f32[256,524]{0,1:T(8,128)}, f32[256,524]{0,1:T(8,128)}, u32[]{:S(2)}, u32[]{:S(2)}) collective-permute-start(f32[256,524]{0,1:T(8,128)} %collective-permute-done.2), channel_id=1, source_target_pairs={{0,64},{64,128},{128,192},{192,256},{256,320},{320,384},{384,448},... | collective-permute-start | bytes 1609736 | tf_op jit(solution)/shard_map/ppermute | solution.py:80
  56.6 41.6 %collective-permute-start.4 = (f32[256,524]{0,1:T(8,128)}, f32[256,524]{0,1:T(8,128)S(1)}, u32[]{:S(2)}, u32[]{:S(2)}) collective-permute-start(f32[256,524]{0,1:T(8,128)} %collective-permute-done.3), channel_id=1, source_target_pairs={{0,64},{64,128},{128,192},{192,256},{256,320},{320,384},{384,448},... | collective-permute-start | bytes 1609736 | tf_op jit(solution)/shard_map/ppermute | solution.py:80
  62.2 17.7 %collective-permute-start.7 = (f32[256,540]{0,1:T(8,128)}, f32[256,540]{0,1:T(8,128)S(1)}, u32[]{:S(2)}, u32[]{:S(2)}) collective-permute-start(f32[256,540]{0,1:T(8,128)} %collective-permute-done.6), channel_id=1, source_target_pairs={{64,0},{128,64},{192,128},{256,192},{320,256},{384,320},{448,384},... | collective-permute-start | bytes 1658888 | tf_op jit(solution)/shard_map/ppermute | solution.py:75
  79.9 16.8 %collective-permute-start.8 = (f32[256,540]{0,1:T(8,128)S(1)}, f32[256,540]{0,1:T(8,128)S(1)}, u32[]{:S(2)}, u32[]{:S(2)}) collective-permute-start(f32[256,540]{0,1:T(8,128)S(1)} %collective-permute-done.7), channel_id=1, source_target_pairs={{64,0},{128,64},{192,128},{256,192},{320,256},{384,320},{448,384},... | collective-permute-start | bytes 1658888 | tf_op jit(solution)/shard_map/ppermute | solution.py:75
  104.0 1.0 copy-start.1
  104.0 1.2 %copy-start.3 = (f32[256,540]{0,1:T(8,128)S(1)}, f32[256,540]{0,1:T(8,128)}, u32[]{:S(2)}) copy-start(f32[256,540]{0,1:T(8,128)} %copy-done.2) | copy-start | bytes 1658884

commit v7 on v6

--- a/solution.py
+++ b/solution.py
@@ -70,15 +70,17 @@
     ahead = slices // 2
     behind = slices - 1 - ahead
     got = {slices - 1: carried}
+    wide_f = CSTEPS * behind
     block = carried
+    ahead_blk = carried[:, chain - wide_f: chain + n + wide_f]
     for r in range(1, ahead + 1):
         block = lax.ppermute(block, "tm", back)
         got[r - 1] = block
-    wide_f = CSTEPS * behind
-    block = carried[:, chain - wide_f: chain + n + wide_f]
-    for r in range(1, behind + 1):
-        block = lax.ppermute(block, "tm", ring)
-        got[slices - 1 - r] = block
+        if r <= behind:
+            if r == behind:
+                ahead_blk, got[r - 1] = lax.optimization_barrier((ahead_blk, block))
+            ahead_blk = lax.ppermute(ahead_blk, "tm", ring)
+            got[slices - 1 - r] = ahead_blk
 
     def part(j, h):
         blk = got[j]

time: 108 us -> 103 us (0.954)
  the two profiles are of different devices: /device:TPU:156 before, /device:TPU:504 now
where the time goes in v7:
time: 103 us; the launch traced here: 102 us
  waiting for transfers between devices  52 us (50%)
  other arithmetic  22.5 us (22%)
  starting transfers between devices  21.3 us (21%)
  local copies, waits for them, and re-layouts  5.36 us (5%)
    ppermute x4, waiting for transfers between devices, local(): block = lax.ppermute(block, 'tm', back)  48.8 us
    ppermute x4, starting transfers between devices, local(): block = lax.ppermute(block, 'tm', back)  11.8 us
    add x14, other arithmetic, advance(): return mid - size * moved + size * coef[2] * spread  11.2 us
    add x6, other arithmetic, local(): current = part(turn, h) + moved  6.83 us
    ppermute x2, starting transfers between devices, shifted(): return lax.ppermute(block, axis, route)  5.56 us
    ppermute x3, starting transfers between devices, local(): ahead_blk = lax.ppermute(ahead_blk, 'tm', ring)  4.02 us
    unnamed x18, local copies, waits for them, and re-layouts  3.45 us
    ppermute x2, waiting for transfers between devices, shifted(): return lax.ppermute(block, axis, route)  2.18 us
  transfers between devices with their start and end apart: 9, of which 7 were waited for; matrix products, arithmetic and copies ran while one was open for 8% of the time, Pallas kernels for 0%

profile of v7, /device:TPU:504, one launch (start us, length us, event | category | flops | bytes accessed | tf_op | source)
XLA Modules:
  0.0 101.5 jit_solution(10668958961904746192)
XLA Ops:
  0.0 1.3 %copy.5 = f32[256,512]{0,1:T(8,128)S(1)} copy(f32[256,512]{1,0:T(8,128)} %param.5) | data formatting | bytes 1048576 | tf_op args[1]
  1.3 1.2 %copy.6 = f32[256,512]{0,1:T(8,128)S(1)} copy(f32[256,512]{1,0:T(8,128)} %param.6) | data formatting | bytes 1048576 | tf_op args[2]
  2.6 0.2 copy.7
  2.8 0.2 copy.8
  3.1 1.9 %collective-permute-start = (f32[4,256,22]{1,2,0:T(8,128)S(1)}, f32[4,256,22]{1,2,0:T(8,128)S(1)}, u32[]{:S(2)}, u32[]{:S(2)}) collective-permute-start(f32[4,256,22]{1,2,0:T(8,128)S(1)} %get-tuple-element.11), channel_id=1, source_target_pairs={{0,1},{1,2},{2,3},{3,4},{4,5},{5,6},{6,7},{7,8},{8,9},{9,10},{10,1... | collective-permute-start | bytes 270344 | tf_op jit(solution)/shard_map/ppermute | solution.py:16
  5.0 3.6 %collective-permute-start.1 = (f32[4,256,22]{1,2,0:T(8,128)S(1)}, f32[4,256,22]{1,2,0:T(8,128)S(1)}, u32[]{:S(2)}, u32[]{:S(2)}) collective-permute-start(f32[4,256,22]{1,2,0:T(8,128)S(1)} %get-tuple-element.12), channel_id=1, source_target_pairs={{1,0},{2,1},{3,2},{4,3},{5,4},{6,5},{7,6},{8,7},{9,8},{10,9},{11,1... | collective-permute-start | bytes 270344 | tf_op jit(solution)/shard_map/ppermute | solution.py:16
  8.6 0.3 collective-permute-done
  9.0 1.8 %collective-permute-done.1 = f32[4,256,22]{1,2,0:T(8,128)S(1)} collective-permute-done((f32[4,256,22]{1,2,0:T(8,128)S(1)}, f32[4,256,22]{1,2,0:T(8,128)S(1)}, u32[]{:S(2)}, u32[]{:S(2)}) %collective-permute-start.1) | collective-permute-done | bytes 90144 | tf_op jit(solution)/shard_map/ppermute | solution.py:16
  10.8 1.4 %pad_maximum_fusion = f32[4,256,556]{1,2,0:T(8,128)S(1)} fusion(f32[4,256,22]{1,2,0:T(8,128)S(1)} %collective-permute-done.1, f32[1,256,512]{1,2,0:T(8,128)} %bitcast.748, f32[1,256,512]{1,2,0:T(8,128)S(1)} %bitcast.746, f32[1,256,512]{1,2,0:T(8,128)S(1)} %bitcast.744, f32[1,256,512]{1,2,0:T(8,128)} %copy-done.4, f32[4,256,22]{1,2,0:T(8,128)S(1)} %collective-permute-done), kind=kLoop, calls=%fused_computation | loop fusion | flops 2846720 | bytes 4554752 | tf_op jit(solution)/shard_map/concatenate | solution.py:24
  12.3 0.8 fusion.2
  13.1 0.8 fusion.19
  13.9 0.8 fusion.16
  14.7 0.8 fusion.13
  15.5 0.8 fusion.10
  16.2 0.8 fusion.45
  17.0 1.3 %fusion.64 = (f32[256,542]{0,1:T(8,128)S(1)}, f32[256,542]{0,1:T(8,128)S(1)}) fusion(f32[256,544]{0,1:T(8,128)S(1)} %fusion.45, f32[4,256,556]{1,2,0:T(8,128)S(1)} %pad_maximum_fusion, f32[256,544]{0,1:T(8,128)S(1)} %slice.1076, f32[256,556]{0,1:T(8,128)S(1)} %slice_bitcast_fusion), kind=kLoop, calls=%fused_computation.158 | loop fusion | flops 6382592 | bytes 7237632 | tf_op jit(solution)/shard_map/add | solution.py:41
  18.3 1.3 %subtract_select_fusion = f32[256,540]{0,1:T(8,128)S(1)} fusion(f32[256,542]{0,1:T(8,128)S(1)} %get-tuple-element.10, f32[4,256,556]{1,2,0:T(8,128)S(1)} %pad_maximum_fusion, f32[256,542]{0,1:T(8,128)S(1)} %get-tuple-element.9, pred[]{:T(512)S(6)} %eq.3), kind=kLoop, calls=%fused_computation.49 | loop fusion | flops 6635520 | bytes 6680577 | tf_op jit(solution)/shard_map/jit(_where)/select_n | solution.py:67
  19.6 3.3 %collective-permute-start.4 = (f32[256,540]{0,1:T(8,128)S(1)}, f32[256,540]{0,1:T(8,128)}, u32[]{:S(2)}, u32[]{:S(2)}) collective-permute-start(f32[256,540]{0,1:T(8,128)S(1)} %subtract_select_fusion), channel_id=1, source_target_pairs={{64,0},{128,64},{192,128},{256,192},{320,256},{384,320},{448,384},... | collective-permute-start | bytes 1658888 | tf_op jit(solution)/shard_map/ppermute | solution.py:77
  22.9 0.8 slice.1081
  23.7 1.3 %collective-permute-start.2 = (f32[256,524]{0,1:T(8,128)}, f32[256,524]{0,1:T(8,128)}, u32[]{:S(2)}, u32[]{:S(2)}) collective-permute-start(f32[256,524]{0,1:T(8,128)} %slice.1081), channel_id=1, source_target_pairs={{0,64},{64,128},{128,192},{192,256},{256,320},{320,384},{384,448},... | collective-permute-start | bytes 1609736 | tf_op jit(solution)/shard_map/ppermute | solution.py:82
  25.0 12.2 %collective-permute-done.4 = f32[256,540]{0,1:T(8,128)} collective-permute-done((f32[256,540]{0,1:T(8,128)S(1)}, f32[256,540]{0,1:T(8,128)}, u32[]{:S(2)}, u32[]{:S(2)}) %collective-permute-start.4) | collective-permute-done | bytes 552992 | tf_op jit(solution)/shard_map/ppermute | solution.py:77
  37.3 2.0 %collective-permute-start.5 = (f32[256,540]{0,1:T(8,128)}, f32[256,540]{0,1:T(8,128)}, u32[]{:S(2)}, u32[]{:S(2)}) collective-permute-start(f32[256,540]{0,1:T(8,128)} %collective-permute-done.4), channel_id=1, source_target_pairs={{64,0},{128,64},{192,128},{256,192},{320,256},{384,320},{448,384},... | collective-permute-start | bytes 1658888 | tf_op jit(solution)/shard_map/ppermute | solution.py:77
  39.3 1.0 collective-permute-done.2
  40.3 1.3 %collective-permute-start.3 = (f32[256,524]{0,1:T(8,128)}, f32[256,524]{0,1:T(8,128)S(1)}, u32[]{:S(2)}, u32[]{:S(2)}) collective-permute-start(f32[256,524]{0,1:T(8,128)} %collective-permute-done.2), channel_id=1, source_target_pairs={{0,64},{64,128},{128,192},{192,256},{256,320},{320,384},{384,448},... | collective-permute-start | bytes 1609736 | tf_op jit(solution)/shard_map/ppermute | solution.py:82
  41.6 1.1 %broadcast_select_fusion = f32[256,540]{0,1:T(8,128)S(1)} fusion(f32[256,540]{0,1:T(8,128)} %collective-permute-done.4, pred[]{:T(512)S(6)} %ge.15), kind=kLoop, calls=%fused_computation.356 | loop fusion | flops 138240 | bytes 1105921 | tf_op jit(solution)/shard_map/jit(_where)/select_n | solution.py:91
  42.7 0.8 fusion.42
  43.5 12.6 %collective-permute-done.5 = f32[256,540]{0,1:T(8,128)} collective-permute-done((f32[256,540]{0,1:T(8,128)}, f32[256,540]{0,1:T(8,128)}, u32[]{:S(2)}, u32[]{:S(2)}) %collective-permute-start.5) | collective-permute-done | bytes 552992 | tf_op jit(solution)/shard_map/ppermute | solution.py:77
  56.1 1.9 %collective-permute-start.6 = (f32[256,540]{0,1:T(8,128)}, f32[256,540]{0,1:T(8,128)S(1)}, u32[]{:S(2)}, u32[]{:S(2)}) collective-permute-start(f32[256,540]{0,1:T(8,128)} %collective-permute-done.5), channel_id=1, source_target_pairs={{64,0},{128,64},{192,128},{256,192},{320,256},{384,320},{448,384},... | collective-permute-start | bytes 1658888 | tf_op jit(solution)/shard_map/ppermute | solution.py:77
  58.0 1.9 %fusion.93 = f32[256,536]{0,1:T(8,128)S(1)} fusion(f32[4,256,556]{1,2,0:T(8,128)S(1)} %pad_maximum_fusion, f32[256,540]{0,1:T(8,128)} %collective-permute-done.5, f32[256,538]{0,1:T(8,128)S(1)} %fusion.42, pred[]{:T(512)S(6)} %ge.14), kind=kLoop, calls=%fused_computation.203 | loop fusion | flops 3704832 | bytes 4947969 | tf_op jit(solution)/shard_map/add | solution.py:97
  59.9 0.8 fusion.89
  60.7 13.3 %collective-permute-done.6 = f32[256,540]{0,1:T(8,128)S(1)} collective-permute-done((f32[256,540]{0,1:T(8,128)}, f32[256,540]{0,1:T(8,128)S(1)}, u32[]{:S(2)}, u32[]{:S(2)}) %collective-permute-start.6) | collective-permute-done | bytes 552992 | tf_op jit(solution)/shard_map/ppermute | solution.py:77
  74.0 1.5 %collective-permute-start.7 = (f32[256,524]{0,1:T(8,128)S(1)}, f32[256,524]{0,1:T(8,128)S(1)}, u32[]{:S(2)}, u32[]{:S(2)}) collective-permute-start(f32[256,524]{0,1:T(8,128)S(1)} %collective-permute-done.3), channel_id=1, source_target_pairs={{0,64},{64,128},{128,192},{192,256},{256,320},{320,384},{384,448},... | collective-permute-start | bytes 1609736 | tf_op jit(solution)/shard_map/ppermute | solution.py:82
  75.4 4.6 %collective-permute-start.8 = (f32[256,540]{0,1:T(8,128)S(1)}, f32[256,540]{0,1:T(8,128)S(1)}, u32[]{:S(2)}, u32[]{:S(2)}) collective-permute-start(f32[256,540]{0,1:T(8,128)S(1)} %collective-permute-done.6), channel_id=1, source_target_pairs={{64,0},{128,64},{192,128},{256,192},{320,256},{384,320},{448,384},... | collective-permute-start | bytes 1658888 | tf_op jit(solution)/shard_map/ppermute | solution.py:77
  80.0 0.8 fusion.86
  80.8 0.7 fusion.82
  81.6 10.7 %collective-permute-done.8 = f32[256,540]{0,1:T(8,128)S(1)} collective-permute-done((f32[256,540]{0,1:T(8,128)S(1)}, f32[256,540]{0,1:T(8,128)S(1)}, u32[]{:S(2)}, u32[]{:S(2)}) %collective-permute-start.8) | collective-permute-done | bytes 552992 | tf_op jit(solution)/shard_map/ppermute | solution.py:77
  92.3 0.8 fusion.127
  93.1 0.7 fusion.123
  93.8 0.7 fusion.120
  94.5 0.7 fusion.116
  95.2 0.8 fusion.161
  96.0 0.7 fusion.157
  96.8 1.8 %fusion.154 = f32[256,516]{0,1:T(8,128)S(1)} fusion(f32[4,256,556]{1,2,0:T(8,128)S(1)} %pad_maximum_fusion, f32[256,524]{0,1:T(8,128)} %collective-permute-done.2, f32[256,518]{0,1:T(8,128)S(1)} %fusion.157), kind=kLoop, calls=%fused_computation.304 | loop fusion | flops 3434496 | bytes 4784128 | tf_op jit(solution)/shard_map/add | solution.py:97
  98.6 0.7 fusion.150
  99.3 0.3 copy-done.1
  99.6 0.2 copy-done.3
  99.8 0.7 fusion.182
  100.5 1.0 copy.14
  (17 shorter events, 0.1 us)
Async XLA Ops:
  0.0 2.6 %copy-start.5 = (f32[256,512]{1,0:T(8,128)S(1)}, f32[256,512]{1,0:T(8,128)}, u32[]{:S(2)}) copy-start(f32[256,512]{1,0:T(8,128)} %param.7) | copy-start | bytes 1572868
  0.0 2.8 %copy-start.6 = (f32[1,256,512]{2,1,0:T(8,128)S(1)}, f32[1,256,512]{2,1,0:T(8,128)}, u32[]{:S(2)}) copy-start(f32[1,256,512]{2,1,0:T(8,128)} %param.4) | copy-start | bytes 1572868
  2.8 6.2 %copy-start = (f32[256,512]{0,1:T(8,128)}, f32[256,512]{0,1:T(8,128)S(1)}, u32[]{:S(2)}) copy-start(f32[256,512]{0,1:T(8,128)S(1)} %copy.7) | copy-start | bytes 1572868
  3.0 6.0 %copy-start.4 = (f32[1,256,512]{1,2,0:T(8,128)}, f32[1,256,512]{1,2,0:T(8,128)S(1)}, u32[]{:S(2)}) copy-start(f32[1,256,512]{1,2,0:T(8,128)S(1)} %copy.8) | copy-start | bytes 1572868
  3.1 5.9 %collective-permute-start = (f32[4,256,22]{1,2,0:T(8,128)S(1)}, f32[4,256,22]{1,2,0:T(8,128)S(1)}, u32[]{:S(2)}, u32[]{:S(2)}) collective-permute-start(f32[4,256,22]{1,2,0:T(8,128)S(1)} %get-tuple-element.11), channel_id=1, source_target_pairs={{0,1},{1,2},{2,3},{3,4},{4,5},{5,6},{6,7},{7,8},{8,9},{9,10},{10,1... | collective-permute-start | bytes 270344 | tf_op jit(solution)/shard_map/ppermute | solution.py:16
  5.0 5.8 %collective-permute-start.1 = (f32[4,256,22]{1,2,0:T(8,128)S(1)}, f32[4,256,22]{1,2,0:T(8,128)S(1)}, u32[]{:S(2)}, u32[]{:S(2)}) collective-permute-start(f32[4,256,22]{1,2,0:T(8,128)S(1)} %get-tuple-element.12), channel_id=1, source_target_pairs={{1,0},{2,1},{3,2},{4,3},{5,4},{6,5},{7,6},{8,7},{9,8},{10,9},{11,1... | collective-permute-start | bytes 270344 | tf_op jit(solution)/shard_map/ppermute | solution.py:16
  19.6 3.3 %copy-start.2 = (f32[256,540]{0,1:T(8,128)}, f32[256,540]{0,1:T(8,128)S(1)}, u32[]{:S(2)}) copy-start(f32[256,540]{0,1:T(8,128)S(1)} %subtract_select_fusion) | copy-start | bytes 1658884
  19.6 17.6 %collective-permute-start.4 = (f32[256,540]{0,1:T(8,128)S(1)}, f32[256,540]{0,1:T(8,128)}, u32[]{:S(2)}, u32[]{:S(2)}) collective-permute-start(f32[256,540]{0,1:T(8,128)S(1)} %subtract_select_fusion), channel_id=1, source_target_pairs={{64,0},{128,64},{192,128},{256,192},{320,256},{384,320},{448,384},... | collective-permute-start | bytes 1658888 | tf_op jit(solution)/shard_map/ppermute | solution.py:77
  23.7 16.6 %collective-permute-start.2 = (f32[256,524]{0,1:T(8,128)}, f32[256,524]{0,1:T(8,128)}, u32[]{:S(2)}, u32[]{:S(2)}) collective-permute-start(f32[256,524]{0,1:T(8,128)} %slice.1081), channel_id=1, source_target_pairs={{0,64},{64,128},{128,192},{192,256},{256,320},{320,384},{384,448},... | collective-permute-start | bytes 1609736 | tf_op jit(solution)/shard_map/ppermute | solution.py:82
  37.3 18.8 %collective-permute-start.5 = (f32[256,540]{0,1:T(8,128)}, f32[256,540]{0,1:T(8,128)}, u32[]{:S(2)}, u32[]{:S(2)}) collective-permute-start(f32[256,540]{0,1:T(8,128)} %collective-permute-done.4), channel_id=1, source_target_pairs={{64,0},{128,64},{192,128},{256,192},{320,256},{384,320},{448,384},... | collective-permute-start | bytes 1658888 | tf_op jit(solution)/shard_map/ppermute | solution.py:77
  40.3 20.4 %collective-permute-start.3 = (f32[256,524]{0,1:T(8,128)}, f32[256,524]{0,1:T(8,128)S(1)}, u32[]{:S(2)}, u32[]{:S(2)}) collective-permute-start(f32[256,524]{0,1:T(8,128)} %collective-permute-done.2), channel_id=1, source_target_pairs={{0,64},{64,128},{128,192},{192,256},{256,320},{320,384},{384,448},... | collective-permute-start | bytes 1609736 | tf_op jit(solution)/shard_map/ppermute | solution.py:82
  56.1 17.9 %collective-permute-start.6 = (f32[256,540]{0,1:T(8,128)}, f32[256,540]{0,1:T(8,128)S(1)}, u32[]{:S(2)}, u32[]{:S(2)}) collective-permute-start(f32[256,540]{0,1:T(8,128)} %collective-permute-done.5), channel_id=1, source_target_pairs={{64,0},{128,64},{192,128},{256,192},{320,256},{384,320},{448,384},... | collective-permute-start | bytes 1658888 | tf_op jit(solution)/shard_map/ppermute | solution.py:77
  74.0 19.8 %collective-permute-start.7 = (f32[256,524]{0,1:T(8,128)S(1)}, f32[256,524]{0,1:T(8,128)S(1)}, u32[]{:S(2)}, u32[]{:S(2)}) collective-permute-start(f32[256,524]{0,1:T(8,128)S(1)} %collective-permute-done.3), channel_id=1, source_target_pairs={{0,64},{64,128},{128,192},{192,256},{256,320},{320,384},{384,448},... | collective-permute-start | bytes 1609736 | tf_op jit(solution)/shard_map/ppermute | solution.py:82
  75.4 16.8 %collective-permute-start.8 = (f32[256,540]{0,1:T(8,128)S(1)}, f32[256,540]{0,1:T(8,128)S(1)}, u32[]{:S(2)}, u32[]{:S(2)}) collective-permute-start(f32[256,540]{0,1:T(8,128)S(1)} %collective-permute-done.6), channel_id=1, source_target_pairs={{64,0},{128,64},{192,128},{256,192},{320,256},{384,320},{448,384},... | collective-permute-start | bytes 1658888 | tf_op jit(solution)/shard_map/ppermute | solution.py:77
  98.6 1.0 %copy-start.1 = (f32[256,512]{0,1:T(8,128)S(1)}, f32[256,512]{0,1:T(8,128)}, u32[]{:S(2)}) copy-start(f32[256,512]{0,1:T(8,128)} %copy-done) | copy-start | bytes 1572868
  98.6 1.2 %copy-start.3 = (f32[256,540]{0,1:T(8,128)S(1)}, f32[256,540]{0,1:T(8,128)}, u32[]{:S(2)}) copy-start(f32[256,540]{0,1:T(8,128)} %copy-done.2) | copy-start | bytes 1658884

commit v8 on v6

--- a/solution.py
+++ b/solution.py
@@ -70,21 +70,21 @@
     ahead = slices // 2
     behind = slices - 1 - ahead
     got = {slices - 1: carried}
-    block = carried
+    wide_f = CSTEPS * ahead
+    block = carried[:, chain - wide_f: chain + n + wide_f]
+    late = carried
     for r in range(1, ahead + 1):
-        block = lax.ppermute(block, "tm", back)
-        got[r - 1] = block
-    wide_f = CSTEPS * behind
-    block = carried[:, chain - wide_f: chain + n + wide_f]
-    for r in range(1, behind + 1):
         block = lax.ppermute(block, "tm", ring)
         got[slices - 1 - r] = block
+        if r <= behind:
+            late = lax.ppermute(late, "tm", back)
+            got[r - 1] = late
 
     def part(j, h):
         blk = got[j]
         extra = (blk.shape[-1] - n) // 2 - h
         blk = blk[:, extra: extra + n + 2 * h]
-        if j >= ahead:
+        if j >= behind:
             return blk
         return jnp.where(me >= slices - 1 - j, blk, jnp.zeros_like(blk))
 

time: 108 us -> 103 us (0.954)
  the two profiles are of different devices: /device:TPU:156 before, /device:TPU:166 now
where the time goes in v8:
time: 103 us; the launch traced here: 102 us
  waiting for transfers between devices  48.3 us (47%)
  starting transfers between devices  26.4 us (26%)
  other arithmetic  22.5 us (22%)
  local copies, waits for them, and re-layouts  4.56 us (4%)
    ppermute x4, waiting for transfers between devices, local(): block = lax.ppermute(block, 'tm', ring)  36.2 us
    add x14, other arithmetic, advance(): return mid - size * moved + size * coef[2] * spread  11.2 us
    ppermute x3, starting transfers between devices, local(): late = lax.ppermute(late, 'tm', back)  11 us
    ppermute x3, waiting for transfers between devices, local(): late = lax.ppermute(late, 'tm', back)  9.99 us
    ppermute x4, starting transfers between devices, local(): block = lax.ppermute(block, 'tm', ring)  9.76 us
    add x6, other arithmetic, local(): current = part(turn, h) + moved  7.83 us
    ppermute x2, starting transfers between devices, shifted(): return lax.ppermute(block, axis, route)  5.56 us
    unnamed x18, local copies, waits for them, and re-layouts  3.45 us
  transfers between devices with their start and end apart: 9, of which 6 were waited for; matrix products, arithmetic and copies ran while one was open for 5% of the time, Pallas kernels for 0%

profile of v8, /device:TPU:166, one launch (start us, length us, event | category | flops | bytes accessed | tf_op | source)
XLA Modules:
  0.0 102.1 jit_solution(10304579481041854804)
XLA Ops:
  0.0 1.3 %copy.5 = f32[256,512]{0,1:T(8,128)S(1)} copy(f32[256,512]{1,0:T(8,128)} %param.5) | data formatting | bytes 1048576 | tf_op args[1]
  1.3 1.2 %copy.6 = f32[256,512]{0,1:T(8,128)S(1)} copy(f32[256,512]{1,0:T(8,128)} %param.6) | data formatting | bytes 1048576 | tf_op args[2]
  2.6 0.2 copy.7
  2.8 0.0 copy-start
  2.8 0.2 copy.8
  3.1 1.9 %collective-permute-start = (f32[4,256,22]{1,2,0:T(8,128)S(1)}, f32[4,256,22]{1,2,0:T(8,128)S(1)}, u32[]{:S(2)}, u32[]{:S(2)}) collective-permute-start(f32[4,256,22]{1,2,0:T(8,128)S(1)} %get-tuple-element.7), channel_id=1, source_target_pairs={{0,1},{1,2},{2,3},{3,4},{4,5},{5,6},{6,7},{7,8},{8,9},{9,10},{10,1... | collective-permute-start | bytes 270344 | tf_op jit(solution)/shard_map/ppermute | solution.py:16
  5.0 3.6 %collective-permute-start.1 = (f32[4,256,22]{1,2,0:T(8,128)S(1)}, f32[4,256,22]{1,2,0:T(8,128)S(1)}, u32[]{:S(2)}, u32[]{:S(2)}) collective-permute-start(f32[4,256,22]{1,2,0:T(8,128)S(1)} %get-tuple-element.8), channel_id=1, source_target_pairs={{1,0},{2,1},{3,2},{4,3},{5,4},{6,5},{7,6},{8,7},{9,8},{10,9},{11,1... | collective-permute-start | bytes 270344 | tf_op jit(solution)/shard_map/ppermute | solution.py:16
  8.6 0.3 collective-permute-done
  9.0 1.8 %collective-permute-done.1 = f32[4,256,22]{1,2,0:T(8,128)S(1)} collective-permute-done((f32[4,256,22]{1,2,0:T(8,128)S(1)}, f32[4,256,22]{1,2,0:T(8,128)S(1)}, u32[]{:S(2)}, u32[]{:S(2)}) %collective-permute-start.1) | collective-permute-done | bytes 90144 | tf_op jit(solution)/shard_map/ppermute | solution.py:16
  10.8 1.4 %pad_maximum_fusion = f32[4,256,556]{1,2,0:T(8,128)S(1)} fusion(f32[4,256,22]{1,2,0:T(8,128)S(1)} %collective-permute-done.1, f32[1,256,512]{1,2,0:T(8,128)} %bitcast.748, f32[1,256,512]{1,2,0:T(8,128)S(1)} %bitcast.746, f32[1,256,512]{1,2,0:T(8,128)S(1)} %bitcast.744, f32[1,256,512]{1,2,0:T(8,128)} %copy-done.4, f32[4,256,22]{1,2,0:T(8,128)S(1)} %collective-permute-done), kind=kLoop, calls=%fused_computation | loop fusion | flops 2846720 | bytes 4554752 | tf_op jit(solution)/shard_map/concatenate | solution.py:24
  12.3 0.8 fusion.2
  13.1 0.8 fusion.19
  13.9 0.8 fusion.16
  14.7 0.8 fusion.13
  15.5 0.8 fusion.10
  16.2 0.8 fusion.45
  17.0 1.3 %fusion.64 = (f32[256,542]{0,1:T(8,128)S(1)}, f32[256,542]{0,1:T(8,128)S(1)}) fusion(f32[256,544]{0,1:T(8,128)S(1)} %fusion.45, f32[4,256,556]{1,2,0:T(8,128)S(1)} %pad_maximum_fusion, f32[256,544]{0,1:T(8,128)S(1)} %slice.1076, f32[256,556]{0,1:T(8,128)S(1)} %slice_bitcast_fusion), kind=kLoop, calls=%fused_computation.158 | loop fusion | flops 6382592 | bytes 7237632 | tf_op jit(solution)/shard_map/add | solution.py:41
  18.3 1.3 %subtract_select_fusion = f32[256,540]{0,1:T(8,128)S(1)} fusion(f32[256,542]{0,1:T(8,128)S(1)} %get-tuple-element.6, f32[4,256,556]{1,2,0:T(8,128)S(1)} %pad_maximum_fusion, f32[256,542]{0,1:T(8,128)S(1)} %get-tuple-element.5, pred[]{:T(512)S(6)} %eq.3), kind=kLoop, calls=%fused_computation.49 | loop fusion | flops 6635520 | bytes 6680577 | tf_op jit(solution)/shard_map/jit(_where)/select_n | solution.py:67
  19.6 2.4 %collective-permute-start.6 = (f32[256,540]{0,1:T(8,128)S(1)}, f32[256,540]{0,1:T(8,128)}, u32[]{:S(2)}, u32[]{:S(2)}) collective-permute-start(f32[256,540]{0,1:T(8,128)S(1)} %subtract_select_fusion), channel_id=1, source_target_pairs={{64,0},{128,64},{192,128},{256,192},{320,256},{384,320},{448,384},... | collective-permute-start | bytes 1658888 | tf_op jit(solution)/shard_map/ppermute | solution.py:80
  22.1 3.5 %collective-permute-start.2 = (f32[256,528]{0,1:T(8,128)S(1)}, f32[256,528]{0,1:T(8,128)}, u32[]{:S(2)}, u32[]{:S(2)}) collective-permute-start(f32[256,528]{0,1:T(8,128)S(1)} %slice.1081), channel_id=1, source_target_pairs={{0,64},{64,128},{128,192},{192,256},{256,320},{320,384},{384,448},... | collective-permute-start | bytes 1622024 | tf_op jit(solution)/shard_map/ppermute | solution.py:77
  25.6 10.0 %collective-permute-done.6 = f32[256,540]{0,1:T(8,128)} collective-permute-done((f32[256,540]{0,1:T(8,128)S(1)}, f32[256,540]{0,1:T(8,128)}, u32[]{:S(2)}, u32[]{:S(2)}) %collective-permute-start.6) | collective-permute-done | bytes 552992 | tf_op jit(solution)/shard_map/ppermute | solution.py:80
  35.5 3.6 %collective-permute-start.7 = (f32[256,540]{0,1:T(8,128)}, f32[256,540]{0,1:T(8,128)}, u32[]{:S(2)}, u32[]{:S(2)}) collective-permute-start(f32[256,540]{0,1:T(8,128)} %collective-permute-done.6), channel_id=1, source_target_pairs={{64,0},{128,64},{192,128},{256,192},{320,256},{384,320},{448,384},... | collective-permute-start | bytes 1658888 | tf_op jit(solution)/shard_map/ppermute | solution.py:80
  39.1 2.3 %collective-permute-start.3 = (f32[256,528]{0,1:T(8,128)}, f32[256,528]{0,1:T(8,128)}, u32[]{:S(2)}, u32[]{:S(2)}) collective-permute-start(f32[256,528]{0,1:T(8,128)} %collective-permute-done.2), channel_id=1, source_target_pairs={{0,64},{64,128},{128,192},{192,256},{256,320},{320,384},{384,448},... | collective-permute-start | bytes 1622024 | tf_op jit(solution)/shard_map/ppermute | solution.py:77
  41.5 0.8 fusion.42
  42.2 15.3 %collective-permute-done.3 = f32[256,528]{0,1:T(8,128)} collective-permute-done((f32[256,528]{0,1:T(8,128)}, f32[256,528]{0,1:T(8,128)}, u32[]{:S(2)}, u32[]{:S(2)}) %collective-permute-start.3) | collective-permute-done | bytes 540704 | tf_op jit(solution)/shard_map/ppermute | solution.py:77
  57.5 1.9 %collective-permute-start.4 = (f32[256,528]{0,1:T(8,128)}, f32[256,528]{0,1:T(8,128)S(1)}, u32[]{:S(2)}, u32[]{:S(2)}) collective-permute-start(f32[256,528]{0,1:T(8,128)} %collective-permute-done.3), channel_id=1, source_target_pairs={{0,64},{64,128},{128,192},{192,256},{256,320},{320,384},{384,448},... | collective-permute-start | bytes 1622024 | tf_op jit(solution)/shard_map/ppermute | solution.py:77
  59.4 0.0 collective-permute-done.7
  59.4 5.1 %collective-permute-start.8 = (f32[256,540]{0,1:T(8,128)}, f32[256,540]{0,1:T(8,128)S(1)}, u32[]{:S(2)}, u32[]{:S(2)}) collective-permute-start(f32[256,540]{0,1:T(8,128)} %collective-permute-done.7), channel_id=1, source_target_pairs={{64,0},{128,64},{192,128},{256,192},{320,256},{384,320},{448,384},... | collective-permute-start | bytes 1658888 | tf_op jit(solution)/shard_map/ppermute | solution.py:80
  64.6 1.9 %fusion.93 = f32[256,536]{0,1:T(8,128)S(1)} fusion(f32[4,256,556]{1,2,0:T(8,128)S(1)} %pad_maximum_fusion, f32[256,540]{0,1:T(8,128)} %collective-permute-done.7, f32[256,538]{0,1:T(8,128)S(1)} %fusion.42, pred[]{:T(512)S(6)} %ge.10), kind=kLoop, calls=%fused_computation.203 | loop fusion | flops 3704832 | bytes 4947969 | tf_op jit(solution)/shard_map/add | solution.py:95
  66.5 0.8 fusion.89
  67.2 7.9 %collective-permute-done.4 = f32[256,528]{0,1:T(8,128)S(1)} collective-permute-done((f32[256,528]{0,1:T(8,128)}, f32[256,528]{0,1:T(8,128)S(1)}, u32[]{:S(2)}, u32[]{:S(2)}) %collective-permute-start.4) | collective-permute-done | bytes 540704 | tf_op jit(solution)/shard_map/ppermute | solution.py:77
  75.1 2.1 %collective-permute-start.5 = (f32[256,528]{0,1:T(8,128)S(1)}, f32[256,528]{0,1:T(8,128)S(1)}, u32[]{:S(2)}, u32[]{:S(2)}) collective-permute-start(f32[256,528]{0,1:T(8,128)S(1)} %collective-permute-done.4), channel_id=1, source_target_pairs={{0,64},{64,128},{128,192},{192,256},{256,320},{320,384},{384,448},... | collective-permute-start | bytes 1622024 | tf_op jit(solution)/shard_map/ppermute | solution.py:77
  77.2 0.8 fusion.86
  78.0 0.7 fusion.82
  78.8 13.0 %collective-permute-done.5 = f32[256,528]{0,1:T(8,128)S(1)} collective-permute-done((f32[256,528]{0,1:T(8,128)S(1)}, f32[256,528]{0,1:T(8,128)S(1)}, u32[]{:S(2)}, u32[]{:S(2)}) %collective-permute-start.5) | collective-permute-done | bytes 540704 | tf_op jit(solution)/shard_map/ppermute | solution.py:77
  91.8 0.8 fusion.127
  92.6 0.7 fusion.123
  93.3 0.7 fusion.120
  94.0 0.7 fusion.116
  94.8 1.8 %fusion.161 = f32[256,520]{0,1:T(8,128)S(1)} fusion(f32[4,256,556]{1,2,0:T(8,128)S(1)} %pad_maximum_fusion, f32[256,528]{0,1:T(8,128)} %collective-permute-done.3, f32[256,522]{0,1:T(8,128)S(1)} %fusion.116), kind=kLoop, calls=%fused_computation.313 | loop fusion | flops 3461120 | bytes 4800512 | tf_op jit(solution)/shard_map/add | solution.py:95
  96.6 0.7 fusion.157
  97.3 1.8 %fusion.154 = f32[256,516]{0,1:T(8,128)S(1)} fusion(f32[4,256,556]{1,2,0:T(8,128)S(1)} %pad_maximum_fusion, f32[256,528]{0,1:T(8,128)} %collective-permute-done.2, f32[256,518]{0,1:T(8,128)S(1)} %fusion.157), kind=kLoop, calls=%fused_computation.304 | loop fusion | flops 3434496 | bytes 4784128 | tf_op jit(solution)/shard_map/add | solution.py:95
  99.2 0.0 copy-start.1
  99.2 0.7 fusion.150
  99.9 0.3 copy-done.1
  100.2 0.2 copy-done.3
  100.4 0.7 fusion.182
  101.1 1.0 copy.14
  (17 shorter events, 0.2 us)
Async XLA Ops:
  0.0 2.6 %copy-start.5 = (f32[256,512]{1,0:T(8,128)S(1)}, f32[256,512]{1,0:T(8,128)}, u32[]{:S(2)}) copy-start(f32[256,512]{1,0:T(8,128)} %param.7) | copy-start | bytes 1572868
  0.0 2.8 %copy-start.6 = (f32[1,256,512]{2,1,0:T(8,128)S(1)}, f32[1,256,512]{2,1,0:T(8,128)}, u32[]{:S(2)}) copy-start(f32[1,256,512]{2,1,0:T(8,128)} %param.4) | copy-start | bytes 1572868
  2.8 6.2 %copy-start = (f32[256,512]{0,1:T(8,128)}, f32[256,512]{0,1:T(8,128)S(1)}, u32[]{:S(2)}) copy-start(f32[256,512]{0,1:T(8,128)S(1)} %copy.7) | copy-start | bytes 1572868
  3.0 6.0 %copy-start.4 = (f32[1,256,512]{1,2,0:T(8,128)}, f32[1,256,512]{1,2,0:T(8,128)S(1)}, u32[]{:S(2)}) copy-start(f32[1,256,512]{1,2,0:T(8,128)S(1)} %copy.8) | copy-start | bytes 1572868
  3.1 5.9 %collective-permute-start = (f32[4,256,22]{1,2,0:T(8,128)S(1)}, f32[4,256,22]{1,2,0:T(8,128)S(1)}, u32[]{:S(2)}, u32[]{:S(2)}) collective-permute-start(f32[4,256,22]{1,2,0:T(8,128)S(1)} %get-tuple-element.7), channel_id=1, source_target_pairs={{0,1},{1,2},{2,3},{3,4},{4,5},{5,6},{6,7},{7,8},{8,9},{9,10},{10,1... | collective-permute-start | bytes 270344 | tf_op jit(solution)/shard_map/ppermute | solution.py:16
  5.0 5.8 %collective-permute-start.1 = (f32[4,256,22]{1,2,0:T(8,128)S(1)}, f32[4,256,22]{1,2,0:T(8,128)S(1)}, u32[]{:S(2)}, u32[]{:S(2)}) collective-permute-start(f32[4,256,22]{1,2,0:T(8,128)S(1)} %get-tuple-element.8), channel_id=1, source_target_pairs={{1,0},{2,1},{3,2},{4,3},{5,4},{6,5},{7,6},{8,7},{9,8},{10,9},{11,1... | collective-permute-start | bytes 270344 | tf_op jit(solution)/shard_map/ppermute | solution.py:16
  19.6 2.4 %copy-start.2 = (f32[256,540]{0,1:T(8,128)}, f32[256,540]{0,1:T(8,128)S(1)}, u32[]{:S(2)}) copy-start(f32[256,540]{0,1:T(8,128)S(1)} %subtract_select_fusion) | copy-start | bytes 1658884
  19.6 15.9 %collective-permute-start.6 = (f32[256,540]{0,1:T(8,128)S(1)}, f32[256,540]{0,1:T(8,128)}, u32[]{:S(2)}, u32[]{:S(2)}) collective-permute-start(f32[256,540]{0,1:T(8,128)S(1)} %subtract_select_fusion), channel_id=1, source_target_pairs={{64,0},{128,64},{192,128},{256,192},{320,256},{384,320},{448,384},... | collective-permute-start | bytes 1658888 | tf_op jit(solution)/shard_map/ppermute | solution.py:80
  22.1 17.0 %collective-permute-start.2 = (f32[256,528]{0,1:T(8,128)S(1)}, f32[256,528]{0,1:T(8,128)}, u32[]{:S(2)}, u32[]{:S(2)}) collective-permute-start(f32[256,528]{0,1:T(8,128)S(1)} %slice.1081), channel_id=1, source_target_pairs={{0,64},{64,128},{128,192},{192,256},{256,320},{320,384},{384,448},... | collective-permute-start | bytes 1622024 | tf_op jit(solution)/shard_map/ppermute | solution.py:77
  35.5 23.9 %collective-permute-start.7 = (f32[256,540]{0,1:T(8,128)}, f32[256,540]{0,1:T(8,128)}, u32[]{:S(2)}, u32[]{:S(2)}) collective-permute-start(f32[256,540]{0,1:T(8,128)} %collective-permute-done.6), channel_id=1, source_target_pairs={{64,0},{128,64},{192,128},{256,192},{320,256},{384,320},{448,384},... | collective-permute-start | bytes 1658888 | tf_op jit(solution)/shard_map/ppermute | solution.py:80
  39.1 18.4 %collective-permute-start.3 = (f32[256,528]{0,1:T(8,128)}, f32[256,528]{0,1:T(8,128)}, u32[]{:S(2)}, u32[]{:S(2)}) collective-permute-start(f32[256,528]{0,1:T(8,128)} %collective-permute-done.2), channel_id=1, source_target_pairs={{0,64},{64,128},{128,192},{192,256},{256,320},{320,384},{384,448},... | collective-permute-start | bytes 1622024 | tf_op jit(solution)/shard_map/ppermute | solution.py:77
  57.5 17.6 %collective-permute-start.4 = (f32[256,528]{0,1:T(8,128)}, f32[256,528]{0,1:T(8,128)S(1)}, u32[]{:S(2)}, u32[]{:S(2)}) collective-permute-start(f32[256,528]{0,1:T(8,128)} %collective-permute-done.3), channel_id=1, source_target_pairs={{0,64},{64,128},{128,192},{192,256},{256,320},{320,384},{384,448},... | collective-permute-start | bytes 1622024 | tf_op jit(solution)/shard_map/ppermute | solution.py:77
  59.4 17.8 %collective-permute-start.8 = (f32[256,540]{0,1:T(8,128)}, f32[256,540]{0,1:T(8,128)S(1)}, u32[]{:S(2)}, u32[]{:S(2)}) collective-permute-start(f32[256,540]{0,1:T(8,128)} %collective-permute-done.7), channel_id=1, source_target_pairs={{64,0},{128,64},{192,128},{256,192},{320,256},{384,320},{448,384},... | collective-permute-start | bytes 1658888 | tf_op jit(solution)/shard_map/ppermute | solution.py:80
  75.1 16.7 %collective-permute-start.5 = (f32[256,528]{0,1:T(8,128)S(1)}, f32[256,528]{0,1:T(8,128)S(1)}, u32[]{:S(2)}, u32[]{:S(2)}) collective-permute-start(f32[256,528]{0,1:T(8,128)S(1)} %collective-permute-done.4), channel_id=1, source_target_pairs={{0,64},{64,128},{128,192},{192,256},{256,320},{320,384},{384,448},... | collective-permute-start | bytes 1622024 | tf_op jit(solution)/shard_map/ppermute | solution.py:77
  99.2 1.0 %copy-start.1 = (f32[256,512]{0,1:T(8,128)S(1)}, f32[256,512]{0,1:T(8,128)}, u32[]{:S(2)}) copy-start(f32[256,512]{0,1:T(8,128)} %copy-done) | copy-start | bytes 1572868
  99.2 1.2 %copy-start.3 = (f32[256,540]{0,1:T(8,128)S(1)}, f32[256,540]{0,1:T(8,128)}, u32[]{:S(2)}) copy-start(f32[256,540]{0,1:T(8,128)} %copy-done.2) | copy-start | bytes 1658884

commit v9 on v7

--- a/solution.py
+++ b/solution.py
@@ -71,16 +71,22 @@
     behind = slices - 1 - ahead
     got = {slices - 1: carried}
     wide_f = CSTEPS * behind
+    near = CSTEPS * (ahead // 2)
+    skip = [((i + 2) % slices, i) for i in range(slices)]
     block = carried
     ahead_blk = carried[:, chain - wide_f: chain + n + wide_f]
-    for r in range(1, ahead + 1):
+    for r in range(1, ahead):
         block = lax.ppermute(block, "tm", back)
         got[r - 1] = block
+        if r == 2:
+            far, fh = run(block, chain, CSTEPS * (ahead - near // CSTEPS), DT * FINE / CSTEPS)
+            far = far[:, fh - near: fh + n + near]
         if r <= behind:
             if r == behind:
                 ahead_blk, got[r - 1] = lax.optimization_barrier((ahead_blk, block))
             ahead_blk = lax.ppermute(ahead_blk, "tm", ring)
             got[slices - 1 - r] = ahead_blk
+    far = lax.ppermute(far, "tm", skip)
 
     def part(j, h):
         blk = got[j]
@@ -90,11 +96,20 @@
             return blk
         return jnp.where(me >= slices - 1 - j, blk, jnp.zeros_like(blk))
 
+    last = ahead - 1
     h = chain
     current = part(0, h)
-    for turn in range(1, slices):
+    for turn in range(1, last):
         moved, h = run(current, h, CSTEPS, DT * FINE / CSTEPS)
         current = part(turn, h) + moved
+    moved, h = run(current, h, CSTEPS, DT * FINE / CSTEPS)
+    current = moved
+    for turn in range(last + 1, slices):
+        moved, h = run(current, h, CSTEPS, DT * FINE / CSTEPS)
+        current = part(turn, h) + moved
+    far = jnp.where(me >= slices - 1 - last, far, jnp.zeros_like(far))
+    far, _ = run(far, near, near, DT * FINE / CSTEPS)
+    current = current + far
     return current[None]
 
 

time: 103 us -> 116 us (1.13)
  waiting for transfers between devices: 52 us -> 63.6 us
  other arithmetic: 22.5 us -> 26.4 us
  starting transfers between devices: 21.3 us -> 18.8 us
    ppermute x0 -> x1, waiting for transfers between devices: none -> 23.1 us  [local(): far = lax.ppermute(far, 'tm', skip)]
    ppermute x4 -> x3, waiting for transfers between devices: 48.8 us -> 36.1 us  [local(): block = lax.ppermute(block, 'tm', back)]
    ppermute x4 -> x3, starting transfers between devices: 11.8 us -> 7.38 us  [local(): block = lax.ppermute(block, 'tm', back)]
    add x14 -> x16, other arithmetic: 11.2 us -> 14.8 us  [advance(): return mid - size * moved + size * coef[2] * spread]
    ppermute x0 -> x1, starting transfers between devices: none -> 3.29 us  [local(): far = lax.ppermute(far, 'tm', skip)]
    add x6 -> x4, other arithmetic: 6.83 us -> 5.2 us  [local(): current = part(turn, h) + moved]
    ppermute x2, waiting for transfers between devices: 2.18 us -> 3.49 us  [shifted(): return lax.ppermute(block, axis, route)]
    ppermute x2, starting transfers between devices: 5.56 us -> 4.33 us  [shifted(): return lax.ppermute(block, axis, route)]
  transfers between devices with their start and end apart: 9 -> 9, of which waited for: 7 -> 6; matrix products, arithmetic and copies ran while one was open for 8% -> 9% of each run, Pallas kernels for 0% -> 0%
where the time goes in v9:
time: 116 us; the launch traced here: 114 us
  waiting for transfers between devices  63.6 us (55%)
  other arithmetic  26.4 us (23%)
  starting transfers between devices  18.8 us (16%)
  local copies, waits for them, and re-layouts  5.19 us (4%)
    ppermute x3, waiting for transfers between devices, local(): block = lax.ppermute(block, 'tm', back)  36.1 us
    ppermute x1, waiting for transfers between devices, local(): far = lax.ppermute(far, 'tm', skip)  23.1 us
    add x16, other arithmetic, advance(): return mid - size * moved + size * coef[2] * spread  14.8 us
    ppermute x3, starting transfers between devices, local(): block = lax.ppermute(block, 'tm', back)  7.38 us
    add x4, other arithmetic, local(): current = part(turn, h) + moved  5.2 us
    ppermute x2, starting transfers between devices, shifted(): return lax.ppermute(block, axis, route)  4.33 us
    ppermute x3, starting transfers between devices, local(): ahead_blk = lax.ppermute(ahead_blk, 'tm', ring)  3.84 us
    ppermute x2, waiting for transfers between devices, shifted(): return lax.ppermute(block, axis, route)  3.49 us
  transfers between devices with their start and end apart: 9, of which 6 were waited for; matrix products, arithmetic and copies ran while one was open for 9% of the time, Pallas kernels for 0%

profile of v9, /device:TPU:504, one launch (start us, length us, event | category | flops | bytes accessed | tf_op | source)
XLA Modules:
  0.0 114.3 jit_solution(4931802026776995175)
XLA Ops:
  0.0 1.3 %copy.7 = f32[256,512]{0,1:T(8,128)S(1)} copy(f32[256,512]{1,0:T(8,128)} %param.7) | data formatting | bytes 1048576 | tf_op args[3]
  1.3 1.2 %copy.6 = f32[256,512]{0,1:T(8,128)S(1)} copy(f32[256,512]{1,0:T(8,128)} %param.6) | data formatting | bytes 1048576 | tf_op args[2]
  2.6 0.2 copy.5
  2.8 0.2 copy.8
  3.1 1.9 %collective-permute-start.1 = (f32[4,256,22]{1,2,0:T(8,128)S(1)}, f32[4,256,22]{1,2,0:T(8,128)S(1)}, u32[]{:S(2)}, u32[]{:S(2)}) collective-permute-start(f32[4,256,22]{1,2,0:T(8,128)S(1)} %get-tuple-element.30), channel_id=1, source_target_pairs={{1,0},{2,1},{3,2},{4,3},{5,4},{6,5},{7,6},{8,7},{9,8},{10,9},{11,1... | collective-permute-start | bytes 270344 | tf_op jit(solution)/shard_map/ppermute | solution.py:16
  5.0 2.4 %collective-permute-start = (f32[4,256,22]{1,2,0:T(8,128)S(1)}, f32[4,256,22]{1,2,0:T(8,128)S(1)}, u32[]{:S(2)}, u32[]{:S(2)}) collective-permute-start(f32[4,256,22]{1,2,0:T(8,128)S(1)} %get-tuple-element.29), channel_id=1, source_target_pairs={{0,1},{1,2},{2,3},{3,4},{4,5},{5,6},{6,7},{7,8},{8,9},{9,10},{10,1... | collective-permute-start | bytes 270344 | tf_op jit(solution)/shard_map/ppermute | solution.py:16
  7.5 3.5 %collective-permute-done = f32[4,256,22]{1,2,0:T(8,128)S(1)} collective-permute-done((f32[4,256,22]{1,2,0:T(8,128)S(1)}, f32[4,256,22]{1,2,0:T(8,128)S(1)}, u32[]{:S(2)}, u32[]{:S(2)}) %collective-permute-start) | collective-permute-done | bytes 90144 | tf_op jit(solution)/shard_map/ppermute | solution.py:16
  10.9 1.4 %pad_maximum_fusion = f32[4,256,556]{1,2,0:T(8,128)S(1)} fusion(f32[4,256,22]{1,2,0:T(8,128)S(1)} %collective-permute-done.1, f32[1,256,512]{1,2,0:T(8,128)S(1)} %bitcast.874, f32[1,256,512]{1,2,0:T(8,128)S(1)} %bitcast.876, f32[1,256,512]{1,2,0:T(8,128)} %bitcast.878, f32[1,256,512]{1,2,0:T(8,128)} %copy-done.6, f32[4,256,22]{1,2,0:T(8,128)S(1)} %collective-permute-done), kind=kLoop, calls=%fused_computation | loop fusion | flops 2846720 | bytes 4554752 | tf_op jit(solution)/shard_map/concatenate | solution.py:24
  12.4 0.8 fusion.2
  13.2 0.8 fusion.19
  14.0 0.8 fusion.16
  14.8 0.8 fusion.13
  15.6 0.8 fusion.10
  16.3 0.8 fusion.43
  17.1 1.3 %fusion.69 = (f32[256,542]{0,1:T(8,128)S(1)}, f32[256,542]{0,1:T(8,128)S(1)}) fusion(f32[256,544]{0,1:T(8,128)S(1)} %fusion.43, f32[4,256,556]{1,2,0:T(8,128)S(1)} %pad_maximum_fusion, f32[256,544]{0,1:T(8,128)S(1)} %slice.1308, f32[256,556]{0,1:T(8,128)S(1)} %slice_bitcast_fusion), kind=kLoop, calls=%fused_computation.183 | loop fusion | flops 6382592 | bytes 7237632 | tf_op jit(solution)/shard_map/add | solution.py:41
  18.4 1.3 %subtract_select_fusion = f32[256,540]{0,1:T(8,128)S(1)} fusion(f32[256,542]{0,1:T(8,128)S(1)} %get-tuple-element.28, f32[4,256,556]{1,2,0:T(8,128)S(1)} %pad_maximum_fusion, f32[256,542]{0,1:T(8,128)S(1)} %get-tuple-element.27, pred[]{:T(512)S(6)} %eq.3), kind=kLoop, calls=%fused_computation.65 | loop fusion | flops 6635520 | bytes 6680577 | tf_op jit(solution)/shard_map/jit(_where)/select_n | solution.py:67
  19.8 3.3 %collective-permute-start.4 = (f32[256,540]{0,1:T(8,128)S(1)}, f32[256,540]{0,1:T(8,128)}, u32[]{:S(2)}, u32[]{:S(2)}) collective-permute-start(f32[256,540]{0,1:T(8,128)S(1)} %subtract_select_fusion), channel_id=1, source_target_pairs={{64,0},{128,64},{192,128},{256,192},{320,256},{384,320},{448,384},... | collective-permute-start | bytes 1658888 | tf_op jit(solution)/shard_map/ppermute | solution.py:79
  23.0 0.8 slice.1313
  23.9 1.3 %collective-permute-start.2 = (f32[256,524]{0,1:T(8,128)}, f32[256,524]{0,1:T(8,128)}, u32[]{:S(2)}, u32[]{:S(2)}) collective-permute-start(f32[256,524]{0,1:T(8,128)} %slice.1313), channel_id=1, source_target_pairs={{0,64},{64,128},{128,192},{192,256},{256,320},{320,384},{384,448},... | collective-permute-start | bytes 1609736 | tf_op jit(solution)/shard_map/ppermute | solution.py:87
  25.2 13.0 %collective-permute-done.4 = f32[256,540]{0,1:T(8,128)} collective-permute-done((f32[256,540]{0,1:T(8,128)S(1)}, f32[256,540]{0,1:T(8,128)}, u32[]{:S(2)}, u32[]{:S(2)}) %collective-permute-start.4) | collective-permute-done | bytes 552992 | tf_op jit(solution)/shard_map/ppermute | solution.py:79
  38.2 2.0 %collective-permute-start.5 = (f32[256,540]{0,1:T(8,128)}, f32[256,540]{0,1:T(8,128)S(1)}, u32[]{:S(2)}, u32[]{:S(2)}) collective-permute-start(f32[256,540]{0,1:T(8,128)} %collective-permute-done.4), channel_id=1, source_target_pairs={{64,0},{128,64},{192,128},{256,192},{320,256},{384,320},{448,384},... | collective-permute-start | bytes 1658888 | tf_op jit(solution)/shard_map/ppermute | solution.py:79
  40.2 0.1 maximum_bitcast_fusion
  40.4 0.8 collective-permute-done.2
  41.2 1.3 %collective-permute-start.3 = (f32[256,524]{0,1:T(8,128)}, f32[256,524]{0,1:T(8,128)S(1)}, u32[]{:S(2)}, u32[]{:S(2)}) collective-permute-start(f32[256,524]{0,1:T(8,128)} %collective-permute-done.2), channel_id=1, source_target_pairs={{0,64},{64,128},{128,192},{192,256},{256,320},{320,384},{384,448},... | collective-permute-start | bytes 1609736 | tf_op jit(solution)/shard_map/ppermute | solution.py:87
  42.5 1.1 broadcast_select_fusion
  43.6 12.6 %collective-permute-done.5 = f32[256,540]{0,1:T(8,128)S(1)} collective-permute-done((f32[256,540]{0,1:T(8,128)}, f32[256,540]{0,1:T(8,128)S(1)}, u32[]{:S(2)}, u32[]{:S(2)}) %collective-permute-start.5) | collective-permute-done | bytes 552992 | tf_op jit(solution)/shard_map/ppermute | solution.py:79
  56.1 2.1 %collective-permute-start.6 = (f32[256,540]{0,1:T(8,128)S(1)}, f32[256,540]{0,1:T(8,128)S(1)}, u32[]{:S(2)}, u32[]{:S(2)}) collective-permute-start(f32[256,540]{0,1:T(8,128)S(1)} %collective-permute-done.5), channel_id=1, source_target_pairs={{64,0},{128,64},{192,128},{256,192},{320,256},{384,320},{448,384},... | collective-permute-start | bytes 1658888 | tf_op jit(solution)/shard_map/ppermute | solution.py:79
  58.2 1.3 %fusion.47 = (f32[256,538]{0,1:T(8,128)S(1)}, f32[256,538]{0,1:T(8,128)S(1)}) fusion(f32[256,540]{0,1:T(8,128)S(1)} %broadcast_select_fusion, f32[4,256,556]{1,2,0:T(8,128)S(1)} %pad_maximum_fusion, f32[256,540]{0,1:T(8,128)S(1)} %collective-permute-done.5), kind=kLoop, calls=%fused_computation.143 | loop fusion | flops 6197760 | bytes 7229440 | tf_op jit(solution)/shard_map/add | solution.py:41
  59.5 1.4 %fusion.91 = (f32[256,536]{0,1:T(8,128)S(1)}, f32[256,536]{0,1:T(8,128)S(1)}) fusion(f32[256,540]{0,1:T(8,128)S(1)} %collective-permute-done.5, f32[256,538]{0,1:T(8,128)S(1)} %get-tuple-element.22, f32[4,256,556]{1,2,0:T(8,128)S(1)} %pad_maximum_fusion, pred[]{:T(512)S(6)} %ge.13, f32[256,538]{0,1:T(8,128)S(1)} %get-tuple-element.23), kind=kLoop, calls=%fused_computation.222 | loop fusion | flops 6449152 | bytes 7700481 | tf_op jit(solution)/shard_map/add | solution.py:104
  60.9 1.3 %fusion.107 = (f32[256,534]{0,1:T(8,128)S(1)}, f32[256,534]{0,1:T(8,128)S(1)}) fusion(f32[256,536]{0,1:T(8,128)S(1)} %get-tuple-element.20, f32[4,256,556]{1,2,0:T(8,128)S(1)} %pad_maximum_fusion, f32[256,536]{0,1:T(8,128)S(1)} %get-tuple-element.21), kind=kLoop, calls=%fused_computation.248 | loop fusion | flops 6151680 | bytes 7131136 | tf_op jit(solution)/shard_map/add | solution.py:41
  62.2 0.2 pad_slice_fusion.29
  62.5 10.6 %collective-permute-done.6 = f32[256,540]{0,1:T(8,128)S(1)} collective-permute-done((f32[256,540]{0,1:T(8,128)S(1)}, f32[256,540]{0,1:T(8,128)S(1)}, u32[]{:S(2)}, u32[]{:S(2)}) %collective-permute-start.6) | collective-permute-done | bytes 552992 | tf_op jit(solution)/shard_map/ppermute | solution.py:79
  73.0 1.3 %collective-permute-start.7 = (f32[256,524]{0,1:T(8,128)S(1)}, f32[256,524]{0,1:T(8,128)S(1)}, u32[]{:S(2)}, u32[]{:S(2)}) collective-permute-start(f32[256,524]{0,1:T(8,128)S(1)} %collective-permute-done.3), channel_id=1, source_target_pairs={{0,64},{64,128},{128,192},{192,256},{256,320},{320,384},{384,448},... | collective-permute-start | bytes 1609736 | tf_op jit(solution)/shard_map/ppermute | solution.py:87
  74.3 1.1 bitcast_multiply_fusion.58
  75.4 0.8 fusion.87
  76.2 0.7 fusion.161
  76.9 3.3 %collective-permute-start.8 = (f32[256,520]{0,1:T(8,128)S(1)}, f32[256,520]{0,1:T(8,128)S(1)}, u32[]{:S(2)}, u32[]{:S(2)}) collective-permute-start(f32[256,520]{0,1:T(8,128)S(1)} %fusion.161), channel_id=1, source_target_pairs={{128,0},{192,64},{256,128},{320,192},{384,256},{448,320},{0,384},{... | collective-permute-start | bytes 1597448 | tf_op jit(solution)/shard_map/ppermute | solution.py:89
  80.2 0.7 fusion.140
  80.9 0.8 fusion.137
  81.7 23.1 %collective-permute-done.8 = f32[256,520]{0,1:T(8,128)S(1)} collective-permute-done((f32[256,520]{0,1:T(8,128)S(1)}, f32[256,520]{0,1:T(8,128)S(1)}, u32[]{:S(2)}, u32[]{:S(2)}) %collective-permute-start.8) | collective-permute-done | bytes 532512 | tf_op jit(solution)/shard_map/ppermute | solution.py:89
  104.9 0.7 fusion.134
  105.6 0.7 fusion.130
  106.3 0.8 fusion.173
  107.1 1.3 %fusion.201 = (f32[256,518]{0,1:T(8,128)S(1)}, f32[256,518]{0,1:T(8,128)S(1)}) fusion(f32[256,520]{0,1:T(8,128)S(1)} %fusion.173, f32[4,256,556]{1,2,0:T(8,128)S(1)} %pad_maximum_fusion, f32[256,520]{0,1:T(8,128)S(1)} %broadcast_select_fusion.1), kind=kLoop, calls=%fused_computation.408 | loop fusion | flops 5967360 | bytes 6918144 | tf_op jit(solution)/shard_map/add | solution.py:41
  108.4 2.4 %slice_add_fusion.4 = (f32[256,516]{0,1:T(8,128)S(1)}, f32[256,516]{0,1:T(8,128)S(1)}) fusion(f32[256,524]{0,1:T(8,128)} %collective-permute-done.2, f32[256,518]{0,1:T(8,128)S(1)} %get-tuple-element.15, f32[4,256,556]{1,2,0:T(8,128)S(1)} %pad_maximum_fusion, f32[256,518]{0,1:T(8,128)S(1)} %get-tuple-element.16), kind=kLoop, calls=%fused_computation.362 | loop fusion | flops 6076416 | bytes 7442432 | tf_op jit(solution)/shard_map/add | solution.py:109
  110.7 1.3 %fusion.177 = (f32[256,514]{0,1:T(8,128)S(1)}, f32[256,514]{0,1:T(8,128)S(1)}) fusion(f32[256,516]{0,1:T(8,128)S(1)} %get-tuple-element.13, f32[4,256,556]{1,2,0:T(8,128)S(1)} %pad_maximum_fusion, f32[256,516]{0,1:T(8,128)S(1)} %get-tuple-element.14), kind=kLoop, calls=%fused_computation.368 | loop fusion | flops 5921280 | bytes 6909952 | tf_op jit(solution)/shard_map/add | solution.py:41
  112.1 1.3 %fusion.216 = f32[1,256,512]{1,2,0:T(8,128)S(1)} fusion(f32[256,540]{0,1:T(8,128)S(1)} %copy-done.5, f32[256,514]{0,1:T(8,128)S(1)} %get-tuple-element.12, f32[256,512]{0,1:T(8,128)S(1)} %copy.7, f32[256,514]{0,1:T(8,128)S(1)} %get-tuple-element.11, f32[256,512]{0,1:T(8,128)S(1)} %copy-done.1, f32[256,512]{0,1:T(8,128)S(1)} %copy-done.3), kind=kLoop, calls=%fused_computation.434 | loop fusion | flops 6160384 | bytes 6832128 | tf_op jit(solution)/shard_map/broadcast_in_dim | solution.py:113
  113.4 1.0 copy.14
  (25 shorter events, 0.2 us)
Async XLA Ops:
  0.0 2.6 %copy-start.7 = (f32[256,512]{1,0:T(8,128)S(1)}, f32[256,512]{1,0:T(8,128)}, u32[]{:S(2)}) copy-start(f32[256,512]{1,0:T(8,128)} %param.5) | copy-start | bytes 1572868
  0.0 2.8 %copy-start.8 = (f32[1,256,512]{2,1,0:T(8,128)S(1)}, f32[1,256,512]{2,1,0:T(8,128)}, u32[]{:S(2)}) copy-start(f32[1,256,512]{2,1,0:T(8,128)} %param.4) | copy-start | bytes 1572868
  2.6 9.8 %copy-start = (f32[256,512]{0,1:T(8,128)}, f32[256,512]{0,1:T(8,128)S(1)}, u32[]{:S(2)}) copy-start(f32[256,512]{0,1:T(8,128)S(1)} %copy.6) | copy-start | bytes 1572868
  2.8 4.6 %copy-start.2 = (f32[256,512]{0,1:T(8,128)}, f32[256,512]{0,1:T(8,128)S(1)}, u32[]{:S(2)}) copy-start(f32[256,512]{0,1:T(8,128)S(1)} %copy.5) | copy-start | bytes 1572868
  3.0 4.4 %copy-start.6 = (f32[1,256,512]{1,2,0:T(8,128)}, f32[1,256,512]{1,2,0:T(8,128)S(1)}, u32[]{:S(2)}) copy-start(f32[1,256,512]{1,2,0:T(8,128)S(1)} %copy.8) | copy-start | bytes 1572868
  3.1 4.4 %collective-permute-start.1 = (f32[4,256,22]{1,2,0:T(8,128)S(1)}, f32[4,256,22]{1,2,0:T(8,128)S(1)}, u32[]{:S(2)}, u32[]{:S(2)}) collective-permute-start(f32[4,256,22]{1,2,0:T(8,128)S(1)} %get-tuple-element.30), channel_id=1, source_target_pairs={{1,0},{2,1},{3,2},{4,3},{5,4},{6,5},{7,6},{8,7},{9,8},{10,9},{11,1... | collective-permute-start | bytes 270344 | tf_op jit(solution)/shard_map/ppermute | solution.py:16
  5.0 5.9 %collective-permute-start = (f32[4,256,22]{1,2,0:T(8,128)S(1)}, f32[4,256,22]{1,2,0:T(8,128)S(1)}, u32[]{:S(2)}, u32[]{:S(2)}) collective-permute-start(f32[4,256,22]{1,2,0:T(8,128)S(1)} %get-tuple-element.29), channel_id=1, source_target_pairs={{0,1},{1,2},{2,3},{3,4},{4,5},{5,6},{6,7},{7,8},{8,9},{9,10},{10,1... | collective-permute-start | bytes 270344 | tf_op jit(solution)/shard_map/ppermute | solution.py:16
  19.8 5.4 %copy-start.4 = (f32[256,540]{0,1:T(8,128)}, f32[256,540]{0,1:T(8,128)S(1)}, u32[]{:S(2)}) copy-start(f32[256,540]{0,1:T(8,128)S(1)} %subtract_select_fusion) | copy-start | bytes 1658884
  19.8 18.4 %collective-permute-start.4 = (f32[256,540]{0,1:T(8,128)S(1)}, f32[256,540]{0,1:T(8,128)}, u32[]{:S(2)}, u32[]{:S(2)}) collective-permute-start(f32[256,540]{0,1:T(8,128)S(1)} %subtract_select_fusion), channel_id=1, source_target_pairs={{64,0},{128,64},{192,128},{256,192},{320,256},{384,320},{448,384},... | collective-permute-start | bytes 1658888 | tf_op jit(solution)/shard_map/ppermute | solution.py:79
  23.9 17.3 %collective-permute-start.2 = (f32[256,524]{0,1:T(8,128)}, f32[256,524]{0,1:T(8,128)}, u32[]{:S(2)}, u32[]{:S(2)}) collective-permute-start(f32[256,524]{0,1:T(8,128)} %slice.1313), channel_id=1, source_target_pairs={{0,64},{64,128},{128,192},{192,256},{256,320},{320,384},{384,448},... | collective-permute-start | bytes 1609736 | tf_op jit(solution)/shard_map/ppermute | solution.py:87
  38.2 18.0 %collective-permute-start.5 = (f32[256,540]{0,1:T(8,128)}, f32[256,540]{0,1:T(8,128)S(1)}, u32[]{:S(2)}, u32[]{:S(2)}) collective-permute-start(f32[256,540]{0,1:T(8,128)} %collective-permute-done.4), channel_id=1, source_target_pairs={{64,0},{128,64},{192,128},{256,192},{320,256},{384,320},{448,384},... | collective-permute-start | bytes 1658888 | tf_op jit(solution)/shard_map/ppermute | solution.py:79
  41.2 21.3 %collective-permute-start.3 = (f32[256,524]{0,1:T(8,128)}, f32[256,524]{0,1:T(8,128)S(1)}, u32[]{:S(2)}, u32[]{:S(2)}) collective-permute-start(f32[256,524]{0,1:T(8,128)} %collective-permute-done.2), channel_id=1, source_target_pairs={{0,64},{64,128},{128,192},{192,256},{256,320},{320,384},{384,448},... | collective-permute-start | bytes 1609736 | tf_op jit(solution)/shard_map/ppermute | solution.py:87
  56.1 16.9 %collective-permute-start.6 = (f32[256,540]{0,1:T(8,128)S(1)}, f32[256,540]{0,1:T(8,128)S(1)}, u32[]{:S(2)}, u32[]{:S(2)}) collective-permute-start(f32[256,540]{0,1:T(8,128)S(1)} %collective-permute-done.5), channel_id=1, source_target_pairs={{64,0},{128,64},{192,128},{256,192},{320,256},{384,320},{448,384},... | collective-permute-start | bytes 1658888 | tf_op jit(solution)/shard_map/ppermute | solution.py:79
  73.0 31.9 %collective-permute-start.7 = (f32[256,524]{0,1:T(8,128)S(1)}, f32[256,524]{0,1:T(8,128)S(1)}, u32[]{:S(2)}, u32[]{:S(2)}) collective-permute-start(f32[256,524]{0,1:T(8,128)S(1)} %collective-permute-done.3), channel_id=1, source_target_pairs={{0,64},{64,128},{128,192},{192,256},{256,320},{320,384},{384,448},... | collective-permute-start | bytes 1609736 | tf_op jit(solution)/shard_map/ppermute | solution.py:87
  76.9 27.9 %collective-permute-start.8 = (f32[256,520]{0,1:T(8,128)S(1)}, f32[256,520]{0,1:T(8,128)S(1)}, u32[]{:S(2)}, u32[]{:S(2)}) collective-permute-start(f32[256,520]{0,1:T(8,128)S(1)} %fusion.161), channel_id=1, source_target_pairs={{128,0},{192,64},{256,128},{320,192},{384,256},{448,320},{0,384},{... | collective-permute-start | bytes 1597448 | tf_op jit(solution)/shard_map/ppermute | solution.py:89
  110.7 1.3 %copy-start.1 = (f32[256,512]{0,1:T(8,128)S(1)}, f32[256,512]{0,1:T(8,128)}, u32[]{:S(2)}) copy-start(f32[256,512]{0,1:T(8,128)} %copy-done) | copy-start | bytes 1572868
  110.7 1.3 %copy-start.3 = (f32[256,512]{0,1:T(8,128)S(1)}, f32[256,512]{0,1:T(8,128)}, u32[]{:S(2)}) copy-start(f32[256,512]{0,1:T(8,128)} %copy-done.2) | copy-start | bytes 1572868
  110.7 1.4 %copy-start.5 = (f32[256,540]{0,1:T(8,128)S(1)}, f32[256,540]{0,1:T(8,128)}, u32[]{:S(2)}) copy-start(f32[256,540]{0,1:T(8,128)} %copy-done.4) | copy-start | bytes 1658884

commit v10 on v7

--- a/solution.py
+++ b/solution.py
@@ -76,9 +76,7 @@
     for r in range(1, ahead + 1):
         block = lax.ppermute(block, "tm", back)
         got[r - 1] = block
-        if r <= behind:
-            if r == behind:
-                ahead_blk, got[r - 1] = lax.optimization_barrier((ahead_blk, block))
+        if r < behind:
             ahead_blk = lax.ppermute(ahead_blk, "tm", ring)
             got[slices - 1 - r] = ahead_blk
 
@@ -92,7 +90,13 @@
 
     h = chain
     current = part(0, h)
-    for turn in range(1, slices):
+    for turn in range(1, behind):
+        moved, h = run(current, h, CSTEPS, DT * FINE / CSTEPS)
+        current = part(turn, h) + moved
+    ahead_blk, current = lax.optimization_barrier((ahead_blk, current))
+    ahead_blk = lax.ppermute(ahead_blk, "tm", ring)
+    got[slices - 1 - behind] = ahead_blk
+    for turn in range(behind, slices):
         moved, h = run(current, h, CSTEPS, DT * FINE / CSTEPS)
         current = part(turn, h) + moved
     return current[None]

time: 103 us -> 102 us (level)
  starting transfers between devices: 21.3 us -> 18.7 us
  waiting for transfers between devices: 52 us -> 53.1 us
    ppermute x4, starting transfers between devices: 11.8 us -> 9.29 us  [local(): block = lax.ppermute(block, 'tm', back)]
    ppermute x4, waiting for transfers between devices: 48.8 us -> 50 us  [local(): block = lax.ppermute(block, 'tm', back)]
where the time goes in v10:
time: 102 us; the launch traced here: 100 us
  waiting for transfers between devices  53.1 us (52%)
  other arithmetic  22.5 us (22%)
  starting transfers between devices  18.7 us (18%)
  local copies, waits for them, and re-layouts  5.36 us (5%)
    ppermute x4, waiting for transfers between devices, local(): block = lax.ppermute(block, 'tm', back)  50 us
    add x14, other arithmetic, advance(): return mid - size * moved + size * coef[2] * spread  11.2 us
    ppermute x4, starting transfers between devices, local(): block = lax.ppermute(block, 'tm', back)  9.29 us
    add x6, other arithmetic, local(): current = part(turn, h) + moved  6.81 us
    ppermute x2, starting transfers between devices, shifted(): return lax.ppermute(block, axis, route)  5.56 us
    ppermute x3, starting transfers between devices, local(): ahead_blk = lax.ppermute(ahead_blk, 'tm', ring)  3.85 us
    unnamed x18, local copies, waits for them, and re-layouts  3.45 us
    ppermute x2, waiting for transfers between devices, shifted(): return lax.ppermute(block, axis, route)  2.18 us
  transfers between devices with their start and end apart: 9, of which 7 were waited for; matrix products, arithmetic and copies ran while one was open for 8% of the time, Pallas kernels for 0%

profile of v10, /device:TPU:504, one launch (start us, length us, event | category | flops | bytes accessed | tf_op | source)
XLA Modules:
  0.0 100.0 jit_solution(4346685889468203760)
XLA Ops:
  0.0 1.3 %copy.5 = f32[256,512]{0,1:T(8,128)S(1)} copy(f32[256,512]{1,0:T(8,128)} %param.5) | data formatting | bytes 1048576 | tf_op args[1]
  1.3 1.2 %copy.6 = f32[256,512]{0,1:T(8,128)S(1)} copy(f32[256,512]{1,0:T(8,128)} %param.6) | data formatting | bytes 1048576 | tf_op args[2]
  2.6 0.2 copy.7
  2.8 0.2 copy.8
  3.1 1.9 %collective-permute-start = (f32[4,256,22]{1,2,0:T(8,128)S(1)}, f32[4,256,22]{1,2,0:T(8,128)S(1)}, u32[]{:S(2)}, u32[]{:S(2)}) collective-permute-start(f32[4,256,22]{1,2,0:T(8,128)S(1)} %get-tuple-element.11), channel_id=1, source_target_pairs={{0,1},{1,2},{2,3},{3,4},{4,5},{5,6},{6,7},{7,8},{8,9},{9,10},{10,1... | collective-permute-start | bytes 270344 | tf_op jit(solution)/shard_map/ppermute | solution.py:16
  5.0 3.6 %collective-permute-start.1 = (f32[4,256,22]{1,2,0:T(8,128)S(1)}, f32[4,256,22]{1,2,0:T(8,128)S(1)}, u32[]{:S(2)}, u32[]{:S(2)}) collective-permute-start(f32[4,256,22]{1,2,0:T(8,128)S(1)} %get-tuple-element.12), channel_id=1, source_target_pairs={{1,0},{2,1},{3,2},{4,3},{5,4},{6,5},{7,6},{8,7},{9,8},{10,9},{11,1... | collective-permute-start | bytes 270344 | tf_op jit(solution)/shard_map/ppermute | solution.py:16
  8.6 0.3 collective-permute-done
  9.0 1.8 %collective-permute-done.1 = f32[4,256,22]{1,2,0:T(8,128)S(1)} collective-permute-done((f32[4,256,22]{1,2,0:T(8,128)S(1)}, f32[4,256,22]{1,2,0:T(8,128)S(1)}, u32[]{:S(2)}, u32[]{:S(2)}) %collective-permute-start.1) | collective-permute-done | bytes 90144 | tf_op jit(solution)/shard_map/ppermute | solution.py:16
  10.8 1.4 %pad_maximum_fusion = f32[4,256,556]{1,2,0:T(8,128)S(1)} fusion(f32[4,256,22]{1,2,0:T(8,128)S(1)} %collective-permute-done.1, f32[1,256,512]{1,2,0:T(8,128)} %bitcast.748, f32[1,256,512]{1,2,0:T(8,128)S(1)} %bitcast.746, f32[1,256,512]{1,2,0:T(8,128)S(1)} %bitcast.744, f32[1,256,512]{1,2,0:T(8,128)} %copy-done.4, f32[4,256,22]{1,2,0:T(8,128)S(1)} %collective-permute-done), kind=kLoop, calls=%fused_computation | loop fusion | flops 2846720 | bytes 4554752 | tf_op jit(solution)/shard_map/concatenate | solution.py:24
  12.3 0.8 fusion.2
  13.1 0.8 fusion.19
  13.9 0.8 fusion.16
  14.7 0.8 fusion.13
  15.5 0.8 fusion.10
  16.2 0.8 fusion.45
  17.0 1.3 %fusion.64 = (f32[256,542]{0,1:T(8,128)S(1)}, f32[256,542]{0,1:T(8,128)S(1)}) fusion(f32[256,544]{0,1:T(8,128)S(1)} %fusion.45, f32[4,256,556]{1,2,0:T(8,128)S(1)} %pad_maximum_fusion, f32[256,544]{0,1:T(8,128)S(1)} %slice.1076, f32[256,556]{0,1:T(8,128)S(1)} %slice_bitcast_fusion), kind=kLoop, calls=%fused_computation.158 | loop fusion | flops 6382592 | bytes 7237632 | tf_op jit(solution)/shard_map/add | solution.py:41
  18.3 1.3 %subtract_select_fusion = f32[256,540]{0,1:T(8,128)S(1)} fusion(f32[256,542]{0,1:T(8,128)S(1)} %get-tuple-element.10, f32[4,256,556]{1,2,0:T(8,128)S(1)} %pad_maximum_fusion, f32[256,542]{0,1:T(8,128)S(1)} %get-tuple-element.9, pred[]{:T(512)S(6)} %eq.3), kind=kLoop, calls=%fused_computation.49 | loop fusion | flops 6635520 | bytes 6680577 | tf_op jit(solution)/shard_map/jit(_where)/select_n | solution.py:67
  19.6 3.3 %collective-permute-start.4 = (f32[256,540]{0,1:T(8,128)S(1)}, f32[256,540]{0,1:T(8,128)}, u32[]{:S(2)}, u32[]{:S(2)}) collective-permute-start(f32[256,540]{0,1:T(8,128)S(1)} %subtract_select_fusion), channel_id=1, source_target_pairs={{64,0},{128,64},{192,128},{256,192},{320,256},{384,320},{448,384},... | collective-permute-start | bytes 1658888 | tf_op jit(solution)/shard_map/ppermute | solution.py:77
  22.9 0.8 slice.1081
  23.7 1.3 %collective-permute-start.2 = (f32[256,524]{0,1:T(8,128)}, f32[256,524]{0,1:T(8,128)}, u32[]{:S(2)}, u32[]{:S(2)}) collective-permute-start(f32[256,524]{0,1:T(8,128)} %slice.1081), channel_id=1, source_target_pairs={{0,64},{64,128},{128,192},{192,256},{256,320},{320,384},{384,448},... | collective-permute-start | bytes 1609736 | tf_op jit(solution)/shard_map/ppermute | solution.py:80
  25.0 12.2 %collective-permute-done.4 = f32[256,540]{0,1:T(8,128)} collective-permute-done((f32[256,540]{0,1:T(8,128)S(1)}, f32[256,540]{0,1:T(8,128)}, u32[]{:S(2)}, u32[]{:S(2)}) %collective-permute-start.4) | collective-permute-done | bytes 552992 | tf_op jit(solution)/shard_map/ppermute | solution.py:77
  37.3 2.0 %collective-permute-start.5 = (f32[256,540]{0,1:T(8,128)}, f32[256,540]{0,1:T(8,128)}, u32[]{:S(2)}, u32[]{:S(2)}) collective-permute-start(f32[256,540]{0,1:T(8,128)} %collective-permute-done.4), channel_id=1, source_target_pairs={{64,0},{128,64},{192,128},{256,192},{320,256},{384,320},{448,384},... | collective-permute-start | bytes 1658888 | tf_op jit(solution)/shard_map/ppermute | solution.py:77
  39.3 1.0 collective-permute-done.2
  40.3 1.3 %collective-permute-start.3 = (f32[256,524]{0,1:T(8,128)}, f32[256,524]{0,1:T(8,128)S(1)}, u32[]{:S(2)}, u32[]{:S(2)}) collective-permute-start(f32[256,524]{0,1:T(8,128)} %collective-permute-done.2), channel_id=1, source_target_pairs={{0,64},{64,128},{128,192},{192,256},{256,320},{320,384},{384,448},... | collective-permute-start | bytes 1609736 | tf_op jit(solution)/shard_map/ppermute | solution.py:80
  41.6 1.1 %broadcast_select_fusion = f32[256,540]{0,1:T(8,128)S(1)} fusion(f32[256,540]{0,1:T(8,128)} %collective-permute-done.4, pred[]{:T(512)S(6)} %ge.14), kind=kLoop, calls=%fused_computation.357 | loop fusion | flops 138240 | bytes 1105921 | tf_op jit(solution)/shard_map/jit(_where)/select_n | solution.py:89
  42.7 0.8 fusion.42
  43.5 12.6 %collective-permute-done.5 = f32[256,540]{0,1:T(8,128)} collective-permute-done((f32[256,540]{0,1:T(8,128)}, f32[256,540]{0,1:T(8,128)}, u32[]{:S(2)}, u32[]{:S(2)}) %collective-permute-start.5) | collective-permute-done | bytes 552992 | tf_op jit(solution)/shard_map/ppermute | solution.py:77
  56.1 1.9 %collective-permute-start.6 = (f32[256,540]{0,1:T(8,128)}, f32[256,540]{0,1:T(8,128)S(1)}, u32[]{:S(2)}, u32[]{:S(2)}) collective-permute-start(f32[256,540]{0,1:T(8,128)} %collective-permute-done.5), channel_id=1, source_target_pairs={{64,0},{128,64},{192,128},{256,192},{320,256},{384,320},{448,384},... | collective-permute-start | bytes 1658888 | tf_op jit(solution)/shard_map/ppermute | solution.py:77
  58.0 1.9 %fusion.93 = f32[256,536]{0,1:T(8,128)S(1)} fusion(f32[4,256,556]{1,2,0:T(8,128)S(1)} %pad_maximum_fusion, f32[256,540]{0,1:T(8,128)} %collective-permute-done.5, f32[256,538]{0,1:T(8,128)S(1)} %fusion.42, pred[]{:T(512)S(6)} %ge.13), kind=kLoop, calls=%fused_computation.203 | loop fusion | flops 3704832 | bytes 4947969 | tf_op jit(solution)/shard_map/add | solution.py:95
  59.9 0.8 fusion.89
  60.7 13.3 %collective-permute-done.6 = f32[256,540]{0,1:T(8,128)S(1)} collective-permute-done((f32[256,540]{0,1:T(8,128)}, f32[256,540]{0,1:T(8,128)S(1)}, u32[]{:S(2)}, u32[]{:S(2)}) %collective-permute-start.6) | collective-permute-done | bytes 552992 | tf_op jit(solution)/shard_map/ppermute | solution.py:77
  74.0 2.1 %collective-permute-start.8 = (f32[256,540]{0,1:T(8,128)S(1)}, f32[256,540]{0,1:T(8,128)S(1)}, u32[]{:S(2)}, u32[]{:S(2)}) collective-permute-start(f32[256,540]{0,1:T(8,128)S(1)} %collective-permute-done.6), channel_id=1, source_target_pairs={{64,0},{128,64},{192,128},{256,192},{320,256},{384,320},{448,384},... | collective-permute-start | bytes 1658888 | tf_op jit(solution)/shard_map/ppermute | solution.py:77
  76.1 0.8 fusion.86
  76.9 1.3 %collective-permute-start.7 = (f32[256,524]{0,1:T(8,128)S(1)}, f32[256,524]{0,1:T(8,128)S(1)}, u32[]{:S(2)}, u32[]{:S(2)}) collective-permute-start(f32[256,524]{0,1:T(8,128)S(1)} %collective-permute-done.3), channel_id=1, source_target_pairs={{0,64},{64,128},{128,192},{192,256},{256,320},{320,384},{384,448},... | collective-permute-start | bytes 1609736 | tf_op jit(solution)/shard_map/ppermute | solution.py:97
  78.2 0.7 fusion.82
  79.0 11.8 %collective-permute-done.8 = f32[256,540]{0,1:T(8,128)S(1)} collective-permute-done((f32[256,540]{0,1:T(8,128)S(1)}, f32[256,540]{0,1:T(8,128)S(1)}, u32[]{:S(2)}, u32[]{:S(2)}) %collective-permute-start.8) | collective-permute-done | bytes 552992 | tf_op jit(solution)/shard_map/ppermute | solution.py:77
  90.8 0.8 fusion.127
  91.6 0.7 fusion.123
  92.3 0.7 fusion.120
  93.0 0.7 fusion.116
  93.8 0.8 fusion.161
  94.5 0.7 fusion.157
  95.3 1.8 %fusion.154 = f32[256,516]{0,1:T(8,128)S(1)} fusion(f32[4,256,556]{1,2,0:T(8,128)S(1)} %pad_maximum_fusion, f32[256,524]{0,1:T(8,128)} %collective-permute-done.2, f32[256,518]{0,1:T(8,128)S(1)} %fusion.157), kind=kLoop, calls=%fused_computation.305 | loop fusion | flops 3434496 | bytes 4784128 | tf_op jit(solution)/shard_map/add | solution.py:101
  97.1 0.7 fusion.150
  97.9 0.3 copy-done.1
  98.1 0.2 copy-done.3
  98.3 0.7 fusion.182
  99.0 1.0 copy.14
  (17 shorter events, 0.1 us)
Async XLA Ops:
  0.0 2.6 %copy-start.5 = (f32[256,512]{1,0:T(8,128)S(1)}, f32[256,512]{1,0:T(8,128)}, u32[]{:S(2)}) copy-start(f32[256,512]{1,0:T(8,128)} %param.7) | copy-start | bytes 1572868
  0.0 2.8 %copy-start.6 = (f32[1,256,512]{2,1,0:T(8,128)S(1)}, f32[1,256,512]{2,1,0:T(8,128)}, u32[]{:S(2)}) copy-start(f32[1,256,512]{2,1,0:T(8,128)} %param.4) | copy-start | bytes 1572868
  2.8 6.2 %copy-start = (f32[256,512]{0,1:T(8,128)}, f32[256,512]{0,1:T(8,128)S(1)}, u32[]{:S(2)}) copy-start(f32[256,512]{0,1:T(8,128)S(1)} %copy.7) | copy-start | bytes 1572868
  3.0 6.0 %copy-start.4 = (f32[1,256,512]{1,2,0:T(8,128)}, f32[1,256,512]{1,2,0:T(8,128)S(1)}, u32[]{:S(2)}) copy-start(f32[1,256,512]{1,2,0:T(8,128)S(1)} %copy.8) | copy-start | bytes 1572868
  3.1 5.9 %collective-permute-start = (f32[4,256,22]{1,2,0:T(8,128)S(1)}, f32[4,256,22]{1,2,0:T(8,128)S(1)}, u32[]{:S(2)}, u32[]{:S(2)}) collective-permute-start(f32[4,256,22]{1,2,0:T(8,128)S(1)} %get-tuple-element.11), channel_id=1, source_target_pairs={{0,1},{1,2},{2,3},{3,4},{4,5},{5,6},{6,7},{7,8},{8,9},{9,10},{10,1... | collective-permute-start | bytes 270344 | tf_op jit(solution)/shard_map/ppermute | solution.py:16
  5.0 5.8 %collective-permute-start.1 = (f32[4,256,22]{1,2,0:T(8,128)S(1)}, f32[4,256,22]{1,2,0:T(8,128)S(1)}, u32[]{:S(2)}, u32[]{:S(2)}) collective-permute-start(f32[4,256,22]{1,2,0:T(8,128)S(1)} %get-tuple-element.12), channel_id=1, source_target_pairs={{1,0},{2,1},{3,2},{4,3},{5,4},{6,5},{7,6},{8,7},{9,8},{10,9},{11,1... | collective-permute-start | bytes 270344 | tf_op jit(solution)/shard_map/ppermute | solution.py:16
  19.6 3.3 %copy-start.2 = (f32[256,540]{0,1:T(8,128)}, f32[256,540]{0,1:T(8,128)S(1)}, u32[]{:S(2)}) copy-start(f32[256,540]{0,1:T(8,128)S(1)} %subtract_select_fusion) | copy-start | bytes 1658884
  19.6 17.6 %collective-permute-start.4 = (f32[256,540]{0,1:T(8,128)S(1)}, f32[256,540]{0,1:T(8,128)}, u32[]{:S(2)}, u32[]{:S(2)}) collective-permute-start(f32[256,540]{0,1:T(8,128)S(1)} %subtract_select_fusion), channel_id=1, source_target_pairs={{64,0},{128,64},{192,128},{256,192},{320,256},{384,320},{448,384},... | collective-permute-start | bytes 1658888 | tf_op jit(solution)/shard_map/ppermute | solution.py:77
  23.7 16.6 %collective-permute-start.2 = (f32[256,524]{0,1:T(8,128)}, f32[256,524]{0,1:T(8,128)}, u32[]{:S(2)}, u32[]{:S(2)}) collective-permute-start(f32[256,524]{0,1:T(8,128)} %slice.1081), channel_id=1, source_target_pairs={{0,64},{64,128},{128,192},{192,256},{256,320},{320,384},{384,448},... | collective-permute-start | bytes 1609736 | tf_op jit(solution)/shard_map/ppermute | solution.py:80
  37.3 18.8 %collective-permute-start.5 = (f32[256,540]{0,1:T(8,128)}, f32[256,540]{0,1:T(8,128)}, u32[]{:S(2)}, u32[]{:S(2)}) collective-permute-start(f32[256,540]{0,1:T(8,128)} %collective-permute-done.4), channel_id=1, source_target_pairs={{64,0},{128,64},{192,128},{256,192},{320,256},{384,320},{448,384},... | collective-permute-start | bytes 1658888 | tf_op jit(solution)/shard_map/ppermute | solution.py:77
  40.3 36.6 %collective-permute-start.3 = (f32[256,524]{0,1:T(8,128)}, f32[256,524]{0,1:T(8,128)S(1)}, u32[]{:S(2)}, u32[]{:S(2)}) collective-permute-start(f32[256,524]{0,1:T(8,128)} %collective-permute-done.2), channel_id=1, source_target_pairs={{0,64},{64,128},{128,192},{192,256},{256,320},{320,384},{384,448},... | collective-permute-start | bytes 1609736 | tf_op jit(solution)/shard_map/ppermute | solution.py:80
  56.1 17.9 %collective-permute-start.6 = (f32[256,540]{0,1:T(8,128)}, f32[256,540]{0,1:T(8,128)S(1)}, u32[]{:S(2)}, u32[]{:S(2)}) collective-permute-start(f32[256,540]{0,1:T(8,128)} %collective-permute-done.5), channel_id=1, source_target_pairs={{64,0},{128,64},{192,128},{256,192},{320,256},{384,320},{448,384},... | collective-permute-start | bytes 1658888 | tf_op jit(solution)/shard_map/ppermute | solution.py:77
  74.0 16.8 %collective-permute-start.8 = (f32[256,540]{0,1:T(8,128)S(1)}, f32[256,540]{0,1:T(8,128)S(1)}, u32[]{:S(2)}, u32[]{:S(2)}) collective-permute-start(f32[256,540]{0,1:T(8,128)S(1)} %collective-permute-done.6), channel_id=1, source_target_pairs={{64,0},{128,64},{192,128},{256,192},{320,256},{384,320},{448,384},... | collective-permute-start | bytes 1658888 | tf_op jit(solution)/shard_map/ppermute | solution.py:77
  76.9 15.4 %collective-permute-start.7 = (f32[256,524]{0,1:T(8,128)S(1)}, f32[256,524]{0,1:T(8,128)S(1)}, u32[]{:S(2)}, u32[]{:S(2)}) collective-permute-start(f32[256,524]{0,1:T(8,128)S(1)} %collective-permute-done.3), channel_id=1, source_target_pairs={{0,64},{64,128},{128,192},{192,256},{256,320},{320,384},{384,448},... | collective-permute-start | bytes 1609736 | tf_op jit(solution)/shard_map/ppermute | solution.py:97
  97.1 1.0 %copy-start.1 = (f32[256,512]{0,1:T(8,128)S(1)}, f32[256,512]{0,1:T(8,128)}, u32[]{:S(2)}) copy-start(f32[256,512]{0,1:T(8,128)} %copy-done) | copy-start | bytes 1572868
  97.1 1.2 %copy-start.3 = (f32[256,540]{0,1:T(8,128)S(1)}, f32[256,540]{0,1:T(8,128)}, u32[]{:S(2)}) copy-start(f32[256,540]{0,1:T(8,128)} %copy-done.2) | copy-start | bytes 1658884

commit v11 on v10

--- a/solution.py
+++ b/solution.py
@@ -88,6 +88,7 @@
             return blk
         return jnp.where(me >= slices - 1 - j, blk, jnp.zeros_like(blk))
 
+    trimmed = lax.optimization_barrier(part(slices - 2, CSTEPS))
     h = chain
     current = part(0, h)
     for turn in range(1, behind):
@@ -98,7 +99,7 @@
     got[slices - 1 - behind] = ahead_blk
     for turn in range(behind, slices):
         moved, h = run(current, h, CSTEPS, DT * FINE / CSTEPS)
-        current = part(turn, h) + moved
+        current = (trimmed if turn == slices - 2 else part(turn, h)) + moved
     return current[None]
 
 

time: 102 us -> 101 us (level)
  waiting for transfers between devices: 53.1 us -> 52 us
  local copies, waits for them, and re-layouts: 5.36 us -> 6.44 us
    add x6 -> x2, other arithmetic: 6.81 us -> 2.72 us  [local(): current = part(turn, h) + moved]
    add x0 -> x4, other arithmetic: none -> 3.04 us  [local(): current = (trimmed if turn == slices - 2 else part(turn, h)) + moved]
    ppermute x4, waiting for transfers between devices: 50 us -> 48.9 us  [local(): block = lax.ppermute(block, 'tm', back)]
    slice x0 -> x1, local copies, waits for them, and re-layouts: none -> 1.08 us  [part(): blk = blk[:, extra:extra + n + 2 * h]]
  transfers between devices with their start and end apart: 9 -> 9, of which waited for: 7 -> 7; matrix products, arithmetic and copies ran while one was open for 8% -> 10% of each run, Pallas kernels for 0% -> 0%
where the time goes in v11:
time: 101 us; the launch traced here: 99 us
  waiting for transfers between devices  52 us (51%)
  other arithmetic  21.5 us (21%)
  starting transfers between devices  18.7 us (19%)
  local copies, waits for them, and re-layouts  6.44 us (6%)
    ppermute x4, waiting for transfers between devices, local(): block = lax.ppermute(block, 'tm', back)  48.9 us
    add x14, other arithmetic, advance(): return mid - size * moved + size * coef[2] * spread  11.2 us
    ppermute x4, starting transfers between devices, local(): block = lax.ppermute(block, 'tm', back)  9.29 us
    ppermute x2, starting transfers between devices, shifted(): return lax.ppermute(block, axis, route)  5.56 us
    ppermute x3, starting transfers between devices, local(): ahead_blk = lax.ppermute(ahead_blk, 'tm', ring)  3.86 us
    unnamed x18, local copies, waits for them, and re-layouts  3.45 us
    add x4, other arithmetic, local(): current = (trimmed if turn == slices - 2 else part(turn, h)) + moved  3.04 us
    add x2, other arithmetic, local(): current = part(turn, h) + moved  2.72 us
  transfers between devices with their start and end apart: 9, of which 7 were waited for; matrix products, arithmetic and copies ran while one was open for 10% of the time, Pallas kernels for 0%

profile of v11, /device:TPU:504, one launch (start us, length us, event | category | flops | bytes accessed | tf_op | source)
XLA Modules:
  0.0 99.0 jit_solution(1203563475725105261)
XLA Ops:
  0.0 1.3 %copy.5 = f32[256,512]{0,1:T(8,128)S(1)} copy(f32[256,512]{1,0:T(8,128)} %param.5) | data formatting | bytes 1048576 | tf_op args[1]
  1.3 1.2 %copy.6 = f32[256,512]{0,1:T(8,128)S(1)} copy(f32[256,512]{1,0:T(8,128)} %param.6) | data formatting | bytes 1048576 | tf_op args[2]
  2.6 0.2 copy.7
  2.8 0.2 copy.8
  3.1 1.9 %collective-permute-start = (f32[4,256,22]{1,2,0:T(8,128)S(1)}, f32[4,256,22]{1,2,0:T(8,128)S(1)}, u32[]{:S(2)}, u32[]{:S(2)}) collective-permute-start(f32[4,256,22]{1,2,0:T(8,128)S(1)} %get-tuple-element.11), channel_id=1, source_target_pairs={{0,1},{1,2},{2,3},{3,4},{4,5},{5,6},{6,7},{7,8},{8,9},{9,10},{10,1... | collective-permute-start | bytes 270344 | tf_op jit(solution)/shard_map/ppermute | solution.py:16
  5.0 3.6 %collective-permute-start.1 = (f32[4,256,22]{1,2,0:T(8,128)S(1)}, f32[4,256,22]{1,2,0:T(8,128)S(1)}, u32[]{:S(2)}, u32[]{:S(2)}) collective-permute-start(f32[4,256,22]{1,2,0:T(8,128)S(1)} %get-tuple-element.12), channel_id=1, source_target_pairs={{1,0},{2,1},{3,2},{4,3},{5,4},{6,5},{7,6},{8,7},{9,8},{10,9},{11,1... | collective-permute-start | bytes 270344 | tf_op jit(solution)/shard_map/ppermute | solution.py:16
  8.6 0.3 collective-permute-done
  9.0 1.8 %collective-permute-done.1 = f32[4,256,22]{1,2,0:T(8,128)S(1)} collective-permute-done((f32[4,256,22]{1,2,0:T(8,128)S(1)}, f32[4,256,22]{1,2,0:T(8,128)S(1)}, u32[]{:S(2)}, u32[]{:S(2)}) %collective-permute-start.1) | collective-permute-done | bytes 90144 | tf_op jit(solution)/shard_map/ppermute | solution.py:16
  10.8 1.4 %pad_maximum_fusion = f32[4,256,556]{1,2,0:T(8,128)S(1)} fusion(f32[4,256,22]{1,2,0:T(8,128)S(1)} %collective-permute-done.1, f32[1,256,512]{1,2,0:T(8,128)} %bitcast.748, f32[1,256,512]{1,2,0:T(8,128)S(1)} %bitcast.746, f32[1,256,512]{1,2,0:T(8,128)S(1)} %bitcast.744, f32[1,256,512]{1,2,0:T(8,128)} %copy-done.4, f32[4,256,22]{1,2,0:T(8,128)S(1)} %collective-permute-done), kind=kLoop, calls=%fused_computation | loop fusion | flops 2846720 | bytes 4554752 | tf_op jit(solution)/shard_map/concatenate | solution.py:24
  12.3 0.8 fusion.2
  13.1 0.8 fusion.19
  13.9 0.8 fusion.16
  14.7 0.8 fusion.13
  15.5 0.8 fusion.10
  16.2 0.8 fusion.45
  17.0 1.3 %fusion.64 = (f32[256,542]{0,1:T(8,128)S(1)}, f32[256,542]{0,1:T(8,128)S(1)}) fusion(f32[256,544]{0,1:T(8,128)S(1)} %fusion.45, f32[4,256,556]{1,2,0:T(8,128)S(1)} %pad_maximum_fusion, f32[256,544]{0,1:T(8,128)S(1)} %slice.1076, f32[256,556]{0,1:T(8,128)S(1)} %slice_bitcast_fusion), kind=kLoop, calls=%fused_computation.158 | loop fusion | flops 6382592 | bytes 7237632 | tf_op jit(solution)/shard_map/add | solution.py:41
  18.3 1.3 %subtract_select_fusion = f32[256,540]{0,1:T(8,128)S(1)} fusion(f32[256,542]{0,1:T(8,128)S(1)} %get-tuple-element.10, f32[4,256,556]{1,2,0:T(8,128)S(1)} %pad_maximum_fusion, f32[256,542]{0,1:T(8,128)S(1)} %get-tuple-element.9, pred[]{:T(512)S(6)} %eq.3), kind=kLoop, calls=%fused_computation.49 | loop fusion | flops 6635520 | bytes 6680577 | tf_op jit(solution)/shard_map/jit(_where)/select_n | solution.py:67
  19.6 3.3 %collective-permute-start.4 = (f32[256,540]{0,1:T(8,128)S(1)}, f32[256,540]{0,1:T(8,128)}, u32[]{:S(2)}, u32[]{:S(2)}) collective-permute-start(f32[256,540]{0,1:T(8,128)S(1)} %subtract_select_fusion), channel_id=1, source_target_pairs={{64,0},{128,64},{192,128},{256,192},{320,256},{384,320},{448,384},... | collective-permute-start | bytes 1658888 | tf_op jit(solution)/shard_map/ppermute | solution.py:77
  22.9 0.8 slice.1081
  23.7 1.3 %collective-permute-start.2 = (f32[256,524]{0,1:T(8,128)}, f32[256,524]{0,1:T(8,128)}, u32[]{:S(2)}, u32[]{:S(2)}) collective-permute-start(f32[256,524]{0,1:T(8,128)} %slice.1081), channel_id=1, source_target_pairs={{0,64},{64,128},{128,192},{192,256},{256,320},{320,384},{384,448},... | collective-permute-start | bytes 1609736 | tf_op jit(solution)/shard_map/ppermute | solution.py:80
  25.0 12.2 %collective-permute-done.4 = f32[256,540]{0,1:T(8,128)} collective-permute-done((f32[256,540]{0,1:T(8,128)S(1)}, f32[256,540]{0,1:T(8,128)}, u32[]{:S(2)}, u32[]{:S(2)}) %collective-permute-start.4) | collective-permute-done | bytes 552992 | tf_op jit(solution)/shard_map/ppermute | solution.py:77
  37.3 2.0 %collective-permute-start.5 = (f32[256,540]{0,1:T(8,128)}, f32[256,540]{0,1:T(8,128)}, u32[]{:S(2)}, u32[]{:S(2)}) collective-permute-start(f32[256,540]{0,1:T(8,128)} %collective-permute-done.4), channel_id=1, source_target_pairs={{64,0},{128,64},{192,128},{256,192},{320,256},{384,320},{448,384},... | collective-permute-start | bytes 1658888 | tf_op jit(solution)/shard_map/ppermute | solution.py:77
  39.3 1.0 collective-permute-done.2
  40.3 1.1 %slice.1082 = f32[256,516]{0,1:T(8,128)S(1)} slice(f32[256,524]{0,1:T(8,128)} %collective-permute-done.2), slice={[0:256], [4:520]} | slice | bytes 1056768 | tf_op jit(solution)/shard_map/slice | solution.py:86
  41.4 1.3 %collective-permute-start.3 = (f32[256,524]{0,1:T(8,128)}, f32[256,524]{0,1:T(8,128)S(1)}, u32[]{:S(2)}, u32[]{:S(2)}) collective-permute-start(f32[256,524]{0,1:T(8,128)} %collective-permute-done.2), channel_id=1, source_target_pairs={{0,64},{64,128},{128,192},{192,256},{256,320},{320,384},{384,448},... | collective-permute-start | bytes 1609736 | tf_op jit(solution)/shard_map/ppermute | solution.py:80
  42.7 1.1 %broadcast_select_fusion = f32[256,540]{0,1:T(8,128)S(1)} fusion(f32[256,540]{0,1:T(8,128)} %collective-permute-done.4, pred[]{:T(512)S(6)} %ge.14), kind=kLoop, calls=%fused_computation.357 | loop fusion | flops 138240 | bytes 1105921 | tf_op jit(solution)/shard_map/jit(_where)/select_n | solution.py:89
  43.8 0.8 fusion.42
  44.6 11.5 %collective-permute-done.5 = f32[256,540]{0,1:T(8,128)} collective-permute-done((f32[256,540]{0,1:T(8,128)}, f32[256,540]{0,1:T(8,128)}, u32[]{:S(2)}, u32[]{:S(2)}) %collective-permute-start.5) | collective-permute-done | bytes 552992 | tf_op jit(solution)/shard_map/ppermute | solution.py:77
  56.1 1.9 %collective-permute-start.6 = (f32[256,540]{0,1:T(8,128)}, f32[256,540]{0,1:T(8,128)S(1)}, u32[]{:S(2)}, u32[]{:S(2)}) collective-permute-start(f32[256,540]{0,1:T(8,128)} %collective-permute-done.5), channel_id=1, source_target_pairs={{64,0},{128,64},{192,128},{256,192},{320,256},{384,320},{448,384},... | collective-permute-start | bytes 1658888 | tf_op jit(solution)/shard_map/ppermute | solution.py:77
  58.0 1.9 %fusion.93 = f32[256,536]{0,1:T(8,128)S(1)} fusion(f32[4,256,556]{1,2,0:T(8,128)S(1)} %pad_maximum_fusion, f32[256,540]{0,1:T(8,128)} %collective-permute-done.5, f32[256,538]{0,1:T(8,128)S(1)} %fusion.42, pred[]{:T(512)S(6)} %ge.13), kind=kLoop, calls=%fused_computation.203 | loop fusion | flops 3704832 | bytes 4947969 | tf_op jit(solution)/shard_map/add | solution.py:96
  59.9 0.8 fusion.89
  60.7 13.3 %collective-permute-done.6 = f32[256,540]{0,1:T(8,128)S(1)} collective-permute-done((f32[256,540]{0,1:T(8,128)}, f32[256,540]{0,1:T(8,128)S(1)}, u32[]{:S(2)}, u32[]{:S(2)}) %collective-permute-start.6) | collective-permute-done | bytes 552992 | tf_op jit(solution)/shard_map/ppermute | solution.py:77
  74.0 2.1 %collective-permute-start.8 = (f32[256,540]{0,1:T(8,128)S(1)}, f32[256,540]{0,1:T(8,128)S(1)}, u32[]{:S(2)}, u32[]{:S(2)}) collective-permute-start(f32[256,540]{0,1:T(8,128)S(1)} %collective-permute-done.6), channel_id=1, source_target_pairs={{64,0},{128,64},{192,128},{256,192},{320,256},{384,320},{448,384},... | collective-permute-start | bytes 1658888 | tf_op jit(solution)/shard_map/ppermute | solution.py:77
  76.1 0.8 fusion.86
  76.9 1.3 %collective-permute-start.7 = (f32[256,524]{0,1:T(8,128)S(1)}, f32[256,524]{0,1:T(8,128)S(1)}, u32[]{:S(2)}, u32[]{:S(2)}) collective-permute-start(f32[256,524]{0,1:T(8,128)S(1)} %collective-permute-done.3), channel_id=1, source_target_pairs={{0,64},{64,128},{128,192},{192,256},{256,320},{320,384},{384,448},... | collective-permute-start | bytes 1609736 | tf_op jit(solution)/shard_map/ppermute | solution.py:98
  78.2 0.7 fusion.82
  79.0 11.8 %collective-permute-done.8 = f32[256,540]{0,1:T(8,128)S(1)} collective-permute-done((f32[256,540]{0,1:T(8,128)S(1)}, f32[256,540]{0,1:T(8,128)S(1)}, u32[]{:S(2)}, u32[]{:S(2)}) %collective-permute-start.8) | collective-permute-done | bytes 552992 | tf_op jit(solution)/shard_map/ppermute | solution.py:77
  90.8 0.8 fusion.127
  91.6 0.7 fusion.123
  92.3 0.7 fusion.120
  93.0 0.7 fusion.116
  93.8 0.8 fusion.161
  94.5 0.7 fusion.157
  95.3 0.8 fusion.154
  96.1 0.7 fusion.150
  96.8 0.3 copy-done.1
  97.3 0.7 fusion.182
  98.0 1.0 %copy.14 = f32[1,256,512]{2,1,0:T(8,128)} copy(f32[1,256,512]{1,2,0:T(8,128)S(1)} %fusion.182) | data formatting | bytes 1048576 | tf_op jit(solution)/shard_map/broadcast_in_dim | solution.py:103
  (18 shorter events, 0.3 us)
Async XLA Ops:
  0.0 2.6 %copy-start.5 = (f32[256,512]{1,0:T(8,128)S(1)}, f32[256,512]{1,0:T(8,128)}, u32[]{:S(2)}) copy-start(f32[256,512]{1,0:T(8,128)} %param.7) | copy-start | bytes 1572868
  0.0 2.8 %copy-start.6 = (f32[1,256,512]{2,1,0:T(8,128)S(1)}, f32[1,256,512]{2,1,0:T(8,128)}, u32[]{:S(2)}) copy-start(f32[1,256,512]{2,1,0:T(8,128)} %param.4) | copy-start | bytes 1572868
  2.8 6.2 %copy-start = (f32[256,512]{0,1:T(8,128)}, f32[256,512]{0,1:T(8,128)S(1)}, u32[]{:S(2)}) copy-start(f32[256,512]{0,1:T(8,128)S(1)} %copy.7) | copy-start | bytes 1572868
  3.0 6.0 %copy-start.4 = (f32[1,256,512]{1,2,0:T(8,128)}, f32[1,256,512]{1,2,0:T(8,128)S(1)}, u32[]{:S(2)}) copy-start(f32[1,256,512]{1,2,0:T(8,128)S(1)} %copy.8) | copy-start | bytes 1572868
  3.1 5.9 %collective-permute-start = (f32[4,256,22]{1,2,0:T(8,128)S(1)}, f32[4,256,22]{1,2,0:T(8,128)S(1)}, u32[]{:S(2)}, u32[]{:S(2)}) collective-permute-start(f32[4,256,22]{1,2,0:T(8,128)S(1)} %get-tuple-element.11), channel_id=1, source_target_pairs={{0,1},{1,2},{2,3},{3,4},{4,5},{5,6},{6,7},{7,8},{8,9},{9,10},{10,1... | collective-permute-start | bytes 270344 | tf_op jit(solution)/shard_map/ppermute | solution.py:16
  5.0 5.8 %collective-permute-start.1 = (f32[4,256,22]{1,2,0:T(8,128)S(1)}, f32[4,256,22]{1,2,0:T(8,128)S(1)}, u32[]{:S(2)}, u32[]{:S(2)}) collective-permute-start(f32[4,256,22]{1,2,0:T(8,128)S(1)} %get-tuple-element.12), channel_id=1, source_target_pairs={{1,0},{2,1},{3,2},{4,3},{5,4},{6,5},{7,6},{8,7},{9,8},{10,9},{11,1... | collective-permute-start | bytes 270344 | tf_op jit(solution)/shard_map/ppermute | solution.py:16
  19.6 3.3 %copy-start.2 = (f32[256,540]{0,1:T(8,128)}, f32[256,540]{0,1:T(8,128)S(1)}, u32[]{:S(2)}) copy-start(f32[256,540]{0,1:T(8,128)S(1)} %subtract_select_fusion) | copy-start | bytes 1658884
  19.6 17.6 %collective-permute-start.4 = (f32[256,540]{0,1:T(8,128)S(1)}, f32[256,540]{0,1:T(8,128)}, u32[]{:S(2)}, u32[]{:S(2)}) collective-permute-start(f32[256,540]{0,1:T(8,128)S(1)} %subtract_select_fusion), channel_id=1, source_target_pairs={{64,0},{128,64},{192,128},{256,192},{320,256},{384,320},{448,384},... | collective-permute-start | bytes 1658888 | tf_op jit(solution)/shard_map/ppermute | solution.py:77
  23.7 16.6 %collective-permute-start.2 = (f32[256,524]{0,1:T(8,128)}, f32[256,524]{0,1:T(8,128)}, u32[]{:S(2)}, u32[]{:S(2)}) collective-permute-start(f32[256,524]{0,1:T(8,128)} %slice.1081), channel_id=1, source_target_pairs={{0,64},{64,128},{128,192},{192,256},{256,320},{320,384},{384,448},... | collective-permute-start | bytes 1609736 | tf_op jit(solution)/shard_map/ppermute | solution.py:80
  37.3 18.8 %collective-permute-start.5 = (f32[256,540]{0,1:T(8,128)}, f32[256,540]{0,1:T(8,128)}, u32[]{:S(2)}, u32[]{:S(2)}) collective-permute-start(f32[256,540]{0,1:T(8,128)} %collective-permute-done.4), channel_id=1, source_target_pairs={{64,0},{128,64},{192,128},{256,192},{320,256},{384,320},{448,384},... | collective-permute-start | bytes 1658888 | tf_op jit(solution)/shard_map/ppermute | solution.py:77
  41.4 35.5 %collective-permute-start.3 = (f32[256,524]{0,1:T(8,128)}, f32[256,524]{0,1:T(8,128)S(1)}, u32[]{:S(2)}, u32[]{:S(2)}) collective-permute-start(f32[256,524]{0,1:T(8,128)} %collective-permute-done.2), channel_id=1, source_target_pairs={{0,64},{64,128},{128,192},{192,256},{256,320},{320,384},{384,448},... | collective-permute-start | bytes 1609736 | tf_op jit(solution)/shard_map/ppermute | solution.py:80
  56.1 17.9 %collective-permute-start.6 = (f32[256,540]{0,1:T(8,128)}, f32[256,540]{0,1:T(8,128)S(1)}, u32[]{:S(2)}, u32[]{:S(2)}) collective-permute-start(f32[256,540]{0,1:T(8,128)} %collective-permute-done.5), channel_id=1, source_target_pairs={{64,0},{128,64},{192,128},{256,192},{320,256},{384,320},{448,384},... | collective-permute-start | bytes 1658888 | tf_op jit(solution)/shard_map/ppermute | solution.py:77
  74.0 16.8 %collective-permute-start.8 = (f32[256,540]{0,1:T(8,128)S(1)}, f32[256,540]{0,1:T(8,128)S(1)}, u32[]{:S(2)}, u32[]{:S(2)}) collective-permute-start(f32[256,540]{0,1:T(8,128)S(1)} %collective-permute-done.6), channel_id=1, source_target_pairs={{64,0},{128,64},{192,128},{256,192},{320,256},{384,320},{448,384},... | collective-permute-start | bytes 1658888 | tf_op jit(solution)/shard_map/ppermute | solution.py:77
  76.9 15.4 %collective-permute-start.7 = (f32[256,524]{0,1:T(8,128)S(1)}, f32[256,524]{0,1:T(8,128)S(1)}, u32[]{:S(2)}, u32[]{:S(2)}) collective-permute-start(f32[256,524]{0,1:T(8,128)S(1)} %collective-permute-done.3), channel_id=1, source_target_pairs={{0,64},{64,128},{128,192},{192,256},{256,320},{320,384},{384,448},... | collective-permute-start | bytes 1609736 | tf_op jit(solution)/shard_map/ppermute | solution.py:98
  96.0 1.0 %copy-start.1 = (f32[256,512]{0,1:T(8,128)S(1)}, f32[256,512]{0,1:T(8,128)}, u32[]{:S(2)}) copy-start(f32[256,512]{0,1:T(8,128)} %copy-done) | copy-start | bytes 1572868
  96.1 1.2 %copy-start.3 = (f32[256,540]{0,1:T(8,128)S(1)}, f32[256,540]{0,1:T(8,128)}, u32[]{:S(2)}) copy-start(f32[256,540]{0,1:T(8,128)} %copy-done.2) | copy-start | bytes 1658884

commit v12 on v11

--- a/solution.py
+++ b/solution.py
@@ -1,6 +1,10 @@
+import functools
+
 import jax
 import jax.numpy as jnp
 from jax import lax
+from jax.experimental import pallas as pl
+from jax.experimental.pallas import tpu as pltpu
 from jax.sharding import PartitionSpec as P
 
 FINE = 8
@@ -41,10 +45,45 @@
     return mid - size * moved + size * coef[2] * spread
 
 
+def front_kernel(x_ref, o_ref, *, lead, keep):
+    c = x_ref[0]
+    vx = x_ref[1]
+    vy = x_ref[2]
+    ka = x_ref[3]
+    axp = jnp.maximum(vx, 0.0)
+    axm = jnp.minimum(vx, 0.0)
+    ayp = jnp.maximum(vy, 0.0)
+    aym = jnp.minimum(vy, 0.0)
+    lane = lax.broadcasted_iota(jnp.int32, c.shape, 1)
+    width = c.shape[0]
+    rows = c.shape[1]
+
+    def step(mid, size):
+        left = pltpu.roll(mid, 1, 0)
+        right = pltpu.roll(mid, width - 1, 0)
+        upper = jnp.where(lane == 0, 0.0, pltpu.roll(mid, 1, 1))
+        lower = jnp.where(lane == rows - 1, 0.0, pltpu.roll(mid, rows - 1, 1))
+        moved = axp * (mid - left) + axm * (right - mid)
+        moved = moved + ayp * (mid - upper) + aym * (lower - mid)
+        spread = upper + lower + left + right - 4.0 * mid
+        return mid - size * moved + size * ka * spread
+
+    field = c
+    for _ in range(FINE):
+        field = step(field, DT)
+    coarse_end = c
+    for _ in range(CSTEPS):
+        coarse_end = step(coarse_end, DT * FINE / CSTEPS)
+    first = lax.axis_index("tm") == 0
+    out = jnp.where(first, field, field - coarse_end)
+    o_ref[...] = out[lead: lead + keep]
+
+
 def local(starts, vel_x, vel_y, kappa):
     slices = lax.axis_size("tm")
     chain = CSTEPS * (slices - 1)
-    top = FINE + chain
+    lead = 8
+    top = FINE + chain + 2
     n = starts.shape[-1]
     packed = jnp.stack([starts[0], vel_x, vel_y, kappa])
     wide = with_halo(packed, "space", top)
@@ -60,11 +99,15 @@
             field = advance(field, coef_at(h), size)
         return field, h
 
-    field, h = run(state, top, FINE, DT)
-    start_c = state[:, top - chain - CSTEPS: top + n + chain + CSTEPS]
-    old_coarse, _ = run(start_c, chain + CSTEPS, CSTEPS, DT * FINE / CSTEPS)
     me = lax.axis_index("tm")
-    carried = jnp.where(me == 0, field, field - old_coarse)
+    keep = n + 2 * (top - lead)
+    cols_first = jnp.swapaxes(wide, 1, 2)
+    out = pl.pallas_call(
+        functools.partial(front_kernel, lead=lead, keep=keep),
+        out_shape=jax.ShapeDtypeStruct((keep, cols_first.shape[-1]), jnp.float32),
+    )(cols_first)
+    carried = jnp.swapaxes(out, 0, 1)
+    have = top - lead
     ring = [(i, i + 1) for i in range(slices - 1)]
     back = [((i + 1) % slices, i) for i in range(slices)]
     ahead = slices // 2
@@ -72,7 +115,7 @@
     got = {slices - 1: carried}
     wide_f = CSTEPS * behind
     block = carried
-    ahead_blk = carried[:, chain - wide_f: chain + n + wide_f]
+    ahead_blk = carried[:, have - wide_f: have + n + wide_f]
     for r in range(1, ahead + 1):
         block = lax.ppermute(block, "tm", back)
         got[r - 1] = block

time: 101 us -> 103 us (1.020)
  Pallas kernels: 0 us -> 7.79 us
  other arithmetic: 21.5 us -> 15.7 us
    pallas_call x0 -> x1, Pallas kernels: none -> 7.79 us  [local(): pl.pallas_call(functools.partial(front_kernel, lead=lead, keep=keep), out...]
    add x14 -> x7, other arithmetic: 11.2 us -> 5.21 us  [advance(): return mid - size * moved + size * coef[2] * spread]
    ppermute x4, waiting for transfers between devices: 48.9 us -> 47.1 us  [local(): block = lax.ppermute(block, 'tm', back)]
    concatenate x1, other arithmetic: 1.41 us -> 3.02 us  [with_halo(): return jnp.concatenate([left, cells, right], axis=-1)]
    select_n x1 -> x0, other arithmetic: 1.31 us -> none  [local(): carried = jnp.where(me == 0, field, field - old_coarse)]
    slice x2 -> x1, local copies, waits for them, and re-layouts: 0.88 us -> 1.92 us  [local(): ahead_blk = carried[:, have - wide_f:have + n + wide_f]]
    unnamed x18 -> x16, local copies, waits for them, and re-layouts: 3.45 us -> 3.44 us
where the time goes in v12:
time: 103 us; the launch traced here: 101 us
  waiting for transfers between devices  51.2 us (50%)
  starting transfers between devices  18.7 us (18%)
  other arithmetic  15.7 us (15%)
  Pallas kernels  7.79 us (8%)
  local copies, waits for them, and re-layouts  7.44 us (7%)
    ppermute x4, waiting for transfers between devices, local(): block = lax.ppermute(block, 'tm', back)  47.1 us
    ppermute x4, starting transfers between devices, local(): block = lax.ppermute(block, 'tm', back)  9.1 us
    pallas_call x1, Pallas kernels, local(): pl.pallas_call(functools.partial(front_kernel, lead=lead, keep=keep), out...  7.79 us
    ppermute x2, starting transfers between devices, shifted(): return lax.ppermute(block, axis, route)  5.56 us
    add x7, other arithmetic, advance(): return mid - size * moved + size * coef[2] * spread  5.21 us
    ppermute x3, starting transfers between devices, local(): ahead_blk = lax.ppermute(ahead_blk, 'tm', ring)  4.04 us
    unnamed x16, local copies, waits for them, and re-layouts  3.44 us
    concatenate x1, other arithmetic, with_halo(): return jnp.concatenate([left, cells, right], axis=-1)  3.02 us
  transfers between devices with their start and end apart: 9, of which 7 were waited for; matrix products, arithmetic and copies ran while one was open for 10% of the time, Pallas kernels for 0%

profile of v12, /device:TPU:504, one launch (start us, length us, event | category | flops | bytes accessed | tf_op | source)
XLA Modules:
  0.0 101.1 jit_solution(1979642236634040871)
XLA Ops:
  0.0 1.3 %copy.5 = f32[256,512]{0,1:T(8,128)S(1)} copy(f32[256,512]{1,0:T(8,128)} %param.5) | data formatting | bytes 1048576 | tf_op args[1]
  1.3 1.2 %copy.6 = f32[256,512]{0,1:T(8,128)S(1)} copy(f32[256,512]{1,0:T(8,128)} %param.6) | data formatting | bytes 1048576 | tf_op args[2]
  2.6 0.0 copy-done.4
  2.6 0.2 copy.7
  2.8 0.0 copy-done.5
  2.8 0.0 copy-start
  2.8 0.2 copy.8
  3.1 1.9 %collective-permute-start = (f32[4,256,24]{1,2,0:T(8,128)S(1)}, f32[4,256,24]{1,2,0:T(8,128)S(1)}, u32[]{:S(2)}, u32[]{:S(2)}) collective-permute-start(f32[4,256,24]{1,2,0:T(8,128)S(1)} %get-tuple-element.11), channel_id=1, source_target_pairs={{0,1},{1,2},{2,3},{3,4},{4,5},{5,6},{6,7},{7,8},{8,9},{9,10},{10,1... | collective-permute-start | bytes 294920 | tf_op jit(solution)/shard_map/ppermute | solution.py:20
  5.0 3.6 %collective-permute-start.1 = (f32[4,256,24]{1,2,0:T(8,128)S(1)}, f32[4,256,24]{1,2,0:T(8,128)S(1)}, u32[]{:S(2)}, u32[]{:S(2)}) collective-permute-start(f32[4,256,24]{1,2,0:T(8,128)S(1)} %get-tuple-element.12), channel_id=1, source_target_pairs={{1,0},{2,1},{3,2},{4,3},{5,4},{6,5},{7,6},{8,7},{9,8},{10,9},{11,1... | collective-permute-start | bytes 294920 | tf_op jit(solution)/shard_map/ppermute | solution.py:20
  8.6 0.4 collective-permute-done
  9.0 1.8 %collective-permute-done.1 = f32[4,256,24]{1,2,0:T(8,128)S(1)} collective-permute-done((f32[4,256,24]{1,2,0:T(8,128)S(1)}, f32[4,256,24]{1,2,0:T(8,128)S(1)}, u32[]{:S(2)}, u32[]{:S(2)}) %collective-permute-start.1) | collective-permute-done | bytes 98336 | tf_op jit(solution)/shard_map/ppermute | solution.py:20
  10.8 3.0 %pad_maximum_fusion = (f32[4,256,560]{1,2,0:T(8,128)S(1)}, f32[4,560,256]{2,1,0:T(8,128)}) fusion(f32[4,256,24]{1,2,0:T(8,128)S(1)} %collective-permute-done.1, f32[1,256,512]{1,2,0:T(8,128)} %bitcast.441, f32[1,256,512]{1,2,0:T(8,128)S(1)} %bitcast.439, f32[1,256,512]{1,2,0:T(8,128)S(1)} %bitcast.437, f32[1,256,512]{1,2,0:T(8,128)} %copy-done.3, ...), kind=kLoop, calls=%fused_computation | loop fusion | flops 2867200 | bytes 6881280 | tf_op jit(solution)/shard_map/concatenate | solution.py:28
  13.8 7.8 %shard_map.46 = f32[544,256]{1,0:T(8,128)} custom-call(f32[4,560,256]{2,1,0:T(8,128)} %get-tuple-element.10.x_ref), custom_call_target="tpu_custom_call" | custom-call | tf_op jit(solution)/shard_map/pallas_call | solution.py:105
  21.6 3.2 %collective-permute-start.4 = (f32[256,544]{0,1:T(8,128)}, f32[256,544]{0,1:T(8,128)}, u32[]{:S(2)}, u32[]{:S(2)}) collective-permute-start(f32[256,544]{0,1:T(8,128)} %bitcast.442), channel_id=1, source_target_pairs={{64,0},{128,64},{192,128},{256,192},{320,256},{384,320},{448,384},... | collective-permute-start | bytes 1671176 | tf_op jit(solution)/shard_map/ppermute | solution.py:120
  24.9 1.9 %slice.624 = f32[256,524]{0,1:T(8,128)} slice(f32[256,544]{0,1:T(8,128)} %bitcast.443), slice={[0:256], [10:534]} | slice | bytes 1073152 | tf_op jit(solution)/shard_map/slice | solution.py:118
  26.8 1.3 %collective-permute-start.2 = (f32[256,524]{0,1:T(8,128)}, f32[256,524]{0,1:T(8,128)}, u32[]{:S(2)}, u32[]{:S(2)}) collective-permute-start(f32[256,524]{0,1:T(8,128)} %slice.624), channel_id=1, source_target_pairs={{0,64},{64,128},{128,192},{192,256},{256,320},{320,384},{384,448},... | collective-permute-start | bytes 1609736 | tf_op jit(solution)/shard_map/ppermute | solution.py:123
  28.1 11.4 %collective-permute-done.4 = f32[256,544]{0,1:T(8,128)} collective-permute-done((f32[256,544]{0,1:T(8,128)}, f32[256,544]{0,1:T(8,128)}, u32[]{:S(2)}, u32[]{:S(2)}) %collective-permute-start.4) | collective-permute-done | bytes 557088 | tf_op jit(solution)/shard_map/ppermute | solution.py:120
  39.5 2.0 %collective-permute-start.5 = (f32[256,544]{0,1:T(8,128)}, f32[256,544]{0,1:T(8,128)}, u32[]{:S(2)}, u32[]{:S(2)}) collective-permute-start(f32[256,544]{0,1:T(8,128)} %collective-permute-done.4), channel_id=1, source_target_pairs={{64,0},{128,64},{192,128},{256,192},{320,256},{384,320},{448,384},... | collective-permute-start | bytes 1671176 | tf_op jit(solution)/shard_map/ppermute | solution.py:120
  41.5 1.8 %collective-permute-done.2 = f32[256,524]{0,1:T(8,128)} collective-permute-done((f32[256,524]{0,1:T(8,128)}, f32[256,524]{0,1:T(8,128)}, u32[]{:S(2)}, u32[]{:S(2)}) %collective-permute-start.2) | collective-permute-done | bytes 536608 | tf_op jit(solution)/shard_map/ppermute | solution.py:123
  43.4 1.1 %slice.625 = f32[256,516]{0,1:T(8,128)S(1)} slice(f32[256,524]{0,1:T(8,128)} %collective-permute-done.2), slice={[0:256], [4:520]} | slice | bytes 1056768 | tf_op jit(solution)/shard_map/slice | solution.py:129
  44.5 1.3 %collective-permute-start.3 = (f32[256,524]{0,1:T(8,128)}, f32[256,524]{0,1:T(8,128)S(1)}, u32[]{:S(2)}, u32[]{:S(2)}) collective-permute-start(f32[256,524]{0,1:T(8,128)} %collective-permute-done.2), channel_id=1, source_target_pairs={{0,64},{64,128},{128,192},{192,256},{256,320},{320,384},{384,448},... | collective-permute-start | bytes 1609736 | tf_op jit(solution)/shard_map/ppermute | solution.py:123
  45.8 1.1 %slice_select_fusion = f32[256,540]{0,1:T(8,128)S(1)} fusion(f32[256,544]{0,1:T(8,128)} %collective-permute-done.4, pred[]{:T(512)S(6)} %ge.14), kind=kLoop, calls=%fused_computation.33 | loop fusion | flops 138240 | bytes 1105921 | tf_op jit(solution)/shard_map/jit(_where)/select_n | solution.py:132
  46.9 0.8 fusion.2
  47.7 10.7 %collective-permute-done.5 = f32[256,544]{0,1:T(8,128)} collective-permute-done((f32[256,544]{0,1:T(8,128)}, f32[256,544]{0,1:T(8,128)}, u32[]{:S(2)}, u32[]{:S(2)}) %collective-permute-start.5) | collective-permute-done | bytes 557088 | tf_op jit(solution)/shard_map/ppermute | solution.py:120
  58.3 1.9 %collective-permute-start.6 = (f32[256,544]{0,1:T(8,128)}, f32[256,544]{0,1:T(8,128)S(1)}, u32[]{:S(2)}, u32[]{:S(2)}) collective-permute-start(f32[256,544]{0,1:T(8,128)} %collective-permute-done.5), channel_id=1, source_target_pairs={{64,0},{128,64},{192,128},{256,192},{320,256},{384,320},{448,384},... | collective-permute-start | bytes 1671176 | tf_op jit(solution)/shard_map/ppermute | solution.py:120
  60.2 1.9 %fusion.21 = f32[256,536]{0,1:T(8,128)S(1)} fusion(f32[4,256,560]{1,2,0:T(8,128)S(1)} %get-tuple-element.9, f32[256,544]{0,1:T(8,128)} %collective-permute-done.5, f32[256,538]{0,1:T(8,128)S(1)} %fusion.2, pred[]{:T(512)S(6)} %ge.13), kind=kLoop, calls=%fused_computation.60 | loop fusion | flops 3704832 | bytes 4947969 | tf_op jit(solution)/shard_map/add | solution.py:139
  62.1 0.8 fusion.17
  62.9 13.3 %collective-permute-done.6 = f32[256,544]{0,1:T(8,128)S(1)} collective-permute-done((f32[256,544]{0,1:T(8,128)}, f32[256,544]{0,1:T(8,128)S(1)}, u32[]{:S(2)}, u32[]{:S(2)}) %collective-permute-start.6) | collective-permute-done | bytes 557088 | tf_op jit(solution)/shard_map/ppermute | solution.py:120
  76.2 1.9 %collective-permute-start.8 = (f32[256,544]{0,1:T(8,128)S(1)}, f32[256,544]{0,1:T(8,128)S(1)}, u32[]{:S(2)}, u32[]{:S(2)}) collective-permute-start(f32[256,544]{0,1:T(8,128)S(1)} %collective-permute-done.6), channel_id=1, source_target_pairs={{64,0},{128,64},{192,128},{256,192},{320,256},{384,320},{448,384},... | collective-permute-start | bytes 1671176 | tf_op jit(solution)/shard_map/ppermute | solution.py:120
  78.1 0.8 fusion.14
  78.9 0.0 collective-permute-done.3
  78.9 1.5 %collective-permute-start.7 = (f32[256,524]{0,1:T(8,128)S(1)}, f32[256,524]{0,1:T(8,128)S(1)}, u32[]{:S(2)}, u32[]{:S(2)}) collective-permute-start(f32[256,524]{0,1:T(8,128)S(1)} %collective-permute-done.3), channel_id=1, source_target_pairs={{0,64},{64,128},{128,192},{192,256},{256,320},{320,384},{384,448},... | collective-permute-start | bytes 1609736 | tf_op jit(solution)/shard_map/ppermute | solution.py:141
  80.4 0.7 fusion.10
  81.2 11.8 %collective-permute-done.8 = f32[256,544]{0,1:T(8,128)S(1)} collective-permute-done((f32[256,544]{0,1:T(8,128)S(1)}, f32[256,544]{0,1:T(8,128)S(1)}, u32[]{:S(2)}, u32[]{:S(2)}) %collective-permute-start.8) | collective-permute-done | bytes 557088 | tf_op jit(solution)/shard_map/ppermute | solution.py:120
  93.0 0.7 fusion.55
  93.7 0.7 fusion.51
  94.4 0.0 collective-permute-done.7
  94.4 0.8 fusion.48
  95.2 0.7 fusion.44
  95.9 0.8 fusion.89
  96.7 0.7 fusion.85
  97.4 0.8 fusion.82
  98.2 0.0 copy-start.1
  98.2 0.7 fusion.78
  99.0 0.3 copy-done.1
  99.3 0.2 copy-done.2
  99.4 0.7 fusion.110
  100.1 1.0 copy.14
  (7 shorter events, 0.0 us)
Async XLA Ops:
  0.0 2.6 %copy-start.4 = (f32[256,512]{1,0:T(8,128)S(1)}, f32[256,512]{1,0:T(8,128)}, u32[]{:S(2)}) copy-start(f32[256,512]{1,0:T(8,128)} %param.7) | copy-start | bytes 1572868
  0.0 2.8 %copy-start.5 = (f32[1,256,512]{2,1,0:T(8,128)S(1)}, f32[1,256,512]{2,1,0:T(8,128)}, u32[]{:S(2)}) copy-start(f32[1,256,512]{2,1,0:T(8,128)} %param.4) | copy-start | bytes 1572868
  2.8 6.2 %copy-start = (f32[256,512]{0,1:T(8,128)}, f32[256,512]{0,1:T(8,128)S(1)}, u32[]{:S(2)}) copy-start(f32[256,512]{0,1:T(8,128)S(1)} %copy.7) | copy-start | bytes 1572868
  3.0 6.0 %copy-start.3 = (f32[1,256,512]{1,2,0:T(8,128)}, f32[1,256,512]{1,2,0:T(8,128)S(1)}, u32[]{:S(2)}) copy-start(f32[1,256,512]{1,2,0:T(8,128)S(1)} %copy.8) | copy-start | bytes 1572868
  3.1 5.9 %collective-permute-start = (f32[4,256,24]{1,2,0:T(8,128)S(1)}, f32[4,256,24]{1,2,0:T(8,128)S(1)}, u32[]{:S(2)}, u32[]{:S(2)}) collective-permute-start(f32[4,256,24]{1,2,0:T(8,128)S(1)} %get-tuple-element.11), channel_id=1, source_target_pairs={{0,1},{1,2},{2,3},{3,4},{4,5},{5,6},{6,7},{7,8},{8,9},{9,10},{10,1... | collective-permute-start | bytes 294920 | tf_op jit(solution)/shard_map/ppermute | solution.py:20
  5.0 5.8 %collective-permute-start.1 = (f32[4,256,24]{1,2,0:T(8,128)S(1)}, f32[4,256,24]{1,2,0:T(8,128)S(1)}, u32[]{:S(2)}, u32[]{:S(2)}) collective-permute-start(f32[4,256,24]{1,2,0:T(8,128)S(1)} %get-tuple-element.12), channel_id=1, source_target_pairs={{1,0},{2,1},{3,2},{4,3},{5,4},{6,5},{7,6},{8,7},{9,8},{10,9},{11,1... | collective-permute-start | bytes 294920 | tf_op jit(solution)/shard_map/ppermute | solution.py:20
  21.6 17.8 %collective-permute-start.4 = (f32[256,544]{0,1:T(8,128)}, f32[256,544]{0,1:T(8,128)}, u32[]{:S(2)}, u32[]{:S(2)}) collective-permute-start(f32[256,544]{0,1:T(8,128)} %bitcast.442), channel_id=1, source_target_pairs={{64,0},{128,64},{192,128},{256,192},{320,256},{384,320},{448,384},... | collective-permute-start | bytes 1671176 | tf_op jit(solution)/shard_map/ppermute | solution.py:120
  26.8 16.6 %collective-permute-start.2 = (f32[256,524]{0,1:T(8,128)}, f32[256,524]{0,1:T(8,128)}, u32[]{:S(2)}, u32[]{:S(2)}) collective-permute-start(f32[256,524]{0,1:T(8,128)} %slice.624), channel_id=1, source_target_pairs={{0,64},{64,128},{128,192},{192,256},{256,320},{320,384},{384,448},... | collective-permute-start | bytes 1609736 | tf_op jit(solution)/shard_map/ppermute | solution.py:123
  39.5 18.8 %collective-permute-start.5 = (f32[256,544]{0,1:T(8,128)}, f32[256,544]{0,1:T(8,128)}, u32[]{:S(2)}, u32[]{:S(2)}) collective-permute-start(f32[256,544]{0,1:T(8,128)} %collective-permute-done.4), channel_id=1, source_target_pairs={{64,0},{128,64},{192,128},{256,192},{320,256},{384,320},{448,384},... | collective-permute-start | bytes 1671176 | tf_op jit(solution)/shard_map/ppermute | solution.py:120
  44.5 34.5 %collective-permute-start.3 = (f32[256,524]{0,1:T(8,128)}, f32[256,524]{0,1:T(8,128)S(1)}, u32[]{:S(2)}, u32[]{:S(2)}) collective-permute-start(f32[256,524]{0,1:T(8,128)} %collective-permute-done.2), channel_id=1, source_target_pairs={{0,64},{64,128},{128,192},{192,256},{256,320},{320,384},{384,448},... | collective-permute-start | bytes 1609736 | tf_op jit(solution)/shard_map/ppermute | solution.py:123
  58.3 17.9 %collective-permute-start.6 = (f32[256,544]{0,1:T(8,128)}, f32[256,544]{0,1:T(8,128)S(1)}, u32[]{:S(2)}, u32[]{:S(2)}) collective-permute-start(f32[256,544]{0,1:T(8,128)} %collective-permute-done.5), channel_id=1, source_target_pairs={{64,0},{128,64},{192,128},{256,192},{320,256},{384,320},{448,384},... | collective-permute-start | bytes 1671176 | tf_op jit(solution)/shard_map/ppermute | solution.py:120
  76.2 16.8 %collective-permute-start.8 = (f32[256,544]{0,1:T(8,128)S(1)}, f32[256,544]{0,1:T(8,128)S(1)}, u32[]{:S(2)}, u32[]{:S(2)}) collective-permute-start(f32[256,544]{0,1:T(8,128)S(1)} %collective-permute-done.6), channel_id=1, source_target_pairs={{64,0},{128,64},{192,128},{256,192},{320,256},{384,320},{448,384},... | collective-permute-start | bytes 1671176 | tf_op jit(solution)/shard_map/ppermute | solution.py:120
  78.9 15.5 %collective-permute-start.7 = (f32[256,524]{0,1:T(8,128)S(1)}, f32[256,524]{0,1:T(8,128)S(1)}, u32[]{:S(2)}, u32[]{:S(2)}) collective-permute-start(f32[256,524]{0,1:T(8,128)S(1)} %collective-permute-done.3), channel_id=1, source_target_pairs={{0,64},{64,128},{128,192},{192,256},{256,320},{320,384},{384,448},... | collective-permute-start | bytes 1609736 | tf_op jit(solution)/shard_map/ppermute | solution.py:141
  98.2 1.0 %copy-start.1 = (f32[256,512]{0,1:T(8,128)S(1)}, f32[256,512]{0,1:T(8,128)}, u32[]{:S(2)}) copy-start(f32[256,512]{0,1:T(8,128)} %copy-done) | copy-start | bytes 1572868
  98.2 1.2 %copy-start.2 = (f32[544,256]{1,0:T(8,128)S(1)}, f32[544,256]{1,0:T(8,128)}, u32[]{:S(2)}) copy-start(f32[544,256]{1,0:T(8,128)} %shard_map.46) | copy-start | bytes 1671172

commit v13 on v10

--- a/solution.py
+++ b/solution.py
@@ -88,6 +88,7 @@
             return blk
         return jnp.where(me >= slices - 1 - j, blk, jnp.zeros_like(blk))
 
+    trimmed, own = lax.optimization_barrier((part(slices - 2, CSTEPS), part(slices - 1, 0)))
     h = chain
     current = part(0, h)
     for turn in range(1, behind):
@@ -98,7 +99,8 @@
     got[slices - 1 - behind] = ahead_blk
     for turn in range(behind, slices):
         moved, h = run(current, h, CSTEPS, DT * FINE / CSTEPS)
-        current = part(turn, h) + moved
+        current = {slices - 2: trimmed, slices - 1: own}.get(turn, None)
+        current = (part(turn, h) if current is None else current) + moved
     return current[None]
 
 

time: 102 us -> 100 us (0.980)
  local copies, waits for them, and re-layouts: 5.36 us -> 7.37 us
  waiting for transfers between devices: 53.1 us -> 51.1 us
  other arithmetic: 22.5 us -> 21.4 us
    add x6 -> x2, other arithmetic: 6.81 us -> 2.72 us  [local(): current = part(turn, h) + moved]
    add x0 -> x4, other arithmetic: none -> 3.04 us  [local(): current = (part(turn, h) if current is None else current) + moved]
    slice x0 -> x2, local copies, waits for them, and re-layouts: none -> 2.17 us  [part(): blk = blk[:, extra:extra + n + 2 * h]]
    ppermute x4, waiting for transfers between devices: 50 us -> 48.9 us  [local(): block = lax.ppermute(block, 'tm', back)]
    unnamed x18 -> x16, local copies, waits for them, and re-layouts: 3.45 us -> 3.28 us
  transfers between devices with their start and end apart: 9 -> 9, of which waited for: 7 -> 6; matrix products, arithmetic and copies ran while one was open for 8% -> 11% of each run, Pallas kernels for 0% -> 0%
where the time goes in v13:
time: 100 us; the launch traced here: 98.8 us
  waiting for transfers between devices  51.1 us (51%)
  other arithmetic  21.4 us (21%)
  starting transfers between devices  18.5 us (18%)
  local copies, waits for them, and re-layouts  7.37 us (7%)
    ppermute x4, waiting for transfers between devices, local(): block = lax.ppermute(block, 'tm', back)  48.9 us
    add x14, other arithmetic, advance(): return mid - size * moved + size * coef[2] * spread  11.2 us
    ppermute x4, starting transfers between devices, local(): block = lax.ppermute(block, 'tm', back)  9.11 us
    ppermute x2, starting transfers between devices, shifted(): return lax.ppermute(block, axis, route)  5.56 us
    ppermute x3, starting transfers between devices, local(): ahead_blk = lax.ppermute(ahead_blk, 'tm', ring)  3.86 us
    unnamed x16, local copies, waits for them, and re-layouts  3.28 us
    add x4, other arithmetic, local(): current = (part(turn, h) if current is None else current) + moved  3.04 us
    add x2, other arithmetic, local(): current = part(turn, h) + moved  2.72 us
  transfers between devices with their start and end apart: 9, of which 6 were waited for; matrix products, arithmetic and copies ran while one was open for 11% of the time, Pallas kernels for 0%

profile of v13, /device:TPU:504, one launch (start us, length us, event | category | flops | bytes accessed | tf_op | source)
XLA Modules:
  0.0 98.8 jit_solution(6961243457899013679)
XLA Ops:
  0.0 1.3 %copy.5 = f32[256,512]{0,1:T(8,128)S(1)} copy(f32[256,512]{1,0:T(8,128)} %param.5) | data formatting | bytes 1048576 | tf_op args[1]
  1.3 1.2 %copy.6 = f32[256,512]{0,1:T(8,128)S(1)} copy(f32[256,512]{1,0:T(8,128)} %param.6) | data formatting | bytes 1048576 | tf_op args[2]
  2.6 0.2 copy.7
  2.8 0.2 copy.8
  3.1 1.9 %collective-permute-start = (f32[4,256,22]{1,2,0:T(8,128)S(1)}, f32[4,256,22]{1,2,0:T(8,128)S(1)}, u32[]{:S(2)}, u32[]{:S(2)}) collective-permute-start(f32[4,256,22]{1,2,0:T(8,128)S(1)} %get-tuple-element.15), channel_id=1, source_target_pairs={{0,1},{1,2},{2,3},{3,4},{4,5},{5,6},{6,7},{7,8},{8,9},{9,10},{10,1... | collective-permute-start | bytes 270344 | tf_op jit(solution)/shard_map/ppermute | solution.py:16
  5.0 3.6 %collective-permute-start.1 = (f32[4,256,22]{1,2,0:T(8,128)S(1)}, f32[4,256,22]{1,2,0:T(8,128)S(1)}, u32[]{:S(2)}, u32[]{:S(2)}) collective-permute-start(f32[4,256,22]{1,2,0:T(8,128)S(1)} %get-tuple-element.16), channel_id=1, source_target_pairs={{1,0},{2,1},{3,2},{4,3},{5,4},{6,5},{7,6},{8,7},{9,8},{10,9},{11,1... | collective-permute-start | bytes 270344 | tf_op jit(solution)/shard_map/ppermute | solution.py:16
  8.6 0.3 collective-permute-done
  9.0 1.8 %collective-permute-done.1 = f32[4,256,22]{1,2,0:T(8,128)S(1)} collective-permute-done((f32[4,256,22]{1,2,0:T(8,128)S(1)}, f32[4,256,22]{1,2,0:T(8,128)S(1)}, u32[]{:S(2)}, u32[]{:S(2)}) %collective-permute-start.1) | collective-permute-done | bytes 90144 | tf_op jit(solution)/shard_map/ppermute | solution.py:16
  10.8 1.4 %pad_maximum_fusion = f32[4,256,556]{1,2,0:T(8,128)S(1)} fusion(f32[4,256,22]{1,2,0:T(8,128)S(1)} %collective-permute-done.1, f32[1,256,512]{1,2,0:T(8,128)} %bitcast.748, f32[1,256,512]{1,2,0:T(8,128)S(1)} %bitcast.746, f32[1,256,512]{1,2,0:T(8,128)S(1)} %bitcast.744, f32[1,256,512]{1,2,0:T(8,128)} %copy-done.3, f32[4,256,22]{1,2,0:T(8,128)S(1)} %collective-permute-done), kind=kLoop, calls=%fused_computation | loop fusion | flops 2846720 | bytes 4554752 | tf_op jit(solution)/shard_map/concatenate | solution.py:24
  12.3 0.8 fusion.2
  13.2 0.8 fusion.19
  13.9 0.8 fusion.16
  14.7 0.8 fusion.13
  15.5 0.8 fusion.10
  16.3 0.8 fusion.45
  17.0 1.3 %fusion.64 = (f32[256,542]{0,1:T(8,128)S(1)}, f32[256,542]{0,1:T(8,128)S(1)}) fusion(f32[256,544]{0,1:T(8,128)S(1)} %fusion.45, f32[4,256,556]{1,2,0:T(8,128)S(1)} %pad_maximum_fusion, f32[256,544]{0,1:T(8,128)S(1)} %slice.1076, f32[256,556]{0,1:T(8,128)S(1)} %slice_bitcast_fusion), kind=kLoop, calls=%fused_computation.158 | loop fusion | flops 6382592 | bytes 7237632 | tf_op jit(solution)/shard_map/add | solution.py:41
  18.3 1.3 %subtract_select_fusion = f32[256,540]{0,1:T(8,128)S(1)} fusion(f32[256,542]{0,1:T(8,128)S(1)} %get-tuple-element.14, f32[4,256,556]{1,2,0:T(8,128)S(1)} %pad_maximum_fusion, f32[256,542]{0,1:T(8,128)S(1)} %get-tuple-element.13, pred[]{:T(512)S(6)} %eq.3), kind=kLoop, calls=%fused_computation.49 | loop fusion | flops 6635520 | bytes 6680577 | tf_op jit(solution)/shard_map/jit(_where)/select_n | solution.py:67
  19.7 3.3 %collective-permute-start.4 = (f32[256,540]{0,1:T(8,128)S(1)}, f32[256,540]{0,1:T(8,128)}, u32[]{:S(2)}, u32[]{:S(2)}) collective-permute-start(f32[256,540]{0,1:T(8,128)S(1)} %subtract_select_fusion), channel_id=1, source_target_pairs={{64,0},{128,64},{192,128},{256,192},{320,256},{384,320},{448,384},... | collective-permute-start | bytes 1658888 | tf_op jit(solution)/shard_map/ppermute | solution.py:77
  22.9 0.8 slice.1080
  23.8 1.3 %collective-permute-start.2 = (f32[256,524]{0,1:T(8,128)}, f32[256,524]{0,1:T(8,128)}, u32[]{:S(2)}, u32[]{:S(2)}) collective-permute-start(f32[256,524]{0,1:T(8,128)} %slice.1080), channel_id=1, source_target_pairs={{0,64},{64,128},{128,192},{192,256},{256,320},{320,384},{384,448},... | collective-permute-start | bytes 1609736 | tf_op jit(solution)/shard_map/ppermute | solution.py:80
  25.1 12.2 %collective-permute-done.4 = f32[256,540]{0,1:T(8,128)} collective-permute-done((f32[256,540]{0,1:T(8,128)S(1)}, f32[256,540]{0,1:T(8,128)}, u32[]{:S(2)}, u32[]{:S(2)}) %collective-permute-start.4) | collective-permute-done | bytes 552992 | tf_op jit(solution)/shard_map/ppermute | solution.py:77
  37.3 2.0 %collective-permute-start.5 = (f32[256,540]{0,1:T(8,128)}, f32[256,540]{0,1:T(8,128)}, u32[]{:S(2)}, u32[]{:S(2)}) collective-permute-start(f32[256,540]{0,1:T(8,128)} %collective-permute-done.4), channel_id=1, source_target_pairs={{64,0},{128,64},{192,128},{256,192},{320,256},{384,320},{448,384},... | collective-permute-start | bytes 1658888 | tf_op jit(solution)/shard_map/ppermute | solution.py:77
  39.4 1.1 %slice.1082 = f32[256,512]{0,1:T(8,128)S(1)} slice(f32[256,540]{0,1:T(8,128)} %copy-done.2), slice={[0:256], [14:526]} | slice | bytes 1048576 | tf_op jit(solution)/shard_map/slice | solution.py:86
  40.5 1.1 %slice.1081 = f32[256,516]{0,1:T(8,128)S(1)} slice(f32[256,524]{0,1:T(8,128)} %collective-permute-done.2), slice={[0:256], [4:520]} | slice | bytes 1056768 | tf_op jit(solution)/shard_map/slice | solution.py:86
  41.5 1.3 %collective-permute-start.3 = (f32[256,524]{0,1:T(8,128)}, f32[256,524]{0,1:T(8,128)S(1)}, u32[]{:S(2)}, u32[]{:S(2)}) collective-permute-start(f32[256,524]{0,1:T(8,128)} %collective-permute-done.2), channel_id=1, source_target_pairs={{0,64},{64,128},{128,192},{192,256},{256,320},{320,384},{384,448},... | collective-permute-start | bytes 1609736 | tf_op jit(solution)/shard_map/ppermute | solution.py:80
  42.8 1.1 %broadcast_select_fusion = f32[256,540]{0,1:T(8,128)S(1)} fusion(f32[256,540]{0,1:T(8,128)} %collective-permute-done.4, pred[]{:T(512)S(6)} %ge.14), kind=kLoop, calls=%fused_computation.356 | loop fusion | flops 138240 | bytes 1105921 | tf_op jit(solution)/shard_map/jit(_where)/select_n | solution.py:89
  44.0 0.8 fusion.42
  44.7 11.4 %collective-permute-done.5 = f32[256,540]{0,1:T(8,128)} collective-permute-done((f32[256,540]{0,1:T(8,128)}, f32[256,540]{0,1:T(8,128)}, u32[]{:S(2)}, u32[]{:S(2)}) %collective-permute-start.5) | collective-permute-done | bytes 552992 | tf_op jit(solution)/shard_map/ppermute | solution.py:77
  56.1 1.9 %collective-permute-start.6 = (f32[256,540]{0,1:T(8,128)}, f32[256,540]{0,1:T(8,128)S(1)}, u32[]{:S(2)}, u32[]{:S(2)}) collective-permute-start(f32[256,540]{0,1:T(8,128)} %collective-permute-done.5), channel_id=1, source_target_pairs={{64,0},{128,64},{192,128},{256,192},{320,256},{384,320},{448,384},... | collective-permute-start | bytes 1658888 | tf_op jit(solution)/shard_map/ppermute | solution.py:77
  58.1 1.9 %fusion.93 = f32[256,536]{0,1:T(8,128)S(1)} fusion(f32[4,256,556]{1,2,0:T(8,128)S(1)} %pad_maximum_fusion, f32[256,540]{0,1:T(8,128)} %collective-permute-done.5, f32[256,538]{0,1:T(8,128)S(1)} %fusion.42, pred[]{:T(512)S(6)} %ge.13), kind=kLoop, calls=%fused_computation.203 | loop fusion | flops 3704832 | bytes 4947969 | tf_op jit(solution)/shard_map/add | solution.py:96
  60.0 0.8 fusion.89
  60.7 13.3 %collective-permute-done.6 = f32[256,540]{0,1:T(8,128)S(1)} collective-permute-done((f32[256,540]{0,1:T(8,128)}, f32[256,540]{0,1:T(8,128)S(1)}, u32[]{:S(2)}, u32[]{:S(2)}) %collective-permute-start.6) | collective-permute-done | bytes 552992 | tf_op jit(solution)/shard_map/ppermute | solution.py:77
  74.0 1.9 %collective-permute-start.8 = (f32[256,540]{0,1:T(8,128)S(1)}, f32[256,540]{0,1:T(8,128)S(1)}, u32[]{:S(2)}, u32[]{:S(2)}) collective-permute-start(f32[256,540]{0,1:T(8,128)S(1)} %collective-permute-done.6), channel_id=1, source_target_pairs={{64,0},{128,64},{192,128},{256,192},{320,256},{384,320},{448,384},... | collective-permute-start | bytes 1658888 | tf_op jit(solution)/shard_map/ppermute | solution.py:77
  75.9 0.8 fusion.86
  76.8 1.3 %collective-permute-start.7 = (f32[256,524]{0,1:T(8,128)S(1)}, f32[256,524]{0,1:T(8,128)S(1)}, u32[]{:S(2)}, u32[]{:S(2)}) collective-permute-start(f32[256,524]{0,1:T(8,128)S(1)} %collective-permute-done.3), channel_id=1, source_target_pairs={{0,64},{64,128},{128,192},{192,256},{256,320},{320,384},{384,448},... | collective-permute-start | bytes 1609736 | tf_op jit(solution)/shard_map/ppermute | solution.py:98
  78.1 0.7 fusion.82
  78.8 12.0 %collective-permute-done.8 = f32[256,540]{0,1:T(8,128)S(1)} collective-permute-done((f32[256,540]{0,1:T(8,128)S(1)}, f32[256,540]{0,1:T(8,128)S(1)}, u32[]{:S(2)}, u32[]{:S(2)}) %collective-permute-start.8) | collective-permute-done | bytes 552992 | tf_op jit(solution)/shard_map/ppermute | solution.py:77
  90.8 0.8 fusion.127
  91.6 0.7 fusion.123
  92.4 0.7 fusion.120
  93.0 0.7 fusion.116
  93.8 0.8 fusion.161
  94.6 0.7 fusion.157
  95.3 0.8 fusion.154
  96.1 0.7 fusion.150
  96.8 0.3 copy-done.1
  97.1 0.7 add_bitcast_fusion
  97.8 1.0 %copy.14 = f32[1,256,512]{2,1,0:T(8,128)} copy(f32[1,256,512]{1,2,0:T(8,128)S(1)} %add_bitcast_fusion) | data formatting | bytes 1048576 | tf_op jit(solution)/shard_map/broadcast_in_dim | solution.py:104
  (17 shorter events, 0.1 us)
Async XLA Ops:
  0.0 2.6 %copy-start.4 = (f32[256,512]{1,0:T(8,128)S(1)}, f32[256,512]{1,0:T(8,128)}, u32[]{:S(2)}) copy-start(f32[256,512]{1,0:T(8,128)} %param.7) | copy-start | bytes 1572868
  0.0 2.8 %copy-start.5 = (f32[1,256,512]{2,1,0:T(8,128)S(1)}, f32[1,256,512]{2,1,0:T(8,128)}, u32[]{:S(2)}) copy-start(f32[1,256,512]{2,1,0:T(8,128)} %param.4) | copy-start | bytes 1572868
  2.8 6.2 %copy-start = (f32[256,512]{0,1:T(8,128)}, f32[256,512]{0,1:T(8,128)S(1)}, u32[]{:S(2)}) copy-start(f32[256,512]{0,1:T(8,128)S(1)} %copy.7) | copy-start | bytes 1572868
  3.0 6.0 %copy-start.3 = (f32[1,256,512]{1,2,0:T(8,128)}, f32[1,256,512]{1,2,0:T(8,128)S(1)}, u32[]{:S(2)}) copy-start(f32[1,256,512]{1,2,0:T(8,128)S(1)} %copy.8) | copy-start | bytes 1572868
  3.1 5.9 %collective-permute-start = (f32[4,256,22]{1,2,0:T(8,128)S(1)}, f32[4,256,22]{1,2,0:T(8,128)S(1)}, u32[]{:S(2)}, u32[]{:S(2)}) collective-permute-start(f32[4,256,22]{1,2,0:T(8,128)S(1)} %get-tuple-element.15), channel_id=1, source_target_pairs={{0,1},{1,2},{2,3},{3,4},{4,5},{5,6},{6,7},{7,8},{8,9},{9,10},{10,1... | collective-permute-start | bytes 270344 | tf_op jit(solution)/shard_map/ppermute | solution.py:16
  5.0 5.8 %collective-permute-start.1 = (f32[4,256,22]{1,2,0:T(8,128)S(1)}, f32[4,256,22]{1,2,0:T(8,128)S(1)}, u32[]{:S(2)}, u32[]{:S(2)}) collective-permute-start(f32[4,256,22]{1,2,0:T(8,128)S(1)} %get-tuple-element.16), channel_id=1, source_target_pairs={{1,0},{2,1},{3,2},{4,3},{5,4},{6,5},{7,6},{8,7},{9,8},{10,9},{11,1... | collective-permute-start | bytes 270344 | tf_op jit(solution)/shard_map/ppermute | solution.py:16
  19.7 3.3 %copy-start.2 = (f32[256,540]{0,1:T(8,128)}, f32[256,540]{0,1:T(8,128)S(1)}, u32[]{:S(2)}) copy-start(f32[256,540]{0,1:T(8,128)S(1)} %subtract_select_fusion) | copy-start | bytes 1658884
  19.7 17.6 %collective-permute-start.4 = (f32[256,540]{0,1:T(8,128)S(1)}, f32[256,540]{0,1:T(8,128)}, u32[]{:S(2)}, u32[]{:S(2)}) collective-permute-start(f32[256,540]{0,1:T(8,128)S(1)} %subtract_select_fusion), channel_id=1, source_target_pairs={{64,0},{128,64},{192,128},{256,192},{320,256},{384,320},{448,384},... | collective-permute-start | bytes 1658888 | tf_op jit(solution)/shard_map/ppermute | solution.py:77
  23.8 16.7 %collective-permute-start.2 = (f32[256,524]{0,1:T(8,128)}, f32[256,524]{0,1:T(8,128)}, u32[]{:S(2)}, u32[]{:S(2)}) collective-permute-start(f32[256,524]{0,1:T(8,128)} %slice.1080), channel_id=1, source_target_pairs={{0,64},{64,128},{128,192},{192,256},{256,320},{320,384},{384,448},... | collective-permute-start | bytes 1609736 | tf_op jit(solution)/shard_map/ppermute | solution.py:80
  37.3 18.8 %collective-permute-start.5 = (f32[256,540]{0,1:T(8,128)}, f32[256,540]{0,1:T(8,128)}, u32[]{:S(2)}, u32[]{:S(2)}) collective-permute-start(f32[256,540]{0,1:T(8,128)} %collective-permute-done.4), channel_id=1, source_target_pairs={{64,0},{128,64},{192,128},{256,192},{320,256},{384,320},{448,384},... | collective-permute-start | bytes 1658888 | tf_op jit(solution)/shard_map/ppermute | solution.py:77
  41.5 35.2 %collective-permute-start.3 = (f32[256,524]{0,1:T(8,128)}, f32[256,524]{0,1:T(8,128)S(1)}, u32[]{:S(2)}, u32[]{:S(2)}) collective-permute-start(f32[256,524]{0,1:T(8,128)} %collective-permute-done.2), channel_id=1, source_target_pairs={{0,64},{64,128},{128,192},{192,256},{256,320},{320,384},{384,448},... | collective-permute-start | bytes 1609736 | tf_op jit(solution)/shard_map/ppermute | solution.py:80
  56.1 17.9 %collective-permute-start.6 = (f32[256,540]{0,1:T(8,128)}, f32[256,540]{0,1:T(8,128)S(1)}, u32[]{:S(2)}, u32[]{:S(2)}) collective-permute-start(f32[256,540]{0,1:T(8,128)} %collective-permute-done.5), channel_id=1, source_target_pairs={{64,0},{128,64},{192,128},{256,192},{320,256},{384,320},{448,384},... | collective-permute-start | bytes 1658888 | tf_op jit(solution)/shard_map/ppermute | solution.py:77
  74.0 16.8 %collective-permute-start.8 = (f32[256,540]{0,1:T(8,128)S(1)}, f32[256,540]{0,1:T(8,128)S(1)}, u32[]{:S(2)}, u32[]{:S(2)}) collective-permute-start(f32[256,540]{0,1:T(8,128)S(1)} %collective-permute-done.6), channel_id=1, source_target_pairs={{64,0},{128,64},{192,128},{256,192},{320,256},{384,320},{448,384},... | collective-permute-start | bytes 1658888 | tf_op jit(solution)/shard_map/ppermute | solution.py:77
  76.8 15.6 %collective-permute-start.7 = (f32[256,524]{0,1:T(8,128)S(1)}, f32[256,524]{0,1:T(8,128)S(1)}, u32[]{:S(2)}, u32[]{:S(2)}) collective-permute-start(f32[256,524]{0,1:T(8,128)S(1)} %collective-permute-done.3), channel_id=1, source_target_pairs={{0,64},{64,128},{128,192},{192,256},{256,320},{320,384},{384,448},... | collective-permute-start | bytes 1609736 | tf_op jit(solution)/shard_map/ppermute | solution.py:98
  96.1 1.0 %copy-start.1 = (f32[256,512]{0,1:T(8,128)S(1)}, f32[256,512]{0,1:T(8,128)}, u32[]{:S(2)}) copy-start(f32[256,512]{0,1:T(8,128)} %copy-done) | copy-start | bytes 1572868
